TPU v7x, 256 devices: a whole 4x4x8 slice. The times are simulated.
256 devices in a mesh: sta: 256 (over y, z, x, core).
Axes of the slice: x: 4, y: 4, z: 8, core: 2. Of those that a mesh axis runs over, the one named last changes fastest.
Arguments:
- records: bfloat16 [20480, 2048], P('sta'), may hold values from -6 to 6
- green: bfloat16 [20480, 2048], P('sta'), may hold values from -4 to 4
- pair_mask: int32 [20480, 720], P('sta'), may hold values 0 or 1
- tile_lists: int32 [20480, 16], P('sta'), may hold values from 0 to 1023
- tile_weights: float32 [20480, 16], P('sta'), may hold values from -0.3125 to 0.3125
- tile_green: bfloat16 [524288, 1024], P('sta'), may hold values from -0.125 to 0.125
Outputs:
- adjoint: bfloat16 [20480, 2048], P('sta')
- kernel: float32 [1024, 1024], P('sta')
All inputs are finite; a program needn't handle non-finite values. No bound on the sum of `pair_mask` on one device may be relied on, other than what follows from the above.
Results may differ from a plain program's by a relative error of at most 0.0034.
Values may be sent and summed in bfloat16 or wider, within the bound.
No kernel may reach another device: no remote copies, remote signals or barrier semaphores. Data moves between devices by JAX's collectives and lax.ppermute only.
A program may use at most 64 MiB of HBM per device.

v0:
```python
import jax
import jax.numpy as jnp
from jax import lax
from jax.sharding import PartitionSpec as P

C = 80
F = 1024
TT = 4
HALF = 4
WIN = 9


def passed_along(value, axis, steps):
    count = lax.axis_size(axis)
    pairs = [(source, (source + steps) % count) for source in range(count)]
    return lax.ppermute(value, axis, pairs)


def add_block(totals, mask_bf, moving, offset):
    columns = mask_bf[:, offset * C : (offset + 1) * C]
    return (
        totals[0] + jnp.dot(columns, moving[0], preferred_element_type=jnp.float32),
        totals[1] + jnp.dot(columns, moving[1], preferred_element_type=jnp.float32),
    )


def local(records, green, pair_mask, tile_lists, tile_weights, tile_green):
    rec = records.astype(jnp.float32)
    grn = green.astype(jnp.float32)
    rec_real, rec_imag = (rec[:, :F], rec[:, F:])
    green_real, green_imag = (grn[:, :F], grn[:, F:])
    cross = jnp.concatenate(
        [
            rec_real * green_real + rec_imag * green_imag,
            rec_real * green_imag - rec_imag * green_real,
        ],
        axis=1,
    ).astype(jnp.bfloat16)
    power = (green_real * green_real + green_imag * green_imag).astype(jnp.bfloat16)
    mask_bf = pair_mask.astype(jnp.bfloat16)
    totals = (jnp.zeros((C, 2 * F), jnp.float32), jnp.zeros((C, F), jnp.float32))
    totals = add_block(totals, mask_bf, (cross, power), HALF)
    moving = passed_along((cross, power), "sta", -HALF)
    totals = add_block(totals, mask_bf, moving, 2 * HALF)
    for stepper in range(2 * HALF):
        moving = passed_along((moving[0], moving[1]), "sta", 1)
        offset = 2 * HALF - 1 - stepper
        if offset != HALF:
            totals = add_block(totals, mask_bf, moving, offset)
    factor = 1.0 / jnp.sqrt(jnp.float32(WIN * C))
    qsum = totals[0] * factor
    psum = totals[1] * factor
    q_real, q_imag = (qsum[:, :F], qsum[:, F:])
    adj_real = rec_real * q_real - rec_imag * q_imag - green_real * psum
    adj_imag = rec_real * q_imag + rec_imag * q_real - green_imag * psum
    adjoint = jnp.concatenate([adj_real, adj_imag], axis=1).astype(jnp.bfloat16)
    tiles_total = TT * lax.axis_size("sta")
    tile_ids = jnp.arange(tiles_total, dtype=jnp.int32)
    onehot = (tile_lists[None, :, :] == tile_ids[:, None, None]).astype(jnp.float32)
    tile_map = jnp.sum(onehot * tile_weights[None, :, :], axis=2)
    spread = jnp.dot(tile_map, adjoint.astype(jnp.float32), precision=lax.Precision.HIGHEST)
    green_wide = tile_green.astype(jnp.float32)
    kernel = lax.psum_scatter(
        jnp.dot(spread, green_wide, precision=lax.Precision.HIGHEST),
        "sta",
        scatter_dimension=0,
        tiled=True,
    )
    return (adjoint, kernel)


def solution(mesh):
    placed = (
        P("sta", None),
        P("sta", None),
        P("sta", None),
        P("sta", None),
        P("sta", None),
        P("sta", None),
    )
    return jax.shard_map(
        local,
        mesh=mesh,
        in_specs=placed,
        out_specs=(P("sta", None), P("sta", None)),
        check_vma=False,
    )
```

profile of v0, /device:TPU:2, one launch (start us, length us, event | category | flops | bytes accessed | tf_op | source)
XLA Modules:
  0.0 424.0 jit_solution(2372331628907537443)
XLA Ops:
  7.2 0.0 all-reduce.3.cloned.1.call-start
  7.2 1.0 convert_element_type.18
  8.2 1.0 convert_element_type.8
  9.3 0.1 add_convert_fusion.1
  9.5 9.9 %collective-permute-start = (bf16[80,2048]{1,0:T(8,128)(2,1)S(1)}, bf16[80,2048]{1,0:T(8,128)(2,1)S(1)}, u32[]{:S(2)}, u32[]{:S(2)}) collective-permute-start(bf16[80,2048]{1,0:T(8,128)(2,1)S(1)} %pad_maximum_fusion), channel_id=1, source_target_pairs={{0,252},{1,253},{2,254},{3,255},{4,0},{5,1},{6,2},{7,3},{8,4},{9,5... | collective-permute-start | bytes 983048 | tf_op jit(solution)/shard_map/ppermute | solution.py:16
  19.4 1.4 collective-permute-start.9
  20.8 1.0 convert_element_type.19
  21.8 0.8 copy.12
  22.6 0.8 copy.13
  23.3 1.3 select_reduce_fusion
  24.6 2.9 collective-permute-done
  27.5 0.0 collective-permute-start.1
  27.5 0.3 fusion.20
  27.8 0.2 fusion.22
  28.0 1.9 collective-permute-done.9
  29.9 0.0 collective-permute-start.10
  29.9 4.1 collective-permute-done.1
  34.0 0.0 collective-permute-start.2
  34.0 0.2 convolution_add_fusion.15
  34.2 1.6 collective-permute-done.10
  35.8 0.0 collective-permute-start.11
  35.8 0.2 convolution_add_fusion.7
  36.0 4.5 %collective-permute-done.2 = bf16[80,2048]{1,0:T(8,128)(2,1)S(1)} collective-permute-done((bf16[80,2048]{1,0:T(8,128)(2,1)S(1)}, bf16[80,2048]{1,0:T(8,128)(2,1)S(1)}, u32[]{:S(2)}, u32[]{:S(2)}) %collective-permute-start.2) | collective-permute-done | bytes 327712 | tf_op jit(solution)/shard_map/ppermute | solution.py:16
  40.5 0.0 collective-permute-start.3
  40.5 0.2 convolution_add_fusion.14
  40.7 1.5 collective-permute-done.11
  42.3 0.0 collective-permute-start.12
  42.3 0.2 convolution_add_fusion.13
  42.5 6.3 %collective-permute-done.12 = bf16[80,1024]{1,0:T(8,128)(2,1)S(1)} collective-permute-done((bf16[80,1024]{1,0:T(8,128)(2,1)S(1)}, bf16[80,1024]{1,0:T(8,128)(2,1)S(1)}, u32[]{:S(2)}, u32[]{:S(2)}) %collective-permute-start.12) | collective-permute-done | bytes 163872 | tf_op jit(solution)/shard_map/ppermute | solution.py:16
  48.8 0.0 collective-permute-start.13
  48.8 0.0 collective-permute-done.3
  48.8 0.0 collective-permute-start.4
  48.8 0.3 convolution_add_fusion.6
  49.1 9.5 %collective-permute-done.13 = bf16[80,1024]{1,0:T(8,128)(2,1)S(1)} collective-permute-done((bf16[80,1024]{1,0:T(8,128)(2,1)S(1)}, bf16[80,1024]{1,0:T(8,128)(2,1)S(1)}, u32[]{:S(2)}, u32[]{:S(2)}) %collective-permute-start.13) | collective-permute-done | bytes 163872 | tf_op jit(solution)/shard_map/ppermute | solution.py:16
  58.6 0.0 collective-permute-start.14
  58.6 0.2 convolution_add_fusion.12
  58.8 11.7 %collective-permute-done.14 = bf16[80,1024]{1,0:T(8,128)(2,1)S(1)} collective-permute-done((bf16[80,1024]{1,0:T(8,128)(2,1)S(1)}, bf16[80,1024]{1,0:T(8,128)(2,1)S(1)}, u32[]{:S(2)}, u32[]{:S(2)}) %collective-permute-start.14) | collective-permute-done | bytes 163872 | tf_op jit(solution)/shard_map/ppermute | solution.py:16
  70.5 0.0 collective-permute-start.15
  70.5 0.0 collective-permute-start.5
  70.5 0.2 convolution_add_fusion.11
  70.7 0.3 convolution_add_fusion.5
  71.0 9.6 %collective-permute-done.15 = bf16[80,1024]{1,0:T(8,128)(2,1)S(1)} collective-permute-done((bf16[80,1024]{1,0:T(8,128)(2,1)S(1)}, bf16[80,1024]{1,0:T(8,128)(2,1)S(1)}, u32[]{:S(2)}, u32[]{:S(2)}) %collective-permute-start.15) | collective-permute-done | bytes 163872 | tf_op jit(solution)/shard_map/ppermute | solution.py:16
  80.7 0.0 collective-permute-start.16
  80.7 3.5 collective-permute-done.5
  84.2 0.2 convolution_add_fusion.10
  84.4 6.4 %collective-permute-done.16 = bf16[80,1024]{1,0:T(8,128)(2,1)S(1)} collective-permute-done((bf16[80,1024]{1,0:T(8,128)(2,1)S(1)}, bf16[80,1024]{1,0:T(8,128)(2,1)S(1)}, u32[]{:S(2)}, u32[]{:S(2)}) %collective-permute-start.16) | collective-permute-done | bytes 163872 | tf_op jit(solution)/shard_map/ppermute | solution.py:16
  90.8 0.2 convolution_add_fusion.9
  91.1 3.3 collective-permute-done.6
  94.3 0.0 collective-permute-start.7
  94.3 0.3 convolution_add_fusion.4
  94.6 0.3 convolution_add_fusion.3
  94.9 11.6 %collective-permute-done.7 = bf16[80,2048]{1,0:T(8,128)(2,1)S(1)} collective-permute-done((bf16[80,2048]{1,0:T(8,128)(2,1)S(1)}, bf16[80,2048]{1,0:T(8,128)(2,1)S(1)}, u32[]{:S(2)}, u32[]{:S(2)}) %collective-permute-start.7) | collective-permute-done | bytes 327712 | tf_op jit(solution)/shard_map/ppermute | solution.py:16
  106.5 0.3 convolution_add_fusion.2
  106.8 0.3 convolution_add_fusion.1
  107.1 11.3 %collective-permute-done.8 = bf16[80,2048]{1,0:T(8,128)(2,1)S(1)} collective-permute-done((bf16[80,2048]{1,0:T(8,128)(2,1)S(1)}, bf16[80,2048]{1,0:T(8,128)(2,1)S(1)}, u32[]{:S(2)}, u32[]{:S(2)}) %collective-permute-start.8) | collective-permute-done | bytes 327712 | tf_op jit(solution)/shard_map/ppermute | solution.py:16
  118.4 0.2 fusion.1
  118.7 0.3 subtract_convert_fusion.1
  119.0 0.0 copy-start
  119.0 0.0 copy-start.1
  119.0 3.6 fusion.24
  122.6 14.8 %fusion.25 = f32[1024,1024]{1,0:T(8,128)} fusion(f32[1024,2048]{1,0:T(8,128)S(1)} %fusion.24, bf16[2048,1024]{1,0:T(8,128)(2,1)S(1)} %copy-done.1), kind=kOutput, calls=%fused_computation.51 | convolution fusion | flops 25769803776 | bytes 16777216 | tf_op jit(solution)/shard_map/dot_general | solution.py:64
  137.4 0.0 all-reduce.3.cloned.1.call-update
  137.4 278.4 %all-reduce.3.cloned.1.call-done = f32[1024,1024]{1,0:T(8,128)} async-done(((f32[1024,1024]{1,0:T(8,128)}), f32[1024,1024]{1,0:T(8,128)}) %all-reduce.3.cloned.1.call-update) | async-done | bytes 4194320
  415.8 1.4 constant_dynamic-slice_fusion
  (9 shorter events, 0.1 us)
Async XLA Ops:
  7.2 408.6 %all-reduce.3.cloned.1.call-start = ((), (), s32[]{:S(2)}) async-start(), calls=%async_computation | async-start | bytes 8388608
  9.5 18.0 %collective-permute-start = (bf16[80,2048]{1,0:T(8,128)(2,1)S(1)}, bf16[80,2048]{1,0:T(8,128)(2,1)S(1)}, u32[]{:S(2)}, u32[]{:S(2)}) collective-permute-start(bf16[80,2048]{1,0:T(8,128)(2,1)S(1)} %pad_maximum_fusion), channel_id=1, source_target_pairs={{0,252},{1,253},{2,254},{3,255},{4,0},{5,1},{6,2},{7,3},{8,4},{9,5... | collective-permute-start | bytes 983048 | tf_op jit(solution)/shard_map/ppermute | solution.py:16
  19.4 10.5 %collective-permute-start.9 = (bf16[80,1024]{1,0:T(8,128)(2,1)S(1)}, bf16[80,1024]{1,0:T(8,128)(2,1)S(1)}, u32[]{:S(2)}, u32[]{:S(2)}) collective-permute-start(bf16[80,1024]{1,0:T(8,128)(2,1)S(1)} %get-tuple-element.6), channel_id=1, source_target_pairs={{0,252},{1,253},{2,254},{3,255},{4,0},{5,1},{6,2},{7,3},{8,4},{9,5... | collective-permute-start | bytes 491528 | tf_op jit(solution)/shard_map/ppermute | solution.py:16
  27.5 6.5 %collective-permute-start.1 = (bf16[80,2048]{1,0:T(8,128)(2,1)S(1)}, bf16[80,2048]{1,0:T(8,128)(2,1)S(1)}, u32[]{:S(2)}, u32[]{:S(2)}) collective-permute-start(bf16[80,2048]{1,0:T(8,128)(2,1)S(1)} %collective-permute-done), channel_id=1, source_target_pairs={{0,1},{1,2},{2,3},{3,4},{4,5},{5,6},{6,7},{7,8},{8,9},{9,10},{10,1... | collective-permute-start | bytes 983048 | tf_op jit(solution)/shard_map/ppermute | solution.py:16
  29.9 5.9 %collective-permute-start.10 = (bf16[80,1024]{1,0:T(8,128)(2,1)S(1)}, bf16[80,1024]{1,0:T(8,128)(2,1)S(1)}, u32[]{:S(2)}, u32[]{:S(2)}) collective-permute-start(bf16[80,1024]{1,0:T(8,128)(2,1)S(1)} %collective-permute-done.9), channel_id=1, source_target_pairs={{0,1},{1,2},{2,3},{3,4},{4,5},{5,6},{6,7},{7,8},{8,9},{9,10},{10,1... | collective-permute-start | bytes 491528 | tf_op jit(solution)/shard_map/ppermute | solution.py:16
  34.0 6.5 %collective-permute-start.2 = (bf16[80,2048]{1,0:T(8,128)(2,1)S(1)}, bf16[80,2048]{1,0:T(8,128)(2,1)S(1)}, u32[]{:S(2)}, u32[]{:S(2)}) collective-permute-start(bf16[80,2048]{1,0:T(8,128)(2,1)S(1)} %collective-permute-done.1), channel_id=1, source_target_pairs={{0,1},{1,2},{2,3},{3,4},{4,5},{5,6},{6,7},{7,8},{8,9},{9,10},{10,1... | collective-permute-start | bytes 983048 | tf_op jit(solution)/shard_map/ppermute | solution.py:16
  35.8 6.5 %collective-permute-start.11 = (bf16[80,1024]{1,0:T(8,128)(2,1)S(1)}, bf16[80,1024]{1,0:T(8,128)(2,1)S(1)}, u32[]{:S(2)}, u32[]{:S(2)}) collective-permute-start(bf16[80,1024]{1,0:T(8,128)(2,1)S(1)} %collective-permute-done.10), channel_id=1, source_target_pairs={{0,1},{1,2},{2,3},{3,4},{4,5},{5,6},{6,7},{7,8},{8,9},{9,10},{10,1... | collective-permute-start | bytes 491528 | tf_op jit(solution)/shard_map/ppermute | solution.py:16
  40.5 8.3 %collective-permute-start.3 = (bf16[80,2048]{1,0:T(8,128)(2,1)S(1)}, bf16[80,2048]{1,0:T(8,128)(2,1)S(1)}, u32[]{:S(2)}, u32[]{:S(2)}) collective-permute-start(bf16[80,2048]{1,0:T(8,128)(2,1)S(1)} %collective-permute-done.2), channel_id=1, source_target_pairs={{0,1},{1,2},{2,3},{3,4},{4,5},{5,6},{6,7},{7,8},{8,9},{9,10},{10,1... | collective-permute-start | bytes 983048 | tf_op jit(solution)/shard_map/ppermute | solution.py:16
  42.3 6.5 %collective-permute-start.12 = (bf16[80,1024]{1,0:T(8,128)(2,1)S(1)}, bf16[80,1024]{1,0:T(8,128)(2,1)S(1)}, u32[]{:S(2)}, u32[]{:S(2)}) collective-permute-start(bf16[80,1024]{1,0:T(8,128)(2,1)S(1)} %collective-permute-done.11), channel_id=1, source_target_pairs={{0,1},{1,2},{2,3},{3,4},{4,5},{5,6},{6,7},{7,8},{8,9},{9,10},{10,1... | collective-permute-start | bytes 491528 | tf_op jit(solution)/shard_map/ppermute | solution.py:16
  48.8 9.8 %collective-permute-start.13 = (bf16[80,1024]{1,0:T(8,128)(2,1)S(1)}, bf16[80,1024]{1,0:T(8,128)(2,1)S(1)}, u32[]{:S(2)}, u32[]{:S(2)}) collective-permute-start(bf16[80,1024]{1,0:T(8,128)(2,1)S(1)} %collective-permute-done.12), channel_id=1, source_target_pairs={{0,1},{1,2},{2,3},{3,4},{4,5},{5,6},{6,7},{7,8},{8,9},{9,10},{10,1... | collective-permute-start | bytes 491528 | tf_op jit(solution)/shard_map/ppermute | solution.py:16
  48.8 21.7 %collective-permute-start.4 = (bf16[80,2048]{1,0:T(8,128)(2,1)S(1)}, bf16[80,2048]{1,0:T(8,128)(2,1)S(1)}, u32[]{:S(2)}, u32[]{:S(2)}) collective-permute-start(bf16[80,2048]{1,0:T(8,128)(2,1)S(1)} %collective-permute-done.3), channel_id=1, source_target_pairs={{0,1},{1,2},{2,3},{3,4},{4,5},{5,6},{6,7},{7,8},{8,9},{9,10},{10,1... | collective-permute-start | bytes 983048 | tf_op jit(solution)/shard_map/ppermute | solution.py:16
  58.6 11.9 %collective-permute-start.14 = (bf16[80,1024]{1,0:T(8,128)(2,1)S(1)}, bf16[80,1024]{1,0:T(8,128)(2,1)S(1)}, u32[]{:S(2)}, u32[]{:S(2)}) collective-permute-start(bf16[80,1024]{1,0:T(8,128)(2,1)S(1)} %collective-permute-done.13), channel_id=1, source_target_pairs={{0,1},{1,2},{2,3},{3,4},{4,5},{5,6},{6,7},{7,8},{8,9},{9,10},{10,1... | collective-permute-start | bytes 491528 | tf_op jit(solution)/shard_map/ppermute | solution.py:16
  70.5 10.2 %collective-permute-start.15 = (bf16[80,1024]{1,0:T(8,128)(2,1)S(1)}, bf16[80,1024]{1,0:T(8,128)(2,1)S(1)}, u32[]{:S(2)}, u32[]{:S(2)}) collective-permute-start(bf16[80,1024]{1,0:T(8,128)(2,1)S(1)} %collective-permute-done.14), channel_id=1, source_target_pairs={{0,1},{1,2},{2,3},{3,4},{4,5},{5,6},{6,7},{7,8},{8,9},{9,10},{10,1... | collective-permute-start | bytes 491528 | tf_op jit(solution)/shard_map/ppermute | solution.py:16
  70.5 13.7 %collective-permute-start.5 = (bf16[80,2048]{1,0:T(8,128)(2,1)S(1)}, bf16[80,2048]{1,0:T(8,128)(2,1)S(1)}, u32[]{:S(2)}, u32[]{:S(2)}) collective-permute-start(bf16[80,2048]{1,0:T(8,128)(2,1)S(1)} %collective-permute-done.4), channel_id=1, source_target_pairs={{0,1},{1,2},{2,3},{3,4},{4,5},{5,6},{6,7},{7,8},{8,9},{9,10},{10,1... | collective-permute-start | bytes 983048 | tf_op jit(solution)/shard_map/ppermute | solution.py:16
  80.7 10.2 %collective-permute-start.16 = (bf16[80,1024]{1,0:T(8,128)(2,1)S(1)}, bf16[80,1024]{1,0:T(8,128)(2,1)S(1)}, u32[]{:S(2)}, u32[]{:S(2)}) collective-permute-start(bf16[80,1024]{1,0:T(8,128)(2,1)S(1)} %collective-permute-done.15), channel_id=1, source_target_pairs={{0,1},{1,2},{2,3},{3,4},{4,5},{5,6},{6,7},{7,8},{8,9},{9,10},{10,1... | collective-permute-start | bytes 491528 | tf_op jit(solution)/shard_map/ppermute | solution.py:16
  84.2 10.2 %collective-permute-start.6 = (bf16[80,2048]{1,0:T(8,128)(2,1)S(1)}, bf16[80,2048]{1,0:T(8,128)(2,1)S(1)}, u32[]{:S(2)}, u32[]{:S(2)}) collective-permute-start(bf16[80,2048]{1,0:T(8,128)(2,1)S(1)} %collective-permute-done.5), channel_id=1, source_target_pairs={{0,1},{1,2},{2,3},{3,4},{4,5},{5,6},{6,7},{7,8},{8,9},{9,10},{10,1... | collective-permute-start | bytes 983048 | tf_op jit(solution)/shard_map/ppermute | solution.py:16
  90.8 27.8 %collective-permute-start.17 = (bf16[80,1024]{1,0:T(8,128)(2,1)S(1)}, bf16[80,1024]{1,0:T(8,128)(2,1)S(1)}, u32[]{:S(2)}, u32[]{:S(2)}) collective-permute-start(bf16[80,1024]{1,0:T(8,128)(2,1)S(1)} %collective-permute-done.16), channel_id=1, source_target_pairs={{0,1},{1,2},{2,3},{3,4},{4,5},{5,6},{6,7},{7,8},{8,9},{9,10},{10,1... | collective-permute-start | bytes 491528 | tf_op jit(solution)/shard_map/ppermute | solution.py:16
  94.3 12.2 %collective-permute-start.7 = (bf16[80,2048]{1,0:T(8,128)(2,1)S(1)}, bf16[80,2048]{1,0:T(8,128)(2,1)S(1)}, u32[]{:S(2)}, u32[]{:S(2)}) collective-permute-start(bf16[80,2048]{1,0:T(8,128)(2,1)S(1)} %collective-permute-done.6), channel_id=1, source_target_pairs={{0,1},{1,2},{2,3},{3,4},{4,5},{5,6},{6,7},{7,8},{8,9},{9,10},{10,1... | collective-permute-start | bytes 983048 | tf_op jit(solution)/shard_map/ppermute | solution.py:16
  106.5 11.9 %collective-permute-start.8 = (bf16[80,2048]{1,0:T(8,128)(2,1)S(1)}, bf16[80,2048]{1,0:T(8,128)(2,1)S(1)}, u32[]{:S(2)}, u32[]{:S(2)}) collective-permute-start(bf16[80,2048]{1,0:T(8,128)(2,1)S(1)} %collective-permute-done.7), channel_id=1, source_target_pairs={{0,1},{1,2},{2,3},{3,4},{4,5},{5,6},{6,7},{7,8},{8,9},{9,10},{10,1... | collective-permute-start | bytes 983048 | tf_op jit(solution)/shard_map/ppermute | solution.py:16
  119.0 3.6 copy-start
  119.0 3.6 copy-start.1
Sparse Core Ops, SparseCore 0:
  137.5 278.2 all-reduce.2
where the time goes:
time: 424 us
  waiting for transfers between devices  368 us (87%)
  matrix products  22.8 us (5%)
  between operations  14.3 us (3%)
  starting transfers between devices  11.4 us (3%)
  other arithmetic  4.47 us (1%)
    unnamed x2, waiting for transfers between devices  278 us
    ppermute x18, waiting for transfers between devices, passed_along(): return lax.ppermute(value, axis, pairs)  89.7 us
    dot_general x1, matrix products, local(): jnp.dot(spread, green_wide, precision=lax.Precision.HIGHEST)  14.8 us
    ppermute x18, starting transfers between devices, passed_along(): return lax.ppermute(value, axis, pairs)  11.4 us
  transfers between devices with their start and end apart: 19, of which 16 were waited for; matrix products, arithmetic and copies ran while one was open for 2% of the time, Pallas kernels for 0%

commit v1 on v0

v1 whole, which is shorter than its diff:
```python
import numpy as np
import jax
import jax.numpy as jnp
from jax import lax
from jax.sharding import Mesh
from jax.sharding import PartitionSpec as P

C = 80
F = 1024
TT = 4
HALF = 4
WIN = 9

SUB = ("y", "z", "x", "c")
SIZES = (4, 4, 8, 2)
RS_ORDER = ("c", "x", "z", "y")


def shifted(value, steps, count):
    pairs = [(source, (source + steps) % count) for source in range(count)]
    return lax.ppermute(value, SUB, pairs)


def tile_order():
    y, z, x, c, i = np.meshgrid(
        *[np.arange(n) for n in SIZES], np.arange(TT), indexing="ij"
    )
    flat = (((y * SIZES[1] + z) * SIZES[2] + x) * SIZES[3] + c) * TT + i
    perm = [SUB.index(a) for a in RS_ORDER] + [4]
    return flat.transpose(perm).reshape(-1).astype(np.int32)


def local(records, green, pair_mask, tile_lists, tile_weights, tile_green):
    count = int(np.prod(SIZES))
    rec = records.astype(jnp.float32)
    grn = green.astype(jnp.float32)
    rec_real, rec_imag = (rec[:, :F], rec[:, F:])
    green_real, green_imag = (grn[:, :F], grn[:, F:])
    both = jnp.concatenate(
        [
            rec_real * green_real + rec_imag * green_imag,
            rec_real * green_imag - rec_imag * green_real,
            green_real * green_real + green_imag * green_imag,
        ],
        axis=1,
    ).astype(jnp.bfloat16)
    mask_bf = pair_mask.astype(jnp.bfloat16)
    total = jnp.dot(
        mask_bf[:, HALF * C : (HALF + 1) * C], both, preferred_element_type=jnp.float32
    )
    for offset in range(WIN):
        if offset == HALF:
            continue
        moving = shifted(both, HALF - offset, count)
        columns = mask_bf[:, offset * C : (offset + 1) * C]
        total = total + jnp.dot(columns, moving, preferred_element_type=jnp.float32)
    factor = 1.0 / jnp.sqrt(jnp.float32(WIN * C))
    total = total * factor
    q_real, q_imag, psum = (total[:, :F], total[:, F : 2 * F], total[:, 2 * F :])
    adj_real = rec_real * q_real - rec_imag * q_imag - green_real * psum
    adj_imag = rec_real * q_imag + rec_imag * q_real - green_imag * psum
    adjoint = jnp.concatenate([adj_real, adj_imag], axis=1).astype(jnp.bfloat16)
    response = jnp.dot(adjoint, tile_green, preferred_element_type=jnp.float32)
    tile_ids = jnp.asarray(tile_order())
    onehot = (tile_lists[None, :, :] == tile_ids[:, None, None]).astype(jnp.float32)
    tile_map = jnp.sum(onehot * tile_weights[None, :, :], axis=2)
    part = jnp.dot(tile_map, response, precision=lax.Precision.HIGHEST)
    for axis in RS_ORDER:
        part = lax.psum_scatter(part, axis, scatter_dimension=0, tiled=True)
    return (adjoint, part)


def solution(mesh):
    devices = np.asarray(mesh.devices).reshape(SIZES)
    grid = Mesh(devices, SUB)
    rows = P(SUB, None)
    return jax.shard_map(
        local,
        mesh=grid,
        in_specs=(rows,) * 6,
        out_specs=(rows, rows),
        check_vma=False,
    )
```

time: 424 us -> 245 us (0.58)
  waiting for transfers between devices: 368 us -> 189 us
  starting transfers between devices: 11.4 us -> 23.4 us
  matrix products: 22.8 us -> 12.1 us
    unnamed x2 -> x5, waiting for transfers between devices: 278 us -> 46 us
    reduce_scatter x0 -> x3, waiting for transfers between devices: none -> 93.4 us  [local(): part = lax.psum_scatter(part, axis, scatter_dimension=0, tiled=True)]
    ppermute x18 -> x8, waiting for transfers between devices: 89.7 us -> 49.7 us  [shifted(): return lax.ppermute(value, SUB, pairs)]
    ppermute x18 -> x8, starting transfers between devices: 11.4 us -> 23.2 us  [shifted(): return lax.ppermute(value, SUB, pairs)]
    dot_general x20 -> x11, matrix products: 22.8 us -> 12.1 us  [the longest x8 5.81 us: local(): total = total + jnp.dot(columns, moving, preferred_element_type=jnp.float32)]
  transfers between devices with their start and end apart: 19 -> 12, of which waited for: 16 -> 8; matrix products, arithmetic and copies ran while one was open for 2% -> 3% of each run, Pallas kernels for 0% -> 0%
where the time goes in v1:
time: 245 us
  waiting for transfers between devices  189 us (77%)
  starting transfers between devices  23.4 us (10%)
  between operations  14.6 us (6%)
  matrix products  12.1 us (5%)
  other arithmetic  3.73 us (2%)
    reduce_scatter x3, waiting for transfers between devices, local(): part = lax.psum_scatter(part, axis, scatter_dimension=0, tiled=True)  93.4 us
    ppermute x8, waiting for transfers between devices, shifted(): return lax.ppermute(value, SUB, pairs)  49.7 us
    unnamed x5, waiting for transfers between devices  46 us
    ppermute x8, starting transfers between devices, shifted(): return lax.ppermute(value, SUB, pairs)  23.2 us
    dot_general x8, matrix products, local(): total = total + jnp.dot(columns, moving, preferred_element_type=jnp.float32)  5.81 us
    dot_general x1, matrix products, local(): part = jnp.dot(tile_map, response, precision=lax.Precision.HIGHEST)  5.05 us
  transfers between devices with their start and end apart: 12, of which 8 were waited for; matrix products, arithmetic and copies ran while one was open for 3% of the time, Pallas kernels for 0%

profile of v1, /device:TPU:2, one launch (start us, length us, event | category | flops | bytes accessed | tf_op | source)
XLA Modules:
  0.0 245.0 jit_solution(8559338779728216566)
XLA Ops:
  7.2 0.0 copy-start.5
  7.2 0.0 copy-start.3
  7.2 0.0 copy-start.4
  7.2 0.0 reduce-scatter.4.cloned.1.call-start
  7.2 0.0 copy-start.2
  7.3 1.1 convert_element_type.12
  8.3 1.0 convert_element_type.13
  9.3 0.1 add_convert_fusion.1
  9.5 2.2 collective-permute-start
  11.7 7.3 %collective-permute-start.6 = (bf16[80,3072]{1,0:T(8,128)(2,1)S(1)}, bf16[80,3072]{1,0:T(8,128)(2,1)}, u32[]{:S(2)}, u32[]{:S(2)}) collective-permute-start(bf16[80,3072]{1,0:T(8,128)(2,1)S(1)} %pad_maximum_fusion), channel_id=1, source_target_pairs={{0,253},{1,254},{2,255},{3,0},{4,1},{5,2},{6,3},{7,4},{8,5},{9,6},... | collective-permute-start | bytes 1474568 | tf_op jit(solution)/shard_map/ppermute | solution.py:21
  19.0 1.4 collective-permute-start.5
  20.5 0.6 collective-permute-start.4
  21.0 0.0 collective-permute-start.3
  21.0 0.0 copy-done.2
  21.0 0.0 copy-done.3
  21.1 0.1 copy.13
  21.1 0.0 copy-done.4
  21.1 0.1 copy.14
  21.2 0.3 fusion.22
  21.6 0.0 copy-done.5
  21.6 1.2 select_reduce_fusion
  22.8 16.1 %collective-permute-done.6 = bf16[80,3072]{1,0:T(8,128)(2,1)} collective-permute-done((bf16[80,3072]{1,0:T(8,128)(2,1)S(1)}, bf16[80,3072]{1,0:T(8,128)(2,1)}, u32[]{:S(2)}, u32[]{:S(2)}) %collective-permute-start.6) | collective-permute-done | bytes 491552 | tf_op jit(solution)/shard_map/ppermute | solution.py:21
  38.9 0.0 collective-permute-start.2
  38.9 1.4 fusion.10
  40.3 7.2 %collective-permute-done.5 = bf16[80,3072]{1,0:T(8,128)(2,1)} collective-permute-done((bf16[80,3072]{1,0:T(8,128)(2,1)S(1)}, bf16[80,3072]{1,0:T(8,128)(2,1)}, u32[]{:S(2)}, u32[]{:S(2)}) %collective-permute-start.5) | collective-permute-done | bytes 491552 | tf_op jit(solution)/shard_map/ppermute | solution.py:21
  47.5 8.1 %collective-permute-start.7 = (bf16[80,3072]{1,0:T(8,128)(2,1)S(1)}, bf16[80,3072]{1,0:T(8,128)(2,1)S(1)}, u32[]{:S(2)}, u32[]{:S(2)}) collective-permute-start(bf16[80,3072]{1,0:T(8,128)(2,1)S(1)} %pad_maximum_fusion), channel_id=1, source_target_pairs={{0,252},{1,253},{2,254},{3,255},{4,0},{5,1},{6,2},{7,3},{8,4},{9,5... | collective-permute-start | bytes 1474568 | tf_op jit(solution)/shard_map/ppermute | solution.py:21
  55.5 1.4 fusion.12
  56.9 5.3 %collective-permute-done.4 = bf16[80,3072]{1,0:T(8,128)(2,1)} collective-permute-done((bf16[80,3072]{1,0:T(8,128)(2,1)S(1)}, bf16[80,3072]{1,0:T(8,128)(2,1)}, u32[]{:S(2)}, u32[]{:S(2)}) %collective-permute-start.4) | collective-permute-done | bytes 491552 | tf_op jit(solution)/shard_map/ppermute | solution.py:21
  62.2 3.7 %collective-permute-start.1 = (bf16[80,3072]{1,0:T(8,128)(2,1)S(1)}, bf16[80,3072]{1,0:T(8,128)(2,1)S(1)}, u32[]{:S(2)}, u32[]{:S(2)}) collective-permute-start(bf16[80,3072]{1,0:T(8,128)(2,1)S(1)} %pad_maximum_fusion), channel_id=1, source_target_pairs={{0,3},{1,4},{2,5},{3,6},{4,7},{5,8},{6,9},{7,10},{8,11},{9,12},{10... | collective-permute-start | bytes 1474568 | tf_op jit(solution)/shard_map/ppermute | solution.py:21
  65.9 1.4 fusion.14
  67.2 0.0 collective-permute-done.3
  67.2 0.3 fusion.16
  67.6 0.0 collective-permute-done.2
  67.6 0.3 fusion.18
  67.9 0.0 collective-permute-done.7
  67.9 0.3 fusion.8
  68.2 0.0 collective-permute-done
  68.2 0.3 convolution_add_fusion.1
  68.5 0.0 copy-start
  68.5 21.1 %collective-permute-done.1 = bf16[80,3072]{1,0:T(8,128)(2,1)S(1)} collective-permute-done((bf16[80,3072]{1,0:T(8,128)(2,1)S(1)}, bf16[80,3072]{1,0:T(8,128)(2,1)S(1)}, u32[]{:S(2)}, u32[]{:S(2)}) %collective-permute-start.1) | collective-permute-done | bytes 491552 | tf_op jit(solution)/shard_map/ppermute | solution.py:21
  89.6 0.6 fusion.7
  90.2 0.2 subtract_convert_fusion.1
  90.4 0.0 copy-done
  90.4 0.0 copy-start.1
  90.4 0.9 fusion.24
  91.3 5.0 %fusion.25 = f32[1024,1024]{1,0:T(8,128)} fusion(f32[1024,80]{0,1:T(8,128)S(1)} %select_reduce_fusion, f32[80,1024]{1,0:T(8,128)S(1)} %fusion.24), kind=kOutput, calls=%fused_computation.36 | convolution fusion | flops 1006632960 | bytes 4849664 | tf_op jit(solution)/shard_map/dot_general | solution.py:67
  96.4 0.0 copy-done.1
  96.4 0.0 copy-start.6
  96.4 0.0 reduce-scatter.4.cloned.1.call-update
  96.4 0.0 reduce-scatter.6.cloned.1.call-start
  96.4 16.9 %reduce-scatter.4.cloned.1.call-done = f32[512,1024]{1,0:T(8,128)} async-done(((f32[1024,1024]{1,0:T(8,128)}), f32[512,1024]{1,0:T(8,128)}) %reduce-scatter.4.cloned.1.call-update) | async-done | bytes 2097168 | tf_op jit(solution)/shard_map/reduce_scatter | solution.py:69
  113.4 0.0 reduce-scatter.6.cloned.1.call-update
  113.4 0.0 reduce-scatter.8.cloned.1.call-start
  113.5 46.6 %reduce-scatter.6.cloned.1.call-done = f32[64,1024]{1,0:T(8,128)} async-done(((f32[512,1024]{1,0:T(8,128)}), f32[64,1024]{1,0:T(8,128)}) %reduce-scatter.6.cloned.1.call-update) | async-done | bytes 262160 | tf_op jit(solution)/shard_map/reduce_scatter | solution.py:69
  160.1 0.0 reduce-scatter.8.cloned.1.call-update
  160.1 0.0 all-reduce.3.cloned.1.call-start
  160.1 29.8 %reduce-scatter.8.cloned.1.call-done = f32[16,1024]{1,0:T(8,128)} async-done(((f32[64,1024]{1,0:T(8,128)}), f32[16,1024]{1,0:T(8,128)}) %reduce-scatter.8.cloned.1.call-update) | async-done | bytes 65552 | tf_op jit(solution)/shard_map/reduce_scatter | solution.py:69
  190.0 0.0 all-reduce.3.cloned.1.call-update
  190.0 0.0 copy-done.6
  190.0 0.6 dynamic-slice
  191.2 45.9 %all-reduce.3.cloned.1.call-done = f32[16,1024]{1,0:T(8,128)} async-done(((f32[16,1024]{1,0:T(8,128)}), f32[16,1024]{1,0:T(8,128)}) %all-reduce.3.cloned.1.call-update) | async-done | bytes 65552
  237.1 1.4 constant_dynamic-slice_fusion
  (3 shorter events, 0.1 us)
Async XLA Ops:
  7.2 14.4 %copy-start.5 = (s32[1024]{0:T(1024)S(1)}, s32[1024]{0:T(1024)}, u32[]{:S(2)}) copy-start(s32[1024]{0:T(1024)} %constant.7.clone) | copy-start | bytes 12292
  7.2 13.9 %copy-start.3 = (s32[80,16]{0,1:T(8,128)S(1)}, s32[80,16]{0,1:T(8,128)}, u32[]{:S(2)}) copy-start(s32[80,16]{0,1:T(8,128)} %param.10) | copy-start | bytes 15364
  7.2 14.0 %copy-start.4 = (f32[80,16]{0,1:T(8,128)S(1)}, f32[80,16]{0,1:T(8,128)}, u32[]{:S(2)}) copy-start(f32[80,16]{0,1:T(8,128)} %param.11) | copy-start | bytes 15364
  7.2 106.2 %reduce-scatter.4.cloned.1.call-start = ((), (), s32[]{:S(2)}) async-start(), calls=%async_computation.3 | async-start | bytes 6291456 | tf_op jit(solution)/shard_map/reduce_scatter | solution.py:69
  7.2 13.8 %copy-start.2 = (s32[80,720]{1,0:T(8,128)S(1)}, s32[80,720]{1,0:T(8,128)}, u32[]{:S(2)}) copy-start(s32[80,720]{1,0:T(8,128)} %param.9) | copy-start | bytes 691204
  9.5 58.6 %collective-permute-start = (bf16[80,3072]{1,0:T(8,128)(2,1)S(1)}, bf16[80,3072]{1,0:T(8,128)(2,1)S(1)}, u32[]{:S(2)}, u32[]{:S(2)}) collective-permute-start(bf16[80,3072]{1,0:T(8,128)(2,1)S(1)} %pad_maximum_fusion), channel_id=1, source_target_pairs={{0,4},{1,5},{2,6},{3,7},{4,8},{5,9},{6,10},{7,11},{8,12},{9,13},{1... | collective-permute-start | bytes 1474568 | tf_op jit(solution)/shard_map/ppermute | solution.py:21
  11.7 27.2 %collective-permute-start.6 = (bf16[80,3072]{1,0:T(8,128)(2,1)S(1)}, bf16[80,3072]{1,0:T(8,128)(2,1)}, u32[]{:S(2)}, u32[]{:S(2)}) collective-permute-start(bf16[80,3072]{1,0:T(8,128)(2,1)S(1)} %pad_maximum_fusion), channel_id=1, source_target_pairs={{0,253},{1,254},{2,255},{3,0},{4,1},{5,2},{6,3},{7,4},{8,5},{9,6},... | collective-permute-start | bytes 1474568 | tf_op jit(solution)/shard_map/ppermute | solution.py:21
  19.0 28.5 %collective-permute-start.5 = (bf16[80,3072]{1,0:T(8,128)(2,1)S(1)}, bf16[80,3072]{1,0:T(8,128)(2,1)}, u32[]{:S(2)}, u32[]{:S(2)}) collective-permute-start(bf16[80,3072]{1,0:T(8,128)(2,1)S(1)} %pad_maximum_fusion), channel_id=1, source_target_pairs={{0,254},{1,255},{2,0},{3,1},{4,2},{5,3},{6,4},{7,5},{8,6},{9,7},{1... | collective-permute-start | bytes 1474568 | tf_op jit(solution)/shard_map/ppermute | solution.py:21
  20.5 41.7 %collective-permute-start.4 = (bf16[80,3072]{1,0:T(8,128)(2,1)S(1)}, bf16[80,3072]{1,0:T(8,128)(2,1)}, u32[]{:S(2)}, u32[]{:S(2)}) collective-permute-start(bf16[80,3072]{1,0:T(8,128)(2,1)S(1)} %pad_maximum_fusion), channel_id=1, source_target_pairs={{0,255},{1,0},{2,1},{3,2},{4,3},{5,4},{6,5},{7,6},{8,7},{9,8},{10,... | collective-permute-start | bytes 1474568 | tf_op jit(solution)/shard_map/ppermute | solution.py:21
  21.0 46.2 %collective-permute-start.3 = (bf16[80,3072]{1,0:T(8,128)(2,1)S(1)}, bf16[80,3072]{1,0:T(8,128)(2,1)S(1)}, u32[]{:S(2)}, u32[]{:S(2)}) collective-permute-start(bf16[80,3072]{1,0:T(8,128)(2,1)S(1)} %pad_maximum_fusion), channel_id=1, source_target_pairs={{0,1},{1,2},{2,3},{3,4},{4,5},{5,6},{6,7},{7,8},{8,9},{9,10},{10,1... | collective-permute-start | bytes 1474568 | tf_op jit(solution)/shard_map/ppermute | solution.py:21
  38.9 28.6 %collective-permute-start.2 = (bf16[80,3072]{1,0:T(8,128)(2,1)S(1)}, bf16[80,3072]{1,0:T(8,128)(2,1)S(1)}, u32[]{:S(2)}, u32[]{:S(2)}) collective-permute-start(bf16[80,3072]{1,0:T(8,128)(2,1)S(1)} %pad_maximum_fusion), channel_id=1, source_target_pairs={{0,2},{1,3},{2,4},{3,5},{4,6},{5,7},{6,8},{7,9},{8,10},{9,11},{10,... | collective-permute-start | bytes 1474568 | tf_op jit(solution)/shard_map/ppermute | solution.py:21
  47.5 20.4 %collective-permute-start.7 = (bf16[80,3072]{1,0:T(8,128)(2,1)S(1)}, bf16[80,3072]{1,0:T(8,128)(2,1)S(1)}, u32[]{:S(2)}, u32[]{:S(2)}) collective-permute-start(bf16[80,3072]{1,0:T(8,128)(2,1)S(1)} %pad_maximum_fusion), channel_id=1, source_target_pairs={{0,252},{1,253},{2,254},{3,255},{4,0},{5,1},{6,2},{7,3},{8,4},{9,5... | collective-permute-start | bytes 1474568 | tf_op jit(solution)/shard_map/ppermute | solution.py:21
  62.2 27.4 %collective-permute-start.1 = (bf16[80,3072]{1,0:T(8,128)(2,1)S(1)}, bf16[80,3072]{1,0:T(8,128)(2,1)S(1)}, u32[]{:S(2)}, u32[]{:S(2)}) collective-permute-start(bf16[80,3072]{1,0:T(8,128)(2,1)S(1)} %pad_maximum_fusion), channel_id=1, source_target_pairs={{0,3},{1,4},{2,5},{3,6},{4,7},{5,8},{6,9},{7,10},{8,11},{9,12},{10... | collective-permute-start | bytes 1474568 | tf_op jit(solution)/shard_map/ppermute | solution.py:21
  68.5 22.0 %copy-start = (bf16[2048,1024]{1,0:T(8,128)(2,1)S(1)}, bf16[2048,1024]{1,0:T(8,128)(2,1)}, u32[]{:S(2)}) copy-start(bf16[2048,1024]{1,0:T(8,128)(2,1)} %param.12) | copy-start | bytes 12582916
  90.4 5.9 %copy-start.1 = (bf16[80,2048]{1,0:T(8,128)(2,1)}, bf16[80,2048]{1,0:T(8,128)(2,1)S(1)}, u32[]{:S(2)}) copy-start(bf16[80,2048]{1,0:T(8,128)(2,1)S(1)} %pad_maximum_fusion.1) | copy-start | bytes 983044
  96.4 93.6 %copy-start.6 = (u32[256]{0:T(256)S(1)}, u32[256]{0:T(256)}, u32[]{:S(2)}) copy-start(u32[256]{0:T(256)} %constant.15) | copy-start | bytes 3076
  96.4 63.7 %reduce-scatter.6.cloned.1.call-start = ((), (), s32[]{:S(2)}) async-start(), calls=%async_computation.4 | async-start | bytes 2359296 | tf_op jit(solution)/shard_map/reduce_scatter | solution.py:69
  113.4 76.5 %reduce-scatter.8.cloned.1.call-start = ((), (), s32[]{:S(2)}) async-start(), calls=%async_computation.5 | async-start | bytes 327680 | tf_op jit(solution)/shard_map/reduce_scatter | solution.py:69
  160.1 77.1 %all-reduce.3.cloned.1.call-start = ((), (), s32[]{:S(2)}) async-start(), calls=%async_computation.6 | async-start | bytes 131072
Sparse Core Ops, SparseCore 0:
  96.5 16.8 reduce-scatter.3
  115.9 44.0 reduce-scatter.5
  162.6 27.3 reduce-scatter.7
  192.1 44.9 all-reduce.2

commit v2 on v1

--- a/solution.py
+++ b/solution.py
@@ -18,6 +18,11 @@
 
 def shifted(value, steps, count):
     pairs = [(source, (source + steps) % count) for source in range(count)]
+    return lax.ppermute(value, SUB, pairs)
+
+
+def swap(value, count):
+    pairs = [(source, source ^ 1) for source in range(count)]
     return lax.ppermute(value, SUB, pairs)
 
 
@@ -45,15 +50,33 @@
         axis=1,
     ).astype(jnp.bfloat16)
     mask_bf = pair_mask.astype(jnp.bfloat16)
-    total = jnp.dot(
-        mask_bf[:, HALF * C : (HALF + 1) * C], both, preferred_element_type=jnp.float32
-    )
-    for offset in range(WIN):
-        if offset == HALF:
-            continue
-        moving = shifted(both, HALF - offset, count)
-        columns = mask_bf[:, offset * C : (offset + 1) * C]
-        total = total + jnp.dot(columns, moving, preferred_element_type=jnp.float32)
+    first = lax.axis_index(SUB) % 2 == 0
+
+    def cols(offset):
+        return mask_bf[:, offset * C : (offset + 1) * C]
+
+    def picked(on_first, on_second):
+        return jnp.where(first, cols(on_first), cols(on_second))
+
+    def add(total, columns, moving):
+        return total + jnp.dot(columns, moving, preferred_element_type=jnp.float32)
+
+    ahead = shifted(both, -2, count)
+    behind = shifted(both, 2, count)
+    total = jnp.dot(cols(HALF), both, preferred_element_type=jnp.float32)
+    total = add(total, cols(HALF + 2), ahead)
+    total = add(total, cols(HALF - 2), behind)
+    ahead2 = shifted(ahead, -2, count)
+    behind2 = shifted(behind, 2, count)
+    width = both.shape[1]
+    swapped = swap(jnp.concatenate([both, ahead, behind], axis=1), count)
+    total = add(total, picked(HALF + 1, HALF - 1), swapped[:, :width])
+    total = add(total, picked(HALF + 3, HALF + 1), swapped[:, width : 2 * width])
+    total = add(total, picked(HALF - 1, HALF - 3), swapped[:, 2 * width :])
+    total = add(total, cols(HALF + 4), ahead2)
+    total = add(total, cols(HALF - 4), behind2)
+    last = swap(jnp.where(first, ahead2, behind2), count)
+    total = add(total, picked(HALF - 3, HALF + 3), last)
     factor = 1.0 / jnp.sqrt(jnp.float32(WIN * C))
     total = total * factor
     q_real, q_imag, psum = (total[:, :F], total[:, F : 2 * F], total[:, 2 * F :])
@@ -65,9 +88,11 @@
     onehot = (tile_lists[None, :, :] == tile_ids[:, None, None]).astype(jnp.float32)
     tile_map = jnp.sum(onehot * tile_weights[None, :, :], axis=2)
     part = jnp.dot(tile_map, response, precision=lax.Precision.HIGHEST)
-    for axis in RS_ORDER:
-        part = lax.psum_scatter(part, axis, scatter_dimension=0, tiled=True)
-    return (adjoint, part)
+    part = part.reshape(SIZES[SUB.index(RS_ORDER[0])], -1, part.shape[1])
+    part = jnp.sum(lax.all_to_all(part, RS_ORDER[0], 0, 0, tiled=False), axis=0)
+    part = part.reshape(-1, TT, part.shape[1])
+    part = lax.all_to_all(part, RS_ORDER[1:], 0, 0, tiled=False)
+    return (adjoint, jnp.sum(part, axis=0))
 
 
 def solution(mesh):

time: 245 us -> 134 us (0.55)
  waiting for transfers between devices: 189 us -> 27.3 us
  blocking collectives: 0 us -> 73 us
  between operations: 14.6 us -> 0.83 us
  starting transfers between devices: 23.4 us -> 11.1 us
  other arithmetic: 3.73 us -> 10.6 us
  matrix products: 12.1 us -> 7.2 us
    reduce_scatter x3 -> x0, waiting for transfers between devices: 93.4 us -> none  [local(): part = lax.psum_scatter(part, axis, scatter_dimension=0, tiled=True)]
    all_to_all x0 -> x2, blocking collectives: none -> 73 us  [the longest x1 64.9 us: local(): part = lax.all_to_all(part, RS_ORDER[1:], 0, 0, tiled=False)]
    unnamed x5 -> x0, waiting for transfers between devices: 46 us -> none
    ppermute x8 -> x4, waiting for transfers between devices: 49.7 us -> 27 us  [shifted(): return lax.ppermute(value, SUB, pairs)]
    ppermute x8 -> x4, starting transfers between devices: 23.2 us -> 10.9 us  [shifted(): return lax.ppermute(value, SUB, pairs)]
    reduce_sum x0 -> x2, other arithmetic: none -> 3.77 us  [the longest x1 2.78 us: local(): part = jnp.sum(lax.all_to_all(part, RS_ORDER[0], 0, 0, tiled=False), axis=0)]
    dot_general x9, matrix products: 6.14 us -> 2.89 us  [the longest x8 2.56 us: add(): return total + jnp.dot(columns, moving, preferred_element_type=jnp.float32)]
  transfers between devices with their start and end apart: 12 -> 6, of which waited for: 8 -> 5; matrix products, arithmetic and copies ran while one was open for 3% -> 3% of each run, Pallas kernels for 0% -> 0%
where the time goes in v2:
time: 134 us
  blocking collectives  73 us (54%)
  waiting for transfers between devices  27.3 us (20%)
  starting transfers between devices  11.1 us (8%)
  other arithmetic  10.6 us (8%)
  matrix products  7.2 us (5%)
  local copies, waits for them, and re-layouts  3.57 us (3%)
    all_to_all x1, blocking collectives, local(): part = lax.all_to_all(part, RS_ORDER[1:], 0, 0, tiled=False)  64.9 us
    ppermute x4, waiting for transfers between devices, shifted(): return lax.ppermute(value, SUB, pairs)  27 us
    ppermute x4, starting transfers between devices, shifted(): return lax.ppermute(value, SUB, pairs)  10.9 us
    all_to_all x1, blocking collectives, local(): part = jnp.sum(lax.all_to_all(part, RS_ORDER[0], 0, 0, tiled=False), axis=0)  8.17 us
    dot_general x1, matrix products, local(): part = jnp.dot(tile_map, response, precision=lax.Precision.HIGHEST)  3.47 us
    reduce_sum x1, other arithmetic, local(): part = jnp.sum(lax.all_to_all(part, RS_ORDER[0], 0, 0, tiled=False), axis=0)  2.78 us
  transfers between devices with their start and end apart: 6, of which 5 were waited for; matrix products, arithmetic and copies ran while one was open for 3% of the time, Pallas kernels for 0%

profile of v2, /device:TPU:2, one launch (start us, length us, event | category | flops | bytes accessed | tf_op | source)
XLA Modules:
  0.0 133.6 jit_solution(3049455467984007372)
XLA Ops:
  0.6 1.0 convert_element_type.13
  1.7 1.0 convert_element_type.12
  2.7 0.8 constant_dynamic-update-slice_fusion.4
  3.5 0.8 constant_dynamic-update-slice_fusion.3
  4.2 0.0 copy-start.3
  4.2 0.0 copy-start.4
  4.2 0.7 constant_dynamic-update-slice_fusion.2
  5.0 2.3 %collective-permute-start = (bf16[80,3072]{1,0:T(8,128)(2,1)S(1)}, bf16[80,3072]{1,0:T(8,128)(2,1)S(1)}, u32[]{:S(2)}, u32[]{:S(2)}) collective-permute-start(bf16[80,3072]{1,0:T(8,128)(2,1)S(1)} %pad_maximum_fusion), channel_id=1, source_target_pairs={{0,254},{1,255},{2,0},{3,1},{4,2},{5,3},{6,4},{7,5},{8,6},{9,7},{1... | collective-permute-start | bytes 1474568 | tf_op jit(solution)/shard_map/ppermute | solution.py:21
  7.3 0.0 collective-permute-start.1
  7.3 1.0 convert_element_type.14
  8.3 0.0 copy-done.3
  8.3 0.1 copy.17
  8.4 0.0 copy-done.4
  8.4 0.1 copy.18
  8.5 0.0 copy-start.2
  8.5 0.3 fusion.21
  8.8 9.2 %collective-permute-done = bf16[80,3072]{1,0:T(8,128)(2,1)S(1)} collective-permute-done((bf16[80,3072]{1,0:T(8,128)(2,1)S(1)}, bf16[80,3072]{1,0:T(8,128)(2,1)S(1)}, u32[]{:S(2)}, u32[]{:S(2)}) %collective-permute-start) | collective-permute-done | bytes 491552 | tf_op jit(solution)/shard_map/ppermute | solution.py:21
  18.0 8.6 %collective-permute-start.3 = (bf16[80,3072]{1,0:T(8,128)(2,1)S(1)}, bf16[80,3072]{1,0:T(8,128)(2,1)S(1)}, u32[]{:S(2)}, u32[]{:S(2)}) collective-permute-start(bf16[80,3072]{1,0:T(8,128)(2,1)S(1)} %collective-permute-done), channel_id=1, source_target_pairs={{0,254},{1,255},{2,0},{3,1},{4,2},{5,3},{6,4},{7,5},{8,6},{9,7},{1... | collective-permute-start | bytes 1474568 | tf_op jit(solution)/shard_map/ppermute | solution.py:21
  26.6 0.5 collective-permute-done.1
  27.1 0.0 collective-permute-start.4
  27.1 0.0 copy-done.2
  27.1 0.0 copy-start.5
  27.2 0.1 collective-permute-start.2
  27.3 9.0 %collective-permute-done.3 = bf16[80,3072]{1,0:T(8,128)(2,1)S(1)} collective-permute-done((bf16[80,3072]{1,0:T(8,128)(2,1)S(1)}, bf16[80,3072]{1,0:T(8,128)(2,1)S(1)}, u32[]{:S(2)}, u32[]{:S(2)}) %collective-permute-start.3) | collective-permute-done | bytes 491552 | tf_op jit(solution)/shard_map/ppermute | solution.py:21
  36.2 8.4 %collective-permute-done.4 = bf16[80,3072]{1,0:T(8,128)(2,1)S(1)} collective-permute-done((bf16[80,3072]{1,0:T(8,128)(2,1)S(1)}, bf16[80,3072]{1,0:T(8,128)(2,1)S(1)}, u32[]{:S(2)}, u32[]{:S(2)}) %collective-permute-start.4) | collective-permute-done | bytes 491552 | tf_op jit(solution)/shard_map/ppermute | solution.py:21
  44.6 0.1 broadcast_select_fusion
  44.7 0.1 collective-permute-start.5
  44.8 0.0 copy-done.5
  44.8 1.2 select_reduce_fusion
  46.0 0.3 convolution_add_fusion.1
  46.3 0.3 collective-permute-done.5
  46.6 0.3 fusion.23
  46.9 0.0 collective-permute-done.2
  46.9 0.3 fusion.10
  47.3 0.3 fusion.12
  47.6 0.3 fusion.8
  47.9 0.4 fusion.3
  48.3 0.3 fusion.7
  48.6 0.0 copy-start
  48.6 0.3 fusion.6
  48.9 0.2 subtract_convert_fusion.1
  49.2 1.6 %copy-done = bf16[2048,1024]{1,0:T(8,128)(2,1)S(1)} copy-done((bf16[2048,1024]{1,0:T(8,128)(2,1)S(1)}, bf16[2048,1024]{1,0:T(8,128)(2,1)}, u32[]{:S(2)}) %copy-start) | copy-done | bytes 4194328
  50.8 0.0 copy-start.1
  50.8 0.8 convolution_bitcast_fusion.2
  51.6 0.0 copy-done.1
  51.7 3.5 %fusion.14 = f32[2,512,1024]{2,1,0:T(8,128)S(1)} fusion(f32[80,1024,1]{1,0,2:T(8,128)S(1)} %convolution_bitcast_fusion.2, f32[10,2,8,512]{3,2,1,0:T(8,128)S(1)} %bitcast.34), kind=kOutput, calls=%fused_computation.22 | convolution fusion | flops 1006632960 | bytes 4849664 | tf_op jit(solution)/shard_map/dot_general | solution.py:90
  55.1 8.2 %all_to_all.10 = f32[2,512,1024]{2,1,0:T(8,128)} all-to-all(f32[2,512,1024]{2,1,0:T(8,128)S(1)} %fusion.14), channel_id=1, replica_groups=mesh['y'=4,'z'=4,'x'=8,'c'=2] {'c'}, dimensions={0} | all-to-all | bytes 8388608 | tf_op jit(solution)/shard_map/all_to_all | solution.py:92
  63.3 2.8 %reduce_sum.28 = f32[512,1024]{1,0:T(8,128)S(1)} reduce(f32[2,512,1024]{2,1,0:T(8,128)} %all_to_all.10, f32[]{:T(128)} %constant.42.clone.1), dimensions={0}, to_apply=%region_1.2 | reduce | flops 524288 | bytes 6291460 | tf_op jit(solution)/shard_map/reduce_sum | solution.py:92
  66.1 1.7 %reshape.12 = f32[128,4,1024]{2,1,0:T(4,128)} reshape(f32[512,1024]{1,0:T(8,128)S(1)} %reduce_sum.28) | data formatting | bytes 4194304 | tf_op jit(solution)/shard_map/reshape | solution.py:93
  67.8 64.9 %all_to_all.11 = f32[128,4,1024]{2,1,0:T(4,128)S(1)} all-to-all(f32[128,4,1024]{2,1,0:T(4,128)} %reshape.12), channel_id=1, replica_groups=mesh['y'=4,'z'=4,'x'=8,'c'=2] {'x','z','y'}, dimensions={0} | all-to-all | bytes 4194304 | tf_op jit(solution)/shard_map/all_to_all | solution.py:94
  132.6 1.0 reduce_sum.29
  (4 shorter events, 0.1 us)
Async XLA Ops:
  4.2 4.1 %copy-start.3 = (s32[80,16]{0,1:T(8,128)S(1)}, s32[80,16]{0,1:T(8,128)}, u32[]{:S(2)}) copy-start(s32[80,16]{0,1:T(8,128)} %param.10) | copy-start | bytes 15364
  4.2 4.1 %copy-start.4 = (f32[80,16]{0,1:T(8,128)S(1)}, f32[80,16]{0,1:T(8,128)}, u32[]{:S(2)}) copy-start(f32[80,16]{0,1:T(8,128)} %param.11) | copy-start | bytes 15364
  5.0 13.0 %collective-permute-start = (bf16[80,3072]{1,0:T(8,128)(2,1)S(1)}, bf16[80,3072]{1,0:T(8,128)(2,1)S(1)}, u32[]{:S(2)}, u32[]{:S(2)}) collective-permute-start(bf16[80,3072]{1,0:T(8,128)(2,1)S(1)} %pad_maximum_fusion), channel_id=1, source_target_pairs={{0,254},{1,255},{2,0},{3,1},{4,2},{5,3},{6,4},{7,5},{8,6},{9,7},{1... | collective-permute-start | bytes 1474568 | tf_op jit(solution)/shard_map/ppermute | solution.py:21
  7.3 19.7 %collective-permute-start.1 = (bf16[80,3072]{1,0:T(8,128)(2,1)S(1)}, bf16[80,3072]{1,0:T(8,128)(2,1)S(1)}, u32[]{:S(2)}, u32[]{:S(2)}) collective-permute-start(bf16[80,3072]{1,0:T(8,128)(2,1)S(1)} %pad_maximum_fusion), channel_id=1, source_target_pairs={{0,2},{1,3},{2,4},{3,5},{4,6},{5,7},{6,8},{7,9},{8,10},{9,11},{10,... | collective-permute-start | bytes 1474568 | tf_op jit(solution)/shard_map/ppermute | solution.py:21
  8.5 18.6 %copy-start.2 = (bf16[80,9216]{1,0:T(8,128)(2,1)S(1)}, bf16[80,9216]{1,0:T(8,128)(2,1)}, u32[]{:S(2)}) copy-start(bf16[80,9216]{1,0:T(8,128)(2,1)} %get-tuple-element.2) | copy-start | bytes 4423684
  18.0 18.2 %collective-permute-start.3 = (bf16[80,3072]{1,0:T(8,128)(2,1)S(1)}, bf16[80,3072]{1,0:T(8,128)(2,1)S(1)}, u32[]{:S(2)}, u32[]{:S(2)}) collective-permute-start(bf16[80,3072]{1,0:T(8,128)(2,1)S(1)} %collective-permute-done), channel_id=1, source_target_pairs={{0,254},{1,255},{2,0},{3,1},{4,2},{5,3},{6,4},{7,5},{8,6},{9,7},{1... | collective-permute-start | bytes 1474568 | tf_op jit(solution)/shard_map/ppermute | solution.py:21
  27.1 17.5 %collective-permute-start.4 = (bf16[80,3072]{1,0:T(8,128)(2,1)S(1)}, bf16[80,3072]{1,0:T(8,128)(2,1)S(1)}, u32[]{:S(2)}, u32[]{:S(2)}) collective-permute-start(bf16[80,3072]{1,0:T(8,128)(2,1)S(1)} %collective-permute-done.1), channel_id=1, source_target_pairs={{0,2},{1,3},{2,4},{3,5},{4,6},{5,7},{6,8},{7,9},{8,10},{9,11},{10,... | collective-permute-start | bytes 1474568 | tf_op jit(solution)/shard_map/ppermute | solution.py:21
  27.1 17.7 %copy-start.5 = (s32[1024]{0:T(1024)S(1)}, s32[1024]{0:T(1024)}, u32[]{:S(2)}) copy-start(s32[1024]{0:T(1024)} %constant.43.clone) | copy-start | bytes 12292
  27.2 19.8 %collective-permute-start.2 = (bf16[80,9216]{1,0:T(8,128)(2,1)S(1)}, bf16[80,9216]{1,0:T(8,128)(2,1)S(1)}, u32[]{:S(2)}, u32[]{:S(2)}) collective-permute-start(bf16[80,9216]{1,0:T(8,128)(2,1)S(1)} %constant_dynamic-update-slice_fusion), channel_id=1, source_target_pairs={{0,1},{1,0},{2,3},{3,2},{4,5},{5,4},{6,7},{7,6},{8,9},{9,8},{10,11... | collective-permute-start | bytes 4423688 | tf_op jit(solution)/shard_map/ppermute | solution.py:26
  44.7 2.0 %collective-permute-start.5 = (bf16[80,3072]{1,0:T(8,128)(2,1)S(1)}, bf16[80,3072]{1,0:T(8,128)(2,1)S(1)}, u32[]{:S(2)}, u32[]{:S(2)}) collective-permute-start(bf16[80,3072]{1,0:T(8,128)(2,1)S(1)} %broadcast_select_fusion), channel_id=1, source_target_pairs={{0,1},{1,0},{2,3},{3,2},{4,5},{5,4},{6,7},{7,6},{8,9},{9,8},{10,11... | collective-permute-start | bytes 1474568 | tf_op jit(solution)/shard_map/ppermute | solution.py:26
  48.6 2.2 %copy-start = (bf16[2048,1024]{1,0:T(8,128)(2,1)S(1)}, bf16[2048,1024]{1,0:T(8,128)(2,1)}, u32[]{:S(2)}) copy-start(bf16[2048,1024]{1,0:T(8,128)(2,1)} %param.12) | copy-start | bytes 12582916
  50.8 0.8 copy-start.1

commit v3 on v2

--- a/solution.py
+++ b/solution.py
@@ -14,6 +14,7 @@
 SUB = ("y", "z", "x", "c")
 SIZES = (4, 4, 8, 2)
 RS_ORDER = ("c", "x", "z", "y")
+STAGES = (("x",), ("z", "y"))
 
 
 def shifted(value, steps, count):
@@ -84,15 +85,18 @@
     adj_imag = rec_real * q_imag + rec_imag * q_real - green_imag * psum
     adjoint = jnp.concatenate([adj_real, adj_imag], axis=1).astype(jnp.bfloat16)
     response = jnp.dot(adjoint, tile_green, preferred_element_type=jnp.float32)
-    tile_ids = jnp.asarray(tile_order())
-    onehot = (tile_lists[None, :, :] == tile_ids[:, None, None]).astype(jnp.float32)
-    tile_map = jnp.sum(onehot * tile_weights[None, :, :], axis=2)
-    part = jnp.dot(tile_map, response, precision=lax.Precision.HIGHEST)
-    part = part.reshape(SIZES[SUB.index(RS_ORDER[0])], -1, part.shape[1])
-    part = jnp.sum(lax.all_to_all(part, RS_ORDER[0], 0, 0, tiled=False), axis=0)
-    part = part.reshape(-1, TT, part.shape[1])
-    part = lax.all_to_all(part, RS_ORDER[1:], 0, 0, tiled=False)
-    return (adjoint, jnp.sum(part, axis=0))
+    responses = jnp.concatenate([response, swap(response, count)], axis=0)
+    lists = jnp.concatenate([tile_lists, swap(tile_lists, count)], axis=0)
+    weights = jnp.concatenate([tile_weights, swap(tile_weights, count)], axis=0)
+    tile_ids = jnp.asarray(tile_order()[: TT * count // SIZES[-1]]) + TT * (lax.axis_index(SUB) % 2)
+    onehot = (lists[None, :, :] == tile_ids[:, None, None]).astype(jnp.float32)
+    tile_map = jnp.sum(onehot * weights[None, :, :], axis=2)
+    part = jnp.dot(tile_map, responses, precision=lax.Precision.HIGHEST)
+    for group in STAGES:
+        ways = int(np.prod([SIZES[SUB.index(a)] for a in group]))
+        part = part.reshape(ways, -1, part.shape[1])
+        part = jnp.sum(lax.all_to_all(part, group, 0, 0, tiled=False), axis=0)
+    return (adjoint, part)
 
 
 def solution(mesh):

time: 134 us -> 116 us (0.87)
  blocking collectives: 73 us -> 50.5 us
  matrix products: 7.2 us -> 10.7 us
  local copies, waits for them, and re-layouts: 3.57 us -> 6.45 us
  other arithmetic: 10.6 us -> 8.35 us
    all_to_all x2, blocking collectives: 73 us -> 50.5 us  [local(): part = jnp.sum(lax.all_to_all(part, group, 0, 0, tiled=False), axis=0)]
    dot_general x8, matrix products: 2.56 us -> 7.69 us  [add(): return total + jnp.dot(columns, moving, preferred_element_type=jnp.float32)]
    reduce_sum x3, other arithmetic: 4.98 us -> 2.01 us  [the longest x1 1.21 us: local(): tile_map = jnp.sum(onehot * weights[None, :, :], axis=2)]
    unnamed x15 -> x17, local copies, waits for them, and re-layouts: 1.86 us -> 4.09 us
    concatenate x1, local copies, waits for them, and re-layouts: 0.03 us -> 1.88 us  [local(): swapped = swap(jnp.concatenate([both, ahead, behind], axis=1), count)]
    dot_general x1, matrix products: 3.47 us -> 1.81 us  [local(): part = jnp.dot(tile_map, responses, precision=lax.Precision.HIGHEST)]
    ppermute x4, waiting for transfers between devices: 27 us -> 25.4 us  [shifted(): return lax.ppermute(value, SUB, pairs)]
    reshape x1, local copies, waits for them, and re-layouts: 1.67 us -> 0.08 us  [local(): part = part.reshape(ways, -1, part.shape[1])]
  transfers between devices with their start and end apart: 6 -> 9, of which waited for: 5 -> 5; matrix products, arithmetic and copies ran while one was open for 3% -> 13% of each run, Pallas kernels for 0% -> 0%
where the time goes in v3:
time: 116 us; the launch traced here: 115 us
  blocking collectives  50.5 us (44%)
  waiting for transfers between devices  27.1 us (23%)
  starting transfers between devices  11.6 us (10%)
  matrix products  10.7 us (9%)
  other arithmetic  8.35 us (7%)
  local copies, waits for them, and re-layouts  6.45 us (6%)
    all_to_all x2, blocking collectives, local(): part = jnp.sum(lax.all_to_all(part, group, 0, 0, tiled=False), axis=0)  50.5 us
    ppermute x4, waiting for transfers between devices, shifted(): return lax.ppermute(value, SUB, pairs)  25.4 us
    ppermute x4, starting transfers between devices, shifted(): return lax.ppermute(value, SUB, pairs)  10.9 us
    dot_general x8, matrix products, add(): return total + jnp.dot(columns, moving, preferred_element_type=jnp.float32)  7.69 us
    unnamed x17, local copies, waits for them, and re-layouts  4.09 us
  transfers between devices with their start and end apart: 9, of which 5 were waited for; matrix products, arithmetic and copies ran while one was open for 13% of the time, Pallas kernels for 0%

profile of v3, /device:TPU:2, one launch (start us, length us, event | category | flops | bytes accessed | tf_op | source)
XLA Modules:
  0.0 115.4 jit_solution(471554677165515567)
XLA Ops:
  0.6 1.0 convert_element_type.13
  1.7 1.0 convert_element_type.12
  2.7 0.8 constant_dynamic-update-slice_fusion.4
  3.4 0.0 copy-start.6
  3.4 0.0 copy-start.4
  3.4 0.8 constant_dynamic-update-slice_fusion.3
  4.2 0.7 constant_dynamic-update-slice_fusion.2
  4.9 0.8 pad_maximum_fusion
  5.7 2.2 %collective-permute-start = (bf16[80,3072]{1,0:T(8,128)(2,1)}, bf16[80,3072]{1,0:T(8,128)(2,1)S(1)}, u32[]{:S(2)}, u32[]{:S(2)}) collective-permute-start(bf16[80,3072]{1,0:T(8,128)(2,1)} %pad_maximum_fusion), channel_id=1, source_target_pairs={{0,254},{1,255},{2,0},{3,1},{4,2},{5,3},{6,4},{7,5},{8,6},{9,7},{1... | collective-permute-start | bytes 1474568 | tf_op jit(solution)/shard_map/ppermute | solution.py:22
  8.0 0.0 collective-permute-start.1
  8.0 0.0 copy-done.5
  8.0 0.0 collective-permute-start.6
  8.0 0.0 copy-done.6
  8.0 0.5 collective-permute-start.7
  8.5 0.0 copy-done.4
  8.5 0.3 fusion.21
  8.9 10.1 %collective-permute-done = bf16[80,3072]{1,0:T(8,128)(2,1)S(1)} collective-permute-done((bf16[80,3072]{1,0:T(8,128)(2,1)}, bf16[80,3072]{1,0:T(8,128)(2,1)S(1)}, u32[]{:S(2)}, u32[]{:S(2)}) %collective-permute-start) | collective-permute-done | bytes 491552 | tf_op jit(solution)/shard_map/ppermute | solution.py:22
  18.9 8.7 %collective-permute-start.3 = (bf16[80,3072]{1,0:T(8,128)(2,1)S(1)}, bf16[80,3072]{1,0:T(8,128)(2,1)S(1)}, u32[]{:S(2)}, u32[]{:S(2)}) collective-permute-start(bf16[80,3072]{1,0:T(8,128)(2,1)S(1)} %collective-permute-done), channel_id=1, source_target_pairs={{0,254},{1,255},{2,0},{3,1},{4,2},{5,3},{6,4},{7,5},{8,6},{9,7},{1... | collective-permute-start | bytes 1474568 | tf_op jit(solution)/shard_map/ppermute | solution.py:22
  27.6 0.5 collective-permute-done.1
  28.1 0.0 collective-permute-start.4
  28.1 0.9 constant_dynamic-update-slice_fusion.1
  29.0 0.0 copy-start.7
  29.0 1.9 %constant_dynamic-update-slice_fusion = bf16[80,9216]{1,0:T(8,128)(2,1)} fusion(bf16[80,9216]{1,0:T(8,128)(2,1)} %constant_dynamic-update-slice_fusion.1, bf16[80,3072]{1,0:T(8,128)(2,1)} %collective-permute-done.1), kind=kLoop, calls=%fused_computation.56 | loop fusion | bytes 983040 | tf_op jit(solution)/shard_map/concatenate | solution.py:73
  30.8 0.0 collective-permute-start.2
  30.8 6.4 %collective-permute-done.3 = bf16[80,3072]{1,0:T(8,128)(2,1)S(1)} collective-permute-done((bf16[80,3072]{1,0:T(8,128)(2,1)S(1)}, bf16[80,3072]{1,0:T(8,128)(2,1)S(1)}, u32[]{:S(2)}, u32[]{:S(2)}) %collective-permute-start.3) | collective-permute-done | bytes 491552 | tf_op jit(solution)/shard_map/ppermute | solution.py:22
  37.2 8.5 %collective-permute-done.4 = bf16[80,3072]{1,0:T(8,128)(2,1)S(1)} collective-permute-done((bf16[80,3072]{1,0:T(8,128)(2,1)}, bf16[80,3072]{1,0:T(8,128)(2,1)S(1)}, u32[]{:S(2)}, u32[]{:S(2)}) %collective-permute-start.4) | collective-permute-done | bytes 491552 | tf_op jit(solution)/shard_map/ppermute | solution.py:22
  45.7 0.0 copy-start.1
  45.7 0.8 copy-done.1
  46.5 0.8 broadcast_select_fusion
  47.3 0.0 collective-permute-start.5
  47.3 0.0 copy-done.7
  47.3 0.0 collective-permute-done.6
  47.3 0.1 pad_add_fusion
  47.4 0.1 copy.14
  47.5 0.3 convolution_add_fusion.1
  47.8 1.7 %collective-permute-done.5 = bf16[80,3072]{1,0:T(8,128)(2,1)} collective-permute-done((bf16[80,3072]{1,0:T(8,128)(2,1)}, bf16[80,3072]{1,0:T(8,128)(2,1)}, u32[]{:S(2)}, u32[]{:S(2)}) %collective-permute-start.5) | collective-permute-done | bytes 491552 | tf_op jit(solution)/shard_map/ppermute | solution.py:27
  49.5 1.4 %fusion.23 = f32[80,3072]{1,0:T(8,128)S(1)} fusion(bf16[80,3072]{1,0:T(8,128)(2,1)} %collective-permute-done.5, pred[]{:T(512)S(6)} %eq.19, bf16[80,720]{1,0:T(8,128)(2,1)S(1)} %convert_element_type.14), kind=kOutput, calls=%fused_computation.37 | convolution fusion | flops 39328000 | bytes 1515521 | tf_op jit(solution)/shard_map/dot_general | solution.py:63
  50.9 0.0 collective-permute-done.2
  50.9 1.4 %fusion.13 = f32[80,3072]{1,0:T(8,128)S(1)} fusion(bf16[80,9216]{1,0:T(8,128)(2,1)} %collective-permute-done.2, pred[]{:T(512)S(6)} %eq.19, bf16[80,720]{1,0:T(8,128)(2,1)S(1)} %convert_element_type.14), kind=kOutput, calls=%fused_computation.19 | convolution fusion | flops 39328000 | bytes 1515521 | tf_op jit(solution)/shard_map/dot_general | solution.py:63
  52.2 1.4 %fusion.15 = f32[80,3072]{1,0:T(8,128)S(1)} fusion(bf16[80,9216]{1,0:T(8,128)(2,1)} %collective-permute-done.2, pred[]{:T(512)S(6)} %eq.19, bf16[80,720]{1,0:T(8,128)(2,1)S(1)} %convert_element_type.14), kind=kOutput, calls=%fused_computation.21 | convolution fusion | flops 39328000 | bytes 1515521 | tf_op jit(solution)/shard_map/dot_general | solution.py:63
  53.6 1.4 %fusion.11 = f32[80,3072]{1,0:T(8,128)S(1)} fusion(bf16[80,9216]{1,0:T(8,128)(2,1)} %collective-permute-done.2, pred[]{:T(512)S(6)} %eq.19, bf16[80,720]{1,0:T(8,128)(2,1)S(1)} %convert_element_type.14), kind=kOutput, calls=%fused_computation.17 | convolution fusion | flops 39328000 | bytes 1515521 | tf_op jit(solution)/shard_map/dot_general | solution.py:63
  55.0 1.4 %fusion.3 = f32[80,3072]{1,0:T(8,128)S(1)} fusion(f32[80,3072]{1,0:T(8,128)S(1)} %fusion.11, f32[80,3072]{1,0:T(8,128)S(1)} %fusion.13, f32[80,3072]{1,0:T(8,128)S(1)} %fusion.15, f32[3072,80]{0,1:T(8,128)S(1)} %convolution_add_fusion.1, bf16[80,3072]{1,0:T(8,128)(2,1)} %collective-permute-done.1, bf16[80,720]{1,0:T(8,128)(2,1)S(1)} %convert_element_type.14), kind=kOutput, calls=%fused_computation.6 | convolution fusion | flops 40304640 | bytes 5427200 | tf_op jit(solution)/shard_map/dot_general | solution.py:63
  56.4 0.0 copy-start.2
  56.4 0.3 fusion.7
  56.7 0.7 copy-done.2
  57.4 0.0 copy-start
  57.4 0.3 fusion.6
  57.7 0.2 subtract_convert_fusion.1
  57.9 1.6 %copy-done = bf16[2048,1024]{1,0:T(8,128)(2,1)S(1)} copy-done((bf16[2048,1024]{1,0:T(8,128)(2,1)S(1)}, bf16[2048,1024]{1,0:T(8,128)(2,1)}, u32[]{:S(2)}) %copy-start) | copy-done | bytes 4194328
  59.6 0.8 fusion.41
  60.4 0.0 copy-done.3
  60.4 0.2 collective-permute-start.8
  60.7 0.0 collective-permute-done.7
  60.7 0.1 pad_maximum_fusion.2
  60.7 0.1 copy.15
  60.8 1.2 %select_reduce_fusion = f32[512,160]{0,1:T(8,128)S(1)} fusion(f32[160,16]{1,0:T(8,128)S(1)} %copy.15, s32[512]{0:T(512)S(1)} %broadcast_add_fusion, s32[160,16]{1,0:T(8,128)S(1)} %copy.14), kind=kLoop, calls=%fused_computation | loop fusion | flops 3850240 | bytes 350208 | tf_op jit(solution)/shard_map/reduce_sum | solution.py:93
  62.1 0.2 copy.18
  62.3 0.0 collective-permute-done.8
  62.3 1.8 %fusion.8 = f32[8,64,1024]{2,1,0:T(8,128)S(1)} fusion(f32[8,64,160]{2,1,0:T(8,128)S(1)} %bitcast.32, f32[80,1024]{1,0:T(8,128)S(1)} %collective-permute-done.8, f32[80,1024]{1,0:T(8,128)S(1)} %fusion.41), kind=kOutput, calls=%fused_computation.14 | convolution fusion | flops 1006796800 | bytes 3080192 | tf_op jit(solution)/shard_map/dot_general | solution.py:94
  64.1 35.4 %all_to_all.10 = f32[8,64,1024]{2,1,0:T(8,128)S(1)} all-to-all(f32[8,64,1024]{2,1,0:T(8,128)S(1)} %fusion.8), channel_id=1, replica_groups=mesh['y'=4,'z'=4,'x'=8,'c'=2] {'x'}, dimensions={0} | all-to-all | bytes 4194304 | tf_op jit(solution)/shard_map/all_to_all | solution.py:98
  99.5 0.1 reduce_sum.28
  99.6 0.1 reshape.12
  99.7 15.1 %all_to_all.11 = f32[16,4,1024]{2,1,0:T(4,128)S(1)} all-to-all(f32[16,4,1024]{2,1,0:T(4,128)S(1)} %reshape.12), channel_id=1, replica_groups=mesh['y'=4,'z'=4,'x'=8,'c'=2] {'z','y'}, dimensions={0} | all-to-all | bytes 524288 | tf_op jit(solution)/shard_map/all_to_all | solution.py:98
  114.8 0.7 reduce_sum.29
  (5 shorter events, 0.0 us)
Async XLA Ops:
  3.4 4.6 %copy-start.5 = (s32[80,16]{0,1:T(8,128)S(1)}, s32[80,16]{0,1:T(8,128)}, u32[]{:S(2)}) copy-start(s32[80,16]{0,1:T(8,128)} %param.10) | copy-start | bytes 15364
  3.4 4.6 %copy-start.6 = (f32[80,16]{0,1:T(8,128)S(1)}, f32[80,16]{0,1:T(8,128)}, u32[]{:S(2)}) copy-start(f32[80,16]{0,1:T(8,128)} %param.11) | copy-start | bytes 15364
  3.4 5.1 %copy-start.4 = (s32[80,720]{1,0:T(8,128)S(1)}, s32[80,720]{1,0:T(8,128)}, u32[]{:S(2)}) copy-start(s32[80,720]{1,0:T(8,128)} %param.9) | copy-start | bytes 691204
  5.7 13.2 %collective-permute-start = (bf16[80,3072]{1,0:T(8,128)(2,1)}, bf16[80,3072]{1,0:T(8,128)(2,1)S(1)}, u32[]{:S(2)}, u32[]{:S(2)}) collective-permute-start(bf16[80,3072]{1,0:T(8,128)(2,1)} %pad_maximum_fusion), channel_id=1, source_target_pairs={{0,254},{1,255},{2,0},{3,1},{4,2},{5,3},{6,4},{7,5},{8,6},{9,7},{1... | collective-permute-start | bytes 1474568 | tf_op jit(solution)/shard_map/ppermute | solution.py:22
  8.0 20.1 %collective-permute-start.1 = (bf16[80,3072]{1,0:T(8,128)(2,1)}, bf16[80,3072]{1,0:T(8,128)(2,1)}, u32[]{:S(2)}, u32[]{:S(2)}) collective-permute-start(bf16[80,3072]{1,0:T(8,128)(2,1)} %pad_maximum_fusion), channel_id=1, source_target_pairs={{0,2},{1,3},{2,4},{3,5},{4,6},{5,7},{6,8},{7,9},{8,10},{9,11},{10,... | collective-permute-start | bytes 1474568 | tf_op jit(solution)/shard_map/ppermute | solution.py:22
  8.0 39.3 %collective-permute-start.6 = (s32[80,16]{0,1:T(8,128)S(1)}, s32[80,16]{0,1:T(8,128)S(1)}, u32[]{:S(2)}, u32[]{:S(2)}) collective-permute-start(s32[80,16]{0,1:T(8,128)S(1)} %copy-done.5), channel_id=1, source_target_pairs={{0,1},{1,0},{2,3},{3,2},{4,5},{5,4},{6,7},{7,6},{8,9},{9,8},{10,11... | collective-permute-start | bytes 15368 | tf_op jit(solution)/shard_map/ppermute | solution.py:27
  8.0 52.7 %collective-permute-start.7 = (f32[80,16]{0,1:T(8,128)S(1)}, f32[80,16]{0,1:T(8,128)S(1)}, u32[]{:S(2)}, u32[]{:S(2)}) collective-permute-start(f32[80,16]{0,1:T(8,128)S(1)} %copy-done.6), channel_id=1, source_target_pairs={{0,1},{1,0},{2,3},{3,2},{4,5},{5,4},{6,7},{7,6},{8,9},{9,8},{10,11... | collective-permute-start | bytes 15368 | tf_op jit(solution)/shard_map/ppermute | solution.py:27
  18.9 18.3 %collective-permute-start.3 = (bf16[80,3072]{1,0:T(8,128)(2,1)S(1)}, bf16[80,3072]{1,0:T(8,128)(2,1)S(1)}, u32[]{:S(2)}, u32[]{:S(2)}) collective-permute-start(bf16[80,3072]{1,0:T(8,128)(2,1)S(1)} %collective-permute-done), channel_id=1, source_target_pairs={{0,254},{1,255},{2,0},{3,1},{4,2},{5,3},{6,4},{7,5},{8,6},{9,7},{1... | collective-permute-start | bytes 1474568 | tf_op jit(solution)/shard_map/ppermute | solution.py:22
  28.1 17.6 %collective-permute-start.4 = (bf16[80,3072]{1,0:T(8,128)(2,1)}, bf16[80,3072]{1,0:T(8,128)(2,1)S(1)}, u32[]{:S(2)}, u32[]{:S(2)}) collective-permute-start(bf16[80,3072]{1,0:T(8,128)(2,1)} %collective-permute-done.1), channel_id=1, source_target_pairs={{0,2},{1,3},{2,4},{3,5},{4,6},{5,7},{6,8},{7,9},{8,10},{9,11},{10,... | collective-permute-start | bytes 1474568 | tf_op jit(solution)/shard_map/ppermute | solution.py:22
  29.0 18.4 %copy-start.7 = (s32[512]{0:T(512)S(1)}, s32[512]{0:T(512)}, u32[]{:S(2)}) copy-start(s32[512]{0:T(512)} %constant.47.clone) | copy-start | bytes 6148
  30.8 20.0 %collective-permute-start.2 = (bf16[80,9216]{1,0:T(8,128)(2,1)}, bf16[80,9216]{1,0:T(8,128)(2,1)}, u32[]{:S(2)}, u32[]{:S(2)}) collective-permute-start(bf16[80,9216]{1,0:T(8,128)(2,1)} %constant_dynamic-update-slice_fusion), channel_id=1, source_target_pairs={{0,1},{1,0},{2,3},{3,2},{4,5},{5,4},{6,7},{7,6},{8,9},{9,8},{10,11... | collective-permute-start | bytes 4423688 | tf_op jit(solution)/shard_map/ppermute | solution.py:27
  45.7 0.8 copy-start.1
  47.3 2.2 %collective-permute-start.5 = (bf16[80,3072]{1,0:T(8,128)(2,1)}, bf16[80,3072]{1,0:T(8,128)(2,1)}, u32[]{:S(2)}, u32[]{:S(2)}) collective-permute-start(bf16[80,3072]{1,0:T(8,128)(2,1)} %broadcast_select_fusion), channel_id=1, source_target_pairs={{0,1},{1,0},{2,3},{3,2},{4,5},{5,4},{6,7},{7,6},{8,9},{9,8},{10,11... | collective-permute-start | bytes 1474568 | tf_op jit(solution)/shard_map/ppermute | solution.py:27
  56.4 1.0 copy-start.2
  57.4 2.2 %copy-start = (bf16[2048,1024]{1,0:T(8,128)(2,1)S(1)}, bf16[2048,1024]{1,0:T(8,128)(2,1)}, u32[]{:S(2)}) copy-start(bf16[2048,1024]{1,0:T(8,128)(2,1)} %param.12) | copy-start | bytes 12582916
  59.6 0.9 copy-start.3
  60.4 1.8 %collective-permute-start.8 = (f32[80,1024]{1,0:T(8,128)S(1)}, f32[80,1024]{1,0:T(8,128)S(1)}, u32[]{:S(2)}, u32[]{:S(2)}) collective-permute-start(f32[80,1024]{1,0:T(8,128)S(1)} %fusion.41), channel_id=1, source_target_pairs={{0,1},{1,0},{2,3},{3,2},{4,5},{5,4},{6,7},{7,6},{8,9},{9,8},{10,11... | collective-permute-start | bytes 983048 | tf_op jit(solution)/shard_map/ppermute | solution.py:27

commit v4 on v3

--- a/solution.py
+++ b/solution.py
@@ -36,7 +36,7 @@
     return flat.transpose(perm).reshape(-1).astype(np.int32)
 
 
-def local(records, green, pair_mask, tile_lists, tile_weights, tile_green):
+def body(records, green, pair_mask, tile_lists, tile_weights, tile_green):
     count = int(np.prod(SIZES))
     rec = records.astype(jnp.float32)
     grn = green.astype(jnp.float32)
@@ -62,13 +62,21 @@
     def add(total, columns, moving):
         return total + jnp.dot(columns, moving, preferred_element_type=jnp.float32)
 
+    lists = jnp.concatenate([tile_lists, swap(tile_lists, count)], axis=0)
+    weights = jnp.concatenate([tile_weights, swap(tile_weights, count)], axis=0)
     ahead = shifted(both, -2, count)
     behind = shifted(both, 2, count)
+    ahead2 = shifted(ahead, -2, count)
+    behind2 = shifted(behind, 2, count)
     total = jnp.dot(cols(HALF), both, preferred_element_type=jnp.float32)
     total = add(total, cols(HALF + 2), ahead)
     total = add(total, cols(HALF - 2), behind)
-    ahead2 = shifted(ahead, -2, count)
-    behind2 = shifted(behind, 2, count)
+    tile_ids = jnp.asarray(tile_order()[: TT * count // SIZES[-1]]) + TT * (
+        lax.axis_index(SUB) % 2
+    )
+    onehot = (lists[None, :, :] == tile_ids[:, None, None]).astype(jnp.float32)
+    tile_map = jnp.sum(onehot * weights[None, :, :], axis=2)
+    total, tile_map = lax.optimization_barrier((total, tile_map))
     width = both.shape[1]
     swapped = swap(jnp.concatenate([both, ahead, behind], axis=1), count)
     total = add(total, picked(HALF + 1, HALF - 1), swapped[:, :width])
@@ -86,11 +94,6 @@
     adjoint = jnp.concatenate([adj_real, adj_imag], axis=1).astype(jnp.bfloat16)
     response = jnp.dot(adjoint, tile_green, preferred_element_type=jnp.float32)
     responses = jnp.concatenate([response, swap(response, count)], axis=0)
-    lists = jnp.concatenate([tile_lists, swap(tile_lists, count)], axis=0)
-    weights = jnp.concatenate([tile_weights, swap(tile_weights, count)], axis=0)
-    tile_ids = jnp.asarray(tile_order()[: TT * count // SIZES[-1]]) + TT * (lax.axis_index(SUB) % 2)
-    onehot = (lists[None, :, :] == tile_ids[:, None, None]).astype(jnp.float32)
-    tile_map = jnp.sum(onehot * weights[None, :, :], axis=2)
     part = jnp.dot(tile_map, responses, precision=lax.Precision.HIGHEST)
     for group in STAGES:
         ways = int(np.prod([SIZES[SUB.index(a)] for a in group]))
@@ -104,7 +107,7 @@
     grid = Mesh(devices, SUB)
     rows = P(SUB, None)
     return jax.shard_map(
-        local,
+        body,
         mesh=grid,
         in_specs=(rows,) * 6,
         out_specs=(rows, rows),

time: 116 us -> 107 us (0.922)
  matrix products: 10.7 us -> 6.54 us
  local copies, waits for them, and re-layouts: 6.45 us -> 4.24 us
  waiting for transfers between devices: 27.1 us -> 25.7 us
    dot_general x8, matrix products: 7.69 us -> 2.55 us  [add(): return total + jnp.dot(columns, moving, preferred_element_type=jnp.float32)]
    ppermute x4, waiting for transfers between devices: 25.4 us -> 23 us  [shifted(): return lax.ppermute(value, SUB, pairs)]
    unnamed x17 -> x21, local copies, waits for them, and re-layouts: 4.09 us -> 3.14 us
  transfers between devices with their start and end apart: 9 -> 9, of which waited for: 5 -> 6; matrix products, arithmetic and copies ran while one was open for 13% -> 5% of each run, Pallas kernels for 0% -> 0%
where the time goes in v4:
time: 107 us; the launch traced here: 106 us
  blocking collectives  49.5 us (46%)
  waiting for transfers between devices  25.7 us (24%)
  starting transfers between devices  11.7 us (11%)
  other arithmetic  7.66 us (7%)
  matrix products  6.54 us (6%)
  local copies, waits for them, and re-layouts  4.24 us (4%)
    all_to_all x2, blocking collectives, body(): part = jnp.sum(lax.all_to_all(part, group, 0, 0, tiled=False), axis=0)  49.5 us
    ppermute x4, waiting for transfers between devices, shifted(): return lax.ppermute(value, SUB, pairs)  23 us
    ppermute x4, starting transfers between devices, shifted(): return lax.ppermute(value, SUB, pairs)  10.9 us
    unnamed x21, local copies, waits for them, and re-layouts  3.14 us
    ppermute x5, waiting for transfers between devices, swap(): return lax.ppermute(value, SUB, pairs)  2.67 us
    dot_general x8, matrix products, add(): return total + jnp.dot(columns, moving, preferred_element_type=jnp.float32)  2.55 us
    unnamed x3, other arithmetic  2.29 us
  transfers between devices with their start and end apart: 9, of which 6 were waited for; matrix products, arithmetic and copies ran while one was open for 5% of the time, Pallas kernels for 0%

profile of v4, /device:TPU:2, one launch (start us, length us, event | category | flops | bytes accessed | tf_op | source)
XLA Modules:
  0.0 106.2 jit_solution(16906580867636868558)
XLA Ops:
  0.6 1.0 convert_element_type.13
  1.7 1.0 convert_element_type.12
  2.7 0.8 constant_dynamic-update-slice_fusion.4
  3.5 0.0 copy-start.7
  3.5 0.0 copy-start.8
  3.5 0.0 copy-start.6
  3.5 0.8 constant_dynamic-update-slice_fusion.3
  4.3 0.7 constant_dynamic-update-slice_fusion.2
  5.0 0.8 pad_maximum_fusion
  5.8 2.2 %collective-permute-start = (bf16[80,3072]{1,0:T(8,128)(2,1)}, bf16[80,3072]{1,0:T(8,128)(2,1)S(1)}, u32[]{:S(2)}, u32[]{:S(2)}) collective-permute-start(bf16[80,3072]{1,0:T(8,128)(2,1)} %pad_maximum_fusion), channel_id=1, source_target_pairs={{0,254},{1,255},{2,0},{3,1},{4,2},{5,3},{6,4},{7,5},{8,6},{9,7},{1... | collective-permute-start | bytes 1474568 | tf_op jit(solution)/shard_map/ppermute | solution.py:22
  8.1 0.0 collective-permute-start.1
  8.1 0.0 copy-done.7
  8.1 0.0 collective-permute-start.2
  8.1 0.0 copy-done.8
  8.1 0.5 collective-permute-start.3
  8.6 0.0 copy-done.1
  8.6 0.0 copy-done.2
  8.6 0.0 copy-done.6
  8.6 0.0 copy-start.4
  8.6 0.6 copy-done.4
  9.3 1.3 %fusion.19 = f32[3072,80]{0,1:T(8,128)S(1)} fusion(bf16[80,720]{1,0:T(8,128)(2,1)S(1)} %convert_element_type.14, bf16[80,1024]{1,0:T(8,128)(2,1)} %copy-done.2, bf16[80,1024]{1,0:T(8,128)(2,1)} %copy-done.1, bf16[80,1024]{1,0:T(8,128)(2,1)S(1)} %get-tuple-element.11), kind=kOutput, calls=%fused_computation.32 | convolution fusion | flops 40796160 | bytes 1495040 | tf_op jit(solution)/shard_map/dot_general | solution.py:71
  10.6 0.0 copy-done.9
  10.6 0.0 collective-permute-done.2
  10.6 0.1 pad_add_fusion
  10.7 0.1 copy.13
  10.8 0.0 collective-permute-done.3
  10.8 0.1 pad_maximum_fusion.2
  10.9 0.1 copy.14
  11.0 1.2 %select_reduce_fusion = f32[512,160]{0,1:T(8,128)S(1)} fusion(f32[160,16]{1,0:T(8,128)S(1)} %copy.14, s32[512]{0:T(512)S(1)} %broadcast_add_fusion, s32[160,16]{1,0:T(8,128)S(1)} %copy.13), kind=kLoop, calls=%fused_computation | loop fusion | flops 3850240 | bytes 350208 | tf_op jit(solution)/shard_map/reduce_sum | solution.py:78
  12.2 6.8 %collective-permute-done = bf16[80,3072]{1,0:T(8,128)(2,1)S(1)} collective-permute-done((bf16[80,3072]{1,0:T(8,128)(2,1)}, bf16[80,3072]{1,0:T(8,128)(2,1)S(1)}, u32[]{:S(2)}, u32[]{:S(2)}) %collective-permute-start) | collective-permute-done | bytes 491552 | tf_op jit(solution)/shard_map/ppermute | solution.py:22
  19.0 8.7 %collective-permute-start.5 = (bf16[80,3072]{1,0:T(8,128)(2,1)S(1)}, bf16[80,3072]{1,0:T(8,128)(2,1)S(1)}, u32[]{:S(2)}, u32[]{:S(2)}) collective-permute-start(bf16[80,3072]{1,0:T(8,128)(2,1)S(1)} %collective-permute-done), channel_id=1, source_target_pairs={{0,254},{1,255},{2,0},{3,1},{4,2},{5,3},{6,4},{7,5},{8,6},{9,7},{1... | collective-permute-start | bytes 1474568 | tf_op jit(solution)/shard_map/ppermute | solution.py:22
  27.7 0.4 collective-permute-done.1
  28.0 0.0 collective-permute-start.6
  28.1 0.8 constant_dynamic-update-slice_fusion.1
  28.9 0.8 constant_dynamic-update-slice_fusion
  29.7 0.0 collective-permute-start.4
  29.7 7.6 %collective-permute-done.5 = bf16[80,3072]{1,0:T(8,128)(2,1)S(1)} collective-permute-done((bf16[80,3072]{1,0:T(8,128)(2,1)S(1)}, bf16[80,3072]{1,0:T(8,128)(2,1)S(1)}, u32[]{:S(2)}, u32[]{:S(2)}) %collective-permute-start.5) | collective-permute-done | bytes 491552 | tf_op jit(solution)/shard_map/ppermute | solution.py:22
  37.3 8.3 %collective-permute-done.6 = bf16[80,3072]{1,0:T(8,128)(2,1)S(1)} collective-permute-done((bf16[80,3072]{1,0:T(8,128)(2,1)S(1)}, bf16[80,3072]{1,0:T(8,128)(2,1)S(1)}, u32[]{:S(2)}, u32[]{:S(2)}) %collective-permute-start.6) | collective-permute-done | bytes 491552 | tf_op jit(solution)/shard_map/ppermute | solution.py:22
  45.6 0.1 broadcast_select_fusion
  45.6 0.1 collective-permute-start.7
  45.7 0.0 copy-done.5
  45.7 0.3 convolution_add_fusion.1
  46.1 0.3 fusion
  46.4 1.2 %collective-permute-done.7 = bf16[80,3072]{1,0:T(8,128)(2,1)S(1)} collective-permute-done((bf16[80,3072]{1,0:T(8,128)(2,1)S(1)}, bf16[80,3072]{1,0:T(8,128)(2,1)S(1)}, u32[]{:S(2)}, u32[]{:S(2)}) %collective-permute-start.7) | collective-permute-done | bytes 491552 | tf_op jit(solution)/shard_map/ppermute | solution.py:27
  47.6 0.3 fusion.21
  47.9 0.0 collective-permute-done.4
  47.9 0.3 fusion.11
  48.2 0.3 fusion.13
  48.6 0.3 fusion.9
  48.9 0.3 fusion.4
  49.2 0.0 copy-start
  49.2 0.3 fusion.3
  49.5 0.2 subtract_convert_fusion.1
  49.8 1.6 %copy-done = bf16[2048,1024]{1,0:T(8,128)(2,1)S(1)} copy-done((bf16[2048,1024]{1,0:T(8,128)(2,1)S(1)}, bf16[2048,1024]{1,0:T(8,128)(2,1)}, u32[]{:S(2)}) %copy-start) | copy-done | bytes 4194328
  51.4 0.8 fusion.39
  52.3 0.0 copy-done.3
  52.3 0.2 collective-permute-start.8
  52.5 1.5 %collective-permute-done.8 = f32[80,1024]{1,0:T(8,128)S(1)} collective-permute-done((f32[80,1024]{1,0:T(8,128)S(1)}, f32[80,1024]{1,0:T(8,128)S(1)}, u32[]{:S(2)}, u32[]{:S(2)}) %collective-permute-start.8) | collective-permute-done | bytes 327712 | tf_op jit(solution)/shard_map/ppermute | solution.py:27
  54.0 1.8 %fusion.5 = f32[512,1024]{1,0:T(8,128)S(1)} fusion(f32[512,160]{0,1:T(8,128)S(1)} %select_reduce_fusion, f32[80,1024]{1,0:T(8,128)S(1)} %collective-permute-done.8, f32[80,1024]{1,0:T(8,128)S(1)} %fusion.39), kind=kOutput, calls=%fused_computation.10 | convolution fusion | flops 1006796800 | bytes 3080192 | tf_op jit(solution)/shard_map/dot_general | solution.py:97
  55.8 35.3 %all_to_all.10 = f32[8,64,1024]{2,1,0:T(8,128)S(1)} all-to-all(f32[8,64,1024]{2,1,0:T(8,128)S(1)} %bitcast.23), channel_id=1, replica_groups=mesh['y'=4,'z'=4,'x'=8,'c'=2] {'x'}, dimensions={0} | all-to-all | bytes 4194304 | tf_op jit(solution)/shard_map/all_to_all | solution.py:101
  91.1 0.1 reduce_sum.28
  91.2 0.1 reshape.14
  91.3 14.3 %all_to_all.11 = f32[16,4,1024]{2,1,0:T(4,128)S(1)} all-to-all(f32[16,4,1024]{2,1,0:T(4,128)S(1)} %reshape.14), channel_id=1, replica_groups=mesh['y'=4,'z'=4,'x'=8,'c'=2] {'z','y'}, dimensions={0} | all-to-all | bytes 524288 | tf_op jit(solution)/shard_map/all_to_all | solution.py:101
  105.6 0.7 reduce_sum.29
  (8 shorter events, 0.1 us)
Async XLA Ops:
  3.5 4.6 %copy-start.7 = (s32[80,16]{0,1:T(8,128)S(1)}, s32[80,16]{0,1:T(8,128)}, u32[]{:S(2)}) copy-start(s32[80,16]{0,1:T(8,128)} %param.10) | copy-start | bytes 15364
  3.5 4.6 %copy-start.8 = (f32[80,16]{0,1:T(8,128)S(1)}, f32[80,16]{0,1:T(8,128)}, u32[]{:S(2)}) copy-start(f32[80,16]{0,1:T(8,128)} %param.11) | copy-start | bytes 15364
  3.5 5.1 %copy-start.6 = (s32[80,720]{1,0:T(8,128)S(1)}, s32[80,720]{1,0:T(8,128)}, u32[]{:S(2)}) copy-start(s32[80,720]{1,0:T(8,128)} %param.9) | copy-start | bytes 691204
  4.2 4.3 %copy-start.1 = (bf16[80,1024]{1,0:T(8,128)(2,1)}, bf16[80,1024]{1,0:T(8,128)(2,1)S(1)}, u32[]{:S(2)}) copy-start(bf16[80,1024]{1,0:T(8,128)(2,1)S(1)} %get-tuple-element.9) | copy-start | bytes 491524
  5.0 3.6 %copy-start.2 = (bf16[80,1024]{1,0:T(8,128)(2,1)}, bf16[80,1024]{1,0:T(8,128)(2,1)S(1)}, u32[]{:S(2)}) copy-start(bf16[80,1024]{1,0:T(8,128)(2,1)S(1)} %get-tuple-element.7) | copy-start | bytes 491524
  5.0 5.6 %copy-start.9 = (s32[512]{0:T(512)S(1)}, s32[512]{0:T(512)}, u32[]{:S(2)}) copy-start(s32[512]{0:T(512)} %constant.47.clone) | copy-start | bytes 6148
  5.8 13.2 %collective-permute-start = (bf16[80,3072]{1,0:T(8,128)(2,1)}, bf16[80,3072]{1,0:T(8,128)(2,1)S(1)}, u32[]{:S(2)}, u32[]{:S(2)}) collective-permute-start(bf16[80,3072]{1,0:T(8,128)(2,1)} %pad_maximum_fusion), channel_id=1, source_target_pairs={{0,254},{1,255},{2,0},{3,1},{4,2},{5,3},{6,4},{7,5},{8,6},{9,7},{1... | collective-permute-start | bytes 1474568 | tf_op jit(solution)/shard_map/ppermute | solution.py:22
  8.1 20.0 %collective-permute-start.1 = (bf16[80,3072]{1,0:T(8,128)(2,1)}, bf16[80,3072]{1,0:T(8,128)(2,1)S(1)}, u32[]{:S(2)}, u32[]{:S(2)}) collective-permute-start(bf16[80,3072]{1,0:T(8,128)(2,1)} %pad_maximum_fusion), channel_id=1, source_target_pairs={{0,2},{1,3},{2,4},{3,5},{4,6},{5,7},{6,8},{7,9},{8,10},{9,11},{10,... | collective-permute-start | bytes 1474568 | tf_op jit(solution)/shard_map/ppermute | solution.py:22
  8.1 2.5 %collective-permute-start.2 = (s32[80,16]{0,1:T(8,128)S(1)}, s32[80,16]{0,1:T(8,128)S(1)}, u32[]{:S(2)}, u32[]{:S(2)}) collective-permute-start(s32[80,16]{0,1:T(8,128)S(1)} %copy-done.7), channel_id=1, source_target_pairs={{0,1},{1,0},{2,3},{3,2},{4,5},{5,4},{6,7},{7,6},{8,9},{9,8},{10,11... | collective-permute-start | bytes 15368 | tf_op jit(solution)/shard_map/ppermute | solution.py:27
  8.1 2.7 %collective-permute-start.3 = (f32[80,16]{0,1:T(8,128)S(1)}, f32[80,16]{0,1:T(8,128)S(1)}, u32[]{:S(2)}, u32[]{:S(2)}) collective-permute-start(f32[80,16]{0,1:T(8,128)S(1)} %copy-done.8), channel_id=1, source_target_pairs={{0,1},{1,0},{2,3},{3,2},{4,5},{5,4},{6,7},{7,6},{8,9},{9,8},{10,11... | collective-permute-start | bytes 15368 | tf_op jit(solution)/shard_map/ppermute | solution.py:27
  8.6 0.7 copy-start.4
  19.0 18.3 %collective-permute-start.5 = (bf16[80,3072]{1,0:T(8,128)(2,1)S(1)}, bf16[80,3072]{1,0:T(8,128)(2,1)S(1)}, u32[]{:S(2)}, u32[]{:S(2)}) collective-permute-start(bf16[80,3072]{1,0:T(8,128)(2,1)S(1)} %collective-permute-done), channel_id=1, source_target_pairs={{0,254},{1,255},{2,0},{3,1},{4,2},{5,3},{6,4},{7,5},{8,6},{9,7},{1... | collective-permute-start | bytes 1474568 | tf_op jit(solution)/shard_map/ppermute | solution.py:22
  28.0 17.5 %collective-permute-start.6 = (bf16[80,3072]{1,0:T(8,128)(2,1)S(1)}, bf16[80,3072]{1,0:T(8,128)(2,1)S(1)}, u32[]{:S(2)}, u32[]{:S(2)}) collective-permute-start(bf16[80,3072]{1,0:T(8,128)(2,1)S(1)} %collective-permute-done.1), channel_id=1, source_target_pairs={{0,2},{1,3},{2,4},{3,5},{4,6},{5,7},{6,8},{7,9},{8,10},{9,11},{10,... | collective-permute-start | bytes 1474568 | tf_op jit(solution)/shard_map/ppermute | solution.py:22
  28.9 16.8 %copy-start.5 = (bf16[80,720]{1,0:T(8,128)(2,1)S(1)}, bf16[80,720]{1,0:T(8,128)(2,1)}, u32[]{:S(2)}) copy-start(bf16[80,720]{1,0:T(8,128)(2,1)} %copy-done.4) | copy-start | bytes 345604
  29.7 18.2 %collective-permute-start.4 = (bf16[80,9216]{1,0:T(8,128)(2,1)}, bf16[80,9216]{1,0:T(8,128)(2,1)S(1)}, u32[]{:S(2)}, u32[]{:S(2)}) collective-permute-start(bf16[80,9216]{1,0:T(8,128)(2,1)} %constant_dynamic-update-slice_fusion), channel_id=1, source_target_pairs={{0,1},{1,0},{2,3},{3,2},{4,5},{5,4},{6,7},{7,6},{8,9},{9,8},{10,11... | collective-permute-start | bytes 4423688 | tf_op jit(solution)/shard_map/ppermute | solution.py:27
  45.6 2.0 %collective-permute-start.7 = (bf16[80,3072]{1,0:T(8,128)(2,1)S(1)}, bf16[80,3072]{1,0:T(8,128)(2,1)S(1)}, u32[]{:S(2)}, u32[]{:S(2)}) collective-permute-start(bf16[80,3072]{1,0:T(8,128)(2,1)S(1)} %broadcast_select_fusion), channel_id=1, source_target_pairs={{0,1},{1,0},{2,3},{3,2},{4,5},{5,4},{6,7},{7,6},{8,9},{9,8},{10,11... | collective-permute-start | bytes 1474568 | tf_op jit(solution)/shard_map/ppermute | solution.py:27
  49.2 2.2 %copy-start = (bf16[2048,1024]{1,0:T(8,128)(2,1)S(1)}, bf16[2048,1024]{1,0:T(8,128)(2,1)}, u32[]{:S(2)}) copy-start(bf16[2048,1024]{1,0:T(8,128)(2,1)} %param.12) | copy-start | bytes 12582916
  51.4 0.9 copy-start.3
  52.3 1.7 %collective-permute-start.8 = (f32[80,1024]{1,0:T(8,128)S(1)}, f32[80,1024]{1,0:T(8,128)S(1)}, u32[]{:S(2)}, u32[]{:S(2)}) collective-permute-start(f32[80,1024]{1,0:T(8,128)S(1)} %fusion.39), channel_id=1, source_target_pairs={{0,1},{1,0},{2,3},{3,2},{4,5},{5,4},{6,7},{7,6},{8,9},{9,8},{10,11... | collective-permute-start | bytes 983048 | tf_op jit(solution)/shard_map/ppermute | solution.py:27

commit v5 on v4

--- a/solution.py
+++ b/solution.py
@@ -15,6 +15,7 @@
 SIZES = (4, 4, 8, 2)
 RS_ORDER = ("c", "x", "z", "y")
 STAGES = (("x",), ("z", "y"))
+PIECES = 2
 
 
 def shifted(value, steps, count):
@@ -62,15 +63,27 @@
     def add(total, columns, moving):
         return total + jnp.dot(columns, moving, preferred_element_type=jnp.float32)
 
+    def add_pieces(total, columns, pieces):
+        start = 0
+        for piece in pieces:
+            rows = piece.shape[0]
+            total = add(total, columns[:, start : start + rows], piece)
+            start += rows
+        return total
+
+    def split(value):
+        step = -(-value.shape[0] // (PIECES * 16)) * 16
+        return [value[i : i + step] for i in range(0, value.shape[0], step)]
+
     lists = jnp.concatenate([tile_lists, swap(tile_lists, count)], axis=0)
     weights = jnp.concatenate([tile_weights, swap(tile_weights, count)], axis=0)
-    ahead = shifted(both, -2, count)
-    behind = shifted(both, 2, count)
-    ahead2 = shifted(ahead, -2, count)
-    behind2 = shifted(behind, 2, count)
+    ahead = [shifted(piece, -2, count) for piece in split(both)]
+    behind = [shifted(piece, 2, count) for piece in split(both)]
+    ahead2 = [shifted(piece, -2, count) for piece in ahead]
+    behind2 = [shifted(piece, 2, count) for piece in behind]
     total = jnp.dot(cols(HALF), both, preferred_element_type=jnp.float32)
-    total = add(total, cols(HALF + 2), ahead)
-    total = add(total, cols(HALF - 2), behind)
+    total = add_pieces(total, cols(HALF + 2), ahead)
+    total = add_pieces(total, cols(HALF - 2), behind)
     tile_ids = jnp.asarray(tile_order()[: TT * count // SIZES[-1]]) + TT * (
         lax.axis_index(SUB) % 2
     )
@@ -78,13 +91,15 @@
     tile_map = jnp.sum(onehot * weights[None, :, :], axis=2)
     total, tile_map = lax.optimization_barrier((total, tile_map))
     width = both.shape[1]
-    swapped = swap(jnp.concatenate([both, ahead, behind], axis=1), count)
+    payload = [both, jnp.concatenate(ahead, axis=0), jnp.concatenate(behind, axis=0)]
+    swapped = swap(jnp.concatenate(payload, axis=1), count)
     total = add(total, picked(HALF + 1, HALF - 1), swapped[:, :width])
     total = add(total, picked(HALF + 3, HALF + 1), swapped[:, width : 2 * width])
     total = add(total, picked(HALF - 1, HALF - 3), swapped[:, 2 * width :])
-    total = add(total, cols(HALF + 4), ahead2)
-    total = add(total, cols(HALF - 4), behind2)
-    last = swap(jnp.where(first, ahead2, behind2), count)
+    total = add_pieces(total, cols(HALF + 4), ahead2)
+    total = add_pieces(total, cols(HALF - 4), behind2)
+    farthest = [jnp.where(first, a, b) for a, b in zip(ahead2, behind2)]
+    last = swap(jnp.concatenate(farthest, axis=0), count)
     total = add(total, picked(HALF - 3, HALF + 3), last)
     factor = 1.0 / jnp.sqrt(jnp.float32(WIN * C))
     total = total * factor

time: 107 us -> 117 us (1.093)
  starting transfers between devices: 11.7 us -> 27.1 us
  waiting for transfers between devices: 25.7 us -> 17.7 us
  matrix products: 6.54 us -> 8.73 us
  other arithmetic: 7.66 us -> 9.51 us
  local copies, waits for them, and re-layouts: 4.24 us -> 2.67 us
    ppermute x4 -> x8, starting transfers between devices: 10.9 us -> 26.2 us  [shifted(): return lax.ppermute(value, SUB, pairs)]
    ppermute x4 -> x8, waiting for transfers between devices: 23 us -> 14.5 us  [shifted(): return lax.ppermute(value, SUB, pairs)]
    dot_general x8 -> x12, matrix products: 2.55 us -> 5.72 us  [add(): return total + jnp.dot(columns, moving, preferred_element_type=jnp.float32)]
    unnamed x21 -> x14, local copies, waits for them, and re-layouts: 3.14 us -> 1.65 us
    unnamed x3 -> x4, other arithmetic: 2.29 us -> 3.25 us
  transfers between devices with their start and end apart: 9 -> 13, of which waited for: 6 -> 7; matrix products, arithmetic and copies ran while one was open for 5% -> 7% of each run, Pallas kernels for 0% -> 0%
where the time goes in v5:
time: 117 us; the launch traced here: 116 us
  blocking collectives  49.8 us (43%)
  starting transfers between devices  27.1 us (23%)
  waiting for transfers between devices  17.7 us (15%)
  other arithmetic  9.51 us (8%)
  matrix products  8.73 us (7%)
  local copies, waits for them, and re-layouts  2.67 us (2%)
    all_to_all x2, blocking collectives, body(): part = jnp.sum(lax.all_to_all(part, group, 0, 0, tiled=False), axis=0)  49.8 us
    ppermute x8, starting transfers between devices, shifted(): return lax.ppermute(value, SUB, pairs)  26.2 us
    ppermute x8, waiting for transfers between devices, shifted(): return lax.ppermute(value, SUB, pairs)  14.5 us
    dot_general x12, matrix products, add(): return total + jnp.dot(columns, moving, preferred_element_type=jnp.float32)  5.72 us
    unnamed x4, other arithmetic  3.25 us
    ppermute x5, waiting for transfers between devices, swap(): return lax.ppermute(value, SUB, pairs)  3.23 us
  transfers between devices with their start and end apart: 13, of which 7 were waited for; matrix products, arithmetic and copies ran while one was open for 7% of the time, Pallas kernels for 0%

profile of v5, /device:TPU:2, one launch (start us, length us, event | category | flops | bytes accessed | tf_op | source)
XLA Modules:
  0.0 116.5 jit_solution(15881637378411197936)
XLA Ops:
  0.6 1.0 convert_element_type.13
  1.7 1.0 convert_element_type.12
  2.7 0.8 constant_dynamic-update-slice_fusion.2
  3.5 0.8 constant_dynamic-update-slice_fusion.1
  4.2 0.7 constant_dynamic-update-slice_fusion
  5.0 0.0 copy-start.6
  5.0 0.0 copy-start.5
  5.0 0.7 slice.124
  5.8 2.2 %collective-permute-start = (bf16[48,3072]{1,0:T(8,128)(2,1)}, bf16[48,3072]{1,0:T(8,128)(2,1)S(1)}, u32[]{:S(2)}, u32[]{:S(2)}) collective-permute-start(bf16[48,3072]{1,0:T(8,128)(2,1)} %slice.124), channel_id=1, source_target_pairs={{0,254},{1,255},{2,0},{3,1},{4,2},{5,3},{6,4},{7,5},{8,6},{9,7},{1... | collective-permute-start | bytes 884744 | tf_op jit(solution)/shard_map/ppermute | solution.py:23
  8.0 0.0 collective-permute-start.2
  8.0 0.7 pad_maximum_fusion.3
  8.7 1.3 %collective-permute-start.3 = (bf16[32,3072]{1,0:T(8,128)(2,1)}, bf16[32,3072]{1,0:T(8,128)(2,1)}, u32[]{:S(2)}, u32[]{:S(2)}) collective-permute-start(bf16[32,3072]{1,0:T(8,128)(2,1)} %pad_maximum_fusion.3), channel_id=1, source_target_pairs={{0,2},{1,3},{2,4},{3,5},{4,6},{5,7},{6,8},{7,9},{8,10},{9,11},{10,... | collective-permute-start | bytes 589832 | tf_op jit(solution)/shard_map/ppermute | solution.py:23
  10.0 7.5 %collective-permute-start.1 = (bf16[32,3072]{1,0:T(8,128)(2,1)}, bf16[32,3072]{1,0:T(8,128)(2,1)}, u32[]{:S(2)}, u32[]{:S(2)}) collective-permute-start(bf16[32,3072]{1,0:T(8,128)(2,1)} %pad_maximum_fusion.3), channel_id=1, source_target_pairs={{0,254},{1,255},{2,0},{3,1},{4,2},{5,3},{6,4},{7,5},{8,6},{9,7},{1... | collective-permute-start | bytes 589832 | tf_op jit(solution)/shard_map/ppermute | solution.py:23
  17.5 0.0 collective-permute-start.4
  17.6 0.3 fusion.30
  17.9 0.8 collective-permute-done.4
  18.7 0.2 collective-permute-start.5
  18.9 0.1 pad_add_fusion
  18.9 0.1 copy.13
  19.0 0.8 collective-permute-done.5
  19.9 0.1 pad_maximum_fusion.4
  20.0 0.1 copy.14
  20.1 1.2 %select_reduce_fusion = f32[512,160]{0,1:T(8,128)S(1)} fusion(f32[160,16]{1,0:T(8,128)S(1)} %copy.14, s32[512]{0:T(512)S(1)} %broadcast_add_fusion, s32[160,16]{1,0:T(8,128)S(1)} %copy.13), kind=kLoop, calls=%fused_computation | loop fusion | flops 3850240 | bytes 350208 | tf_op jit(solution)/shard_map/reduce_sum | solution.py:91
  21.3 0.4 collective-permute-done.1
  21.7 7.2 %collective-permute-start.8 = (bf16[32,3072]{1,0:T(8,128)(2,1)}, bf16[32,3072]{1,0:T(8,128)(2,1)S(1)}, u32[]{:S(2)}, u32[]{:S(2)}) collective-permute-start(bf16[32,3072]{1,0:T(8,128)(2,1)} %collective-permute-done.1), channel_id=1, source_target_pairs={{0,254},{1,255},{2,0},{3,1},{4,2},{5,3},{6,4},{7,5},{8,6},{9,7},{1... | collective-permute-start | bytes 589832 | tf_op jit(solution)/shard_map/ppermute | solution.py:23
  28.9 0.0 collective-permute-done.3
  28.9 0.0 collective-permute-start.10
  28.9 1.3 %fusion.24 = f32[3072,80]{0,1:T(8,128)S(1)} fusion(bf16[32,3072]{1,0:T(8,128)(2,1)} %collective-permute-done.3, bf16[80,720]{1,0:T(8,128)(2,1)S(1)} %convert_element_type.14), kind=kOutput, calls=%fused_computation.45 | convolution fusion | flops 15728640 | bytes 1200128 | tf_op jit(solution)/shard_map/dot_general | solution.py:64
  30.2 0.0 collective-permute-done
  30.2 1.0 maximum_dynamic-update-slice_fusion.1
  31.2 0.0 collective-permute-done.2
  31.2 1.0 maximum_dynamic-update-slice_fusion
  32.1 0.1 collective-permute-start.6
  32.2 8.0 %collective-permute-start.7 = (bf16[48,3072]{1,0:T(8,128)(2,1)S(1)}, bf16[48,3072]{1,0:T(8,128)(2,1)S(1)}, u32[]{:S(2)}, u32[]{:S(2)}) collective-permute-start(bf16[48,3072]{1,0:T(8,128)(2,1)S(1)} %collective-permute-done), channel_id=1, source_target_pairs={{0,254},{1,255},{2,0},{3,1},{4,2},{5,3},{6,4},{7,5},{8,6},{9,7},{1... | collective-permute-start | bytes 884744 | tf_op jit(solution)/shard_map/ppermute | solution.py:23
  40.2 0.0 collective-permute-start.9
  40.2 0.3 convolution_add_fusion.1
  40.6 0.3 fusion.26
  40.9 0.0 collective-permute-done.8
  40.9 6.1 %collective-permute-done.7 = bf16[48,3072]{1,0:T(8,128)(2,1)S(1)} collective-permute-done((bf16[48,3072]{1,0:T(8,128)(2,1)S(1)}, bf16[48,3072]{1,0:T(8,128)(2,1)S(1)}, u32[]{:S(2)}, u32[]{:S(2)}) %collective-permute-start.7) | collective-permute-done | bytes 294944 | tf_op jit(solution)/shard_map/ppermute | solution.py:23
  47.1 7.9 %collective-permute-done.9 = bf16[48,3072]{1,0:T(8,128)(2,1)S(1)} collective-permute-done((bf16[48,3072]{1,0:T(8,128)(2,1)S(1)}, bf16[48,3072]{1,0:T(8,128)(2,1)S(1)}, u32[]{:S(2)}, u32[]{:S(2)}) %collective-permute-start.9) | collective-permute-done | bytes 294944 | tf_op jit(solution)/shard_map/ppermute | solution.py:23
  55.1 0.3 collective-permute-start.11
  55.4 1.3 %fusion.2 = f32[80,3072]{1,0:T(8,128)S(1)} fusion(f32[3072,80]{0,1:T(8,128)S(1)} %fusion.24, f32[3072,80]{0,1:T(8,128)S(1)} %fusion.26, f32[3072,80]{0,1:T(8,128)S(1)} %convolution_add_fusion.1, bf16[32,3072]{1,0:T(8,128)(2,1)} %collective-permute-done.1, bf16[80,720]{1,0:T(8,128)(2,1)S(1)} %convert_element_type.14), kind=kOutput, calls=%fused_computation.6 | convolution fusion | flops 16465920 | bytes 4149248 | tf_op jit(solution)/shard_map/dot_general | solution.py:64
  56.6 0.3 convolution_bitcast_fusion
  56.9 0.3 collective-permute-done.11
  57.2 0.3 fusion.32
  57.5 0.0 collective-permute-done.6
  57.5 0.3 fusion.17
  57.9 0.3 fusion.15
  58.2 0.3 fusion.4
  58.6 0.3 fusion.10
  58.8 0.3 fusion.9
  59.2 0.0 copy-start
  59.2 0.3 fusion.8
  59.5 0.2 subtract_convert_fusion.1
  59.7 1.6 %copy-done = bf16[2048,1024]{1,0:T(8,128)(2,1)S(1)} copy-done((bf16[2048,1024]{1,0:T(8,128)(2,1)S(1)}, bf16[2048,1024]{1,0:T(8,128)(2,1)}, u32[]{:S(2)}) %copy-start) | copy-done | bytes 4194328
  61.4 0.8 fusion.50
  62.2 0.3 collective-permute-start.12
  62.6 1.4 %collective-permute-done.12 = f32[80,1024]{1,0:T(8,128)S(1)} collective-permute-done((f32[80,1024]{1,0:T(8,128)S(1)}, f32[80,1024]{1,0:T(8,128)S(1)}, u32[]{:S(2)}, u32[]{:S(2)}) %collective-permute-start.12) | collective-permute-done | bytes 327712 | tf_op jit(solution)/shard_map/ppermute | solution.py:28
  63.9 1.8 %fusion.11 = f32[512,1024]{1,0:T(8,128)S(1)} fusion(f32[512,160]{0,1:T(8,128)S(1)} %select_reduce_fusion, f32[80,1024]{1,0:T(8,128)S(1)} %collective-permute-done.12, f32[80,1024]{1,0:T(8,128)S(1)} %fusion.50), kind=kOutput, calls=%fused_computation.19 | convolution fusion | flops 1006796800 | bytes 3080192 | tf_op jit(solution)/shard_map/dot_general | solution.py:112
  65.8 35.4 %all_to_all.10 = f32[8,64,1024]{2,1,0:T(8,128)S(1)} all-to-all(f32[8,64,1024]{2,1,0:T(8,128)S(1)} %bitcast.35), channel_id=1, replica_groups=mesh['y'=4,'z'=4,'x'=8,'c'=2] {'x'}, dimensions={0} | all-to-all | bytes 4194304 | tf_op jit(solution)/shard_map/all_to_all | solution.py:116
  101.2 0.1 reduce_sum.28
  101.3 0.1 reshape.14
  101.4 14.4 %all_to_all.11 = f32[16,4,1024]{2,1,0:T(4,128)S(1)} all-to-all(f32[16,4,1024]{2,1,0:T(4,128)S(1)} %reshape.14), channel_id=1, replica_groups=mesh['y'=4,'z'=4,'x'=8,'c'=2] {'z','y'}, dimensions={0} | all-to-all | bytes 524288 | tf_op jit(solution)/shard_map/all_to_all | solution.py:116
  115.8 0.7 reduce_sum.29
  (18 shorter events, 0.2 us)
Async XLA Ops:
  4.2 13.3 %copy-start.4 = (s32[80,16]{0,1:T(8,128)S(1)}, s32[80,16]{0,1:T(8,128)}, u32[]{:S(2)}) copy-start(s32[80,16]{0,1:T(8,128)} %param.10) | copy-start | bytes 15364
  4.2 13.3 %copy-start.2 = (s32[80,720]{1,0:T(8,128)S(1)}, s32[80,720]{1,0:T(8,128)}, u32[]{:S(2)}) copy-start(s32[80,720]{1,0:T(8,128)} %param.9) | copy-start | bytes 691204
  5.0 12.9 %copy-start.6 = (s32[512]{0:T(512)S(1)}, s32[512]{0:T(512)}, u32[]{:S(2)}) copy-start(s32[512]{0:T(512)} %constant.47.clone) | copy-start | bytes 6148
  5.0 13.7 %copy-start.5 = (f32[80,16]{0,1:T(8,128)S(1)}, f32[80,16]{0,1:T(8,128)}, u32[]{:S(2)}) copy-start(f32[80,16]{0,1:T(8,128)} %param.11) | copy-start | bytes 15364
  5.8 24.4 %collective-permute-start = (bf16[48,3072]{1,0:T(8,128)(2,1)}, bf16[48,3072]{1,0:T(8,128)(2,1)S(1)}, u32[]{:S(2)}, u32[]{:S(2)}) collective-permute-start(bf16[48,3072]{1,0:T(8,128)(2,1)} %slice.124), channel_id=1, source_target_pairs={{0,254},{1,255},{2,0},{3,1},{4,2},{5,3},{6,4},{7,5},{8,6},{9,7},{1... | collective-permute-start | bytes 884744 | tf_op jit(solution)/shard_map/ppermute | solution.py:23
  8.0 23.2 %collective-permute-start.2 = (bf16[48,3072]{1,0:T(8,128)(2,1)}, bf16[48,3072]{1,0:T(8,128)(2,1)S(1)}, u32[]{:S(2)}, u32[]{:S(2)}) collective-permute-start(bf16[48,3072]{1,0:T(8,128)(2,1)} %slice.124), channel_id=1, source_target_pairs={{0,2},{1,3},{2,4},{3,5},{4,6},{5,7},{6,8},{7,9},{8,10},{9,11},{10,... | collective-permute-start | bytes 884744 | tf_op jit(solution)/shard_map/ppermute | solution.py:23
  8.7 20.2 %collective-permute-start.3 = (bf16[32,3072]{1,0:T(8,128)(2,1)}, bf16[32,3072]{1,0:T(8,128)(2,1)}, u32[]{:S(2)}, u32[]{:S(2)}) collective-permute-start(bf16[32,3072]{1,0:T(8,128)(2,1)} %pad_maximum_fusion.3), channel_id=1, source_target_pairs={{0,2},{1,3},{2,4},{3,5},{4,6},{5,7},{6,8},{7,9},{8,10},{9,11},{10,... | collective-permute-start | bytes 589832 | tf_op jit(solution)/shard_map/ppermute | solution.py:23
  10.0 11.7 %collective-permute-start.1 = (bf16[32,3072]{1,0:T(8,128)(2,1)}, bf16[32,3072]{1,0:T(8,128)(2,1)}, u32[]{:S(2)}, u32[]{:S(2)}) collective-permute-start(bf16[32,3072]{1,0:T(8,128)(2,1)} %pad_maximum_fusion.3), channel_id=1, source_target_pairs={{0,254},{1,255},{2,0},{3,1},{4,2},{5,3},{6,4},{7,5},{8,6},{9,7},{1... | collective-permute-start | bytes 589832 | tf_op jit(solution)/shard_map/ppermute | solution.py:23
  17.5 1.2 %collective-permute-start.4 = (s32[80,16]{0,1:T(8,128)S(1)}, s32[80,16]{0,1:T(8,128)S(1)}, u32[]{:S(2)}, u32[]{:S(2)}) collective-permute-start(s32[80,16]{0,1:T(8,128)S(1)} %copy-done.4), channel_id=1, source_target_pairs={{0,1},{1,0},{2,3},{3,2},{4,5},{5,4},{6,7},{7,6},{8,9},{9,8},{10,11... | collective-permute-start | bytes 15368 | tf_op jit(solution)/shard_map/ppermute | solution.py:28
  18.7 1.2 %collective-permute-start.5 = (f32[80,16]{0,1:T(8,128)S(1)}, f32[80,16]{0,1:T(8,128)S(1)}, u32[]{:S(2)}, u32[]{:S(2)}) collective-permute-start(f32[80,16]{0,1:T(8,128)S(1)} %copy-done.5), channel_id=1, source_target_pairs={{0,1},{1,0},{2,3},{3,2},{4,5},{5,4},{6,7},{7,6},{8,9},{9,8},{10,11... | collective-permute-start | bytes 15368 | tf_op jit(solution)/shard_map/ppermute | solution.py:28
  20.1 10.1 %copy-start.3 = (bf16[80,9216]{1,0:T(8,128)(2,1)S(1)}, bf16[80,9216]{1,0:T(8,128)(2,1)}, u32[]{:S(2)}) copy-start(bf16[80,9216]{1,0:T(8,128)(2,1)} %get-tuple-element.6) | copy-start | bytes 4423684
  21.7 19.2 %collective-permute-start.8 = (bf16[32,3072]{1,0:T(8,128)(2,1)}, bf16[32,3072]{1,0:T(8,128)(2,1)S(1)}, u32[]{:S(2)}, u32[]{:S(2)}) collective-permute-start(bf16[32,3072]{1,0:T(8,128)(2,1)} %collective-permute-done.1), channel_id=1, source_target_pairs={{0,254},{1,255},{2,0},{3,1},{4,2},{5,3},{6,4},{7,5},{8,6},{9,7},{1... | collective-permute-start | bytes 589832 | tf_op jit(solution)/shard_map/ppermute | solution.py:23
  28.9 12.0 %collective-permute-start.10 = (bf16[32,3072]{1,0:T(8,128)(2,1)}, bf16[32,3072]{1,0:T(8,128)(2,1)S(1)}, u32[]{:S(2)}, u32[]{:S(2)}) collective-permute-start(bf16[32,3072]{1,0:T(8,128)(2,1)} %collective-permute-done.3), channel_id=1, source_target_pairs={{0,2},{1,3},{2,4},{3,5},{4,6},{5,7},{6,8},{7,9},{8,10},{9,11},{10,... | collective-permute-start | bytes 589832 | tf_op jit(solution)/shard_map/ppermute | solution.py:23
  32.1 25.4 %collective-permute-start.6 = (bf16[80,9216]{1,0:T(8,128)(2,1)S(1)}, bf16[80,9216]{1,0:T(8,128)(2,1)S(1)}, u32[]{:S(2)}, u32[]{:S(2)}) collective-permute-start(bf16[80,9216]{1,0:T(8,128)(2,1)S(1)} %maximum_dynamic-update-slice_fusion), channel_id=1, source_target_pairs={{0,1},{1,0},{2,3},{3,2},{4,5},{5,4},{6,7},{7,6},{8,9},{9,8},{10,11... | collective-permute-start | bytes 4423688 | tf_op jit(solution)/shard_map/ppermute | solution.py:28
  32.2 14.9 %collective-permute-start.7 = (bf16[48,3072]{1,0:T(8,128)(2,1)S(1)}, bf16[48,3072]{1,0:T(8,128)(2,1)S(1)}, u32[]{:S(2)}, u32[]{:S(2)}) collective-permute-start(bf16[48,3072]{1,0:T(8,128)(2,1)S(1)} %collective-permute-done), channel_id=1, source_target_pairs={{0,254},{1,255},{2,0},{3,1},{4,2},{5,3},{6,4},{7,5},{8,6},{9,7},{1... | collective-permute-start | bytes 884744 | tf_op jit(solution)/shard_map/ppermute | solution.py:23
  40.2 14.8 %collective-permute-start.9 = (bf16[48,3072]{1,0:T(8,128)(2,1)S(1)}, bf16[48,3072]{1,0:T(8,128)(2,1)S(1)}, u32[]{:S(2)}, u32[]{:S(2)}) collective-permute-start(bf16[48,3072]{1,0:T(8,128)(2,1)S(1)} %collective-permute-done.2), channel_id=1, source_target_pairs={{0,2},{1,3},{2,4},{3,5},{4,6},{5,7},{6,8},{7,9},{8,10},{9,11},{10,... | collective-permute-start | bytes 884744 | tf_op jit(solution)/shard_map/ppermute | solution.py:23
  55.1 2.1 %collective-permute-start.11 = (bf16[80,3072]{1,0:T(8,128)(2,1)S(1)}, bf16[80,3072]{1,0:T(8,128)(2,1)S(1)}, u32[]{:S(2)}, u32[]{:S(2)}) collective-permute-start(bf16[80,3072]{1,0:T(8,128)(2,1)S(1)} %pad_maximum_fusion.1), channel_id=1, source_target_pairs={{0,1},{1,0},{2,3},{3,2},{4,5},{5,4},{6,7},{7,6},{8,9},{9,8},{10,11... | collective-permute-start | bytes 1474568 | tf_op jit(solution)/shard_map/ppermute | solution.py:28
  59.2 2.2 %copy-start = (bf16[2048,1024]{1,0:T(8,128)(2,1)S(1)}, bf16[2048,1024]{1,0:T(8,128)(2,1)}, u32[]{:S(2)}) copy-start(bf16[2048,1024]{1,0:T(8,128)(2,1)} %param.12) | copy-start | bytes 12582916
  61.4 0.8 copy-start.1
  62.2 1.7 %collective-permute-start.12 = (f32[80,1024]{1,0:T(8,128)S(1)}, f32[80,1024]{1,0:T(8,128)S(1)}, u32[]{:S(2)}, u32[]{:S(2)}) collective-permute-start(f32[80,1024]{1,0:T(8,128)S(1)} %fusion.50), channel_id=1, source_target_pairs={{0,1},{1,0},{2,3},{3,2},{4,5},{5,4},{6,7},{7,6},{8,9},{9,8},{10,11... | collective-permute-start | bytes 983048 | tf_op jit(solution)/shard_map/ppermute | solution.py:28

commit v6 on v4

--- a/solution.py
+++ b/solution.py
@@ -66,26 +66,26 @@
     weights = jnp.concatenate([tile_weights, swap(tile_weights, count)], axis=0)
     ahead = shifted(both, -2, count)
     behind = shifted(both, 2, count)
+    neighbour = swap(both, count)
     ahead2 = shifted(ahead, -2, count)
     behind2 = shifted(behind, 2, count)
     total = jnp.dot(cols(HALF), both, preferred_element_type=jnp.float32)
     total = add(total, cols(HALF + 2), ahead)
     total = add(total, cols(HALF - 2), behind)
+    total = add(total, picked(HALF + 1, HALF - 1), neighbour)
     tile_ids = jnp.asarray(tile_order()[: TT * count // SIZES[-1]]) + TT * (
         lax.axis_index(SUB) % 2
     )
     onehot = (lists[None, :, :] == tile_ids[:, None, None]).astype(jnp.float32)
     tile_map = jnp.sum(onehot * weights[None, :, :], axis=2)
     total, tile_map = lax.optimization_barrier((total, tile_map))
-    width = both.shape[1]
-    swapped = swap(jnp.concatenate([both, ahead, behind], axis=1), count)
-    total = add(total, picked(HALF + 1, HALF - 1), swapped[:, :width])
-    total = add(total, picked(HALF + 3, HALF + 1), swapped[:, width : 2 * width])
-    total = add(total, picked(HALF - 1, HALF - 3), swapped[:, 2 * width :])
-    total = add(total, cols(HALF + 4), ahead2)
-    total = add(total, cols(HALF - 4), behind2)
+    swapped = swap(jnp.concatenate([ahead, behind], axis=0), count)
+    columns = [picked(HALF + 3, HALF + 1), picked(HALF - 1, HALF - 3)]
+    total = add(total, jnp.concatenate(columns, axis=1), swapped)
     last = swap(jnp.where(first, ahead2, behind2), count)
-    total = add(total, picked(HALF - 3, HALF + 3), last)
+    columns = [cols(HALF + 4), cols(HALF - 4), picked(HALF - 3, HALF + 3)]
+    stacked = jnp.concatenate([ahead2, behind2, last], axis=0)
+    total = add(total, jnp.concatenate(columns, axis=1), stacked)
     factor = 1.0 / jnp.sqrt(jnp.float32(WIN * C))
     total = total * factor
     q_real, q_imag, psum = (total[:, :F], total[:, F : 2 * F], total[:, 2 * F :])

time: 107 us -> 106 us (level)
  local copies, waits for them, and re-layouts: 4.24 us -> 1.76 us
  matrix products: 6.54 us -> 8.41 us
  blocking collectives: 49.5 us -> 48.1 us
  starting transfers between devices: 11.7 us -> 10.4 us
  waiting for transfers between devices: 25.7 us -> 26.9 us
    unnamed x3 -> x0, other arithmetic: 2.29 us -> none
    ppermute x4, waiting for transfers between devices: 23 us -> 25 us  [shifted(): return lax.ppermute(value, SUB, pairs)]
    dot_general x8 -> x5, matrix products: 2.55 us -> 4.36 us  [add(): return total + jnp.dot(columns, moving, preferred_element_type=jnp.float32)]
    unnamed x21 -> x18, local copies, waits for them, and re-layouts: 3.14 us -> 1.48 us
    slice x0 -> x1, other arithmetic: none -> 1.56 us  [cols(): return mask_bf[:, offset * C:(offset + 1) * C]]
    all_to_all x2, blocking collectives: 49.5 us -> 48.1 us  [body(): part = jnp.sum(lax.all_to_all(part, group, 0, 0, tiled=False), axis=0)]
    ppermute x4, starting transfers between devices: 10.9 us -> 9.46 us  [shifted(): return lax.ppermute(value, SUB, pairs)]
    ppermute x5 -> x6, waiting for transfers between devices: 2.67 us -> 1.92 us  [swap(): return lax.ppermute(value, SUB, pairs)]
  transfers between devices with their start and end apart: 9 -> 10, of which waited for: 6 -> 6; matrix products, arithmetic and copies ran while one was open for 5% -> 9% of each run, Pallas kernels for 0% -> 0%
where the time goes in v6:
time: 106 us; the launch traced here: 105 us
  blocking collectives  48.1 us (45%)
  waiting for transfers between devices  26.9 us (25%)
  starting transfers between devices  10.4 us (10%)
  other arithmetic  8.57 us (8%)
  matrix products  8.41 us (8%)
  local copies, waits for them, and re-layouts  1.76 us (2%)
    all_to_all x2, blocking collectives, body(): part = jnp.sum(lax.all_to_all(part, group, 0, 0, tiled=False), axis=0)  48.1 us
    ppermute x4, waiting for transfers between devices, shifted(): return lax.ppermute(value, SUB, pairs)  25 us
    ppermute x4, starting transfers between devices, shifted(): return lax.ppermute(value, SUB, pairs)  9.46 us
    dot_general x5, matrix products, add(): return total + jnp.dot(columns, moving, preferred_element_type=jnp.float32)  4.36 us
  transfers between devices with their start and end apart: 10, of which 6 were waited for; matrix products, arithmetic and copies ran while one was open for 9% of the time, Pallas kernels for 0%

profile of v6, /device:TPU:2, one launch (start us, length us, event | category | flops | bytes accessed | tf_op | source)
XLA Modules:
  0.0 105.0 jit_solution(4489698244275903137)
XLA Ops:
  0.6 0.0 copy-start.6
  0.6 0.0 copy-start.7
  0.7 0.0 copy-start.4
  0.7 1.1 %convert_element_type.12 = f32[80,2048]{1,0:T(8,128)S(1)} convert(bf16[80,2048]{1,0:T(8,128)(2,1)} %param.7) | non-fusion elementwise | flops 163840 | bytes 983040 | tf_op jit(solution)/shard_map/convert_element_type | solution.py:41
  1.7 0.0 copy-start.8
  1.7 1.0 convert_element_type.13
  2.8 0.1 add_convert_fusion.1
  2.9 0.0 copy-start.1
  2.9 0.0 copy-start.2
  2.9 0.9 pad_maximum_fusion.1
  3.8 0.0 collective-permute-start.2
  3.8 2.2 %collective-permute-start = (bf16[80,3072]{1,0:T(8,128)(2,1)}, bf16[80,3072]{1,0:T(8,128)(2,1)S(1)}, u32[]{:S(2)}, u32[]{:S(2)}) collective-permute-start(bf16[80,3072]{1,0:T(8,128)(2,1)} %pad_maximum_fusion.1), channel_id=1, source_target_pairs={{0,254},{1,255},{2,0},{3,1},{4,2},{5,3},{6,4},{7,5},{8,6},{9,7},{1... | collective-permute-start | bytes 1474568 | tf_op jit(solution)/shard_map/ppermute | solution.py:22
  6.1 0.0 collective-permute-start.1
  6.1 0.0 copy-done.6
  6.1 0.2 collective-permute-start.3
  6.3 0.0 copy-done.7
  6.3 0.3 collective-permute-start.4
  6.6 0.0 copy-done.1
  6.6 0.0 copy-done.2
  6.6 0.0 copy-done.4
  6.6 0.7 convert_element_type.14
  7.3 1.3 %fusion.29 = f32[3072,80]{0,1:T(8,128)S(1)} fusion(bf16[80,720]{1,0:T(8,128)(2,1)} %convert_element_type.14, bf16[80,1024]{1,0:T(8,128)(2,1)} %copy-done.2, bf16[80,1024]{1,0:T(8,128)(2,1)} %copy-done.1, bf16[80,1024]{1,0:T(8,128)(2,1)S(1)} %get-tuple-element.8), kind=kOutput, calls=%fused_computation.37 | convolution fusion | flops 40796160 | bytes 1495040 | tf_op jit(solution)/shard_map/dot_general | solution.py:72
  8.6 1.6 %fusion.39 = (bf16[80,80]{1,0:T(8,128)(2,1)S(1)}, bf16[80,80]{1,0:T(8,128)(2,1)S(1)}, bf16[80,80]{1,0:T(8,128)(2,1)S(1)}, bf16[80,80]{1,0:T(8,128)(2,1)S(1)}, bf16[80,80]{1,0:T(8,128)(2,1)}) fusion(bf16[80,720]{1,0:T(8,128)(2,1)} %convert_element_type.14, pred[]{:T(512)S(6)} %eq.19), kind=kLoop, calls=%fused_computation.53 | loop fusion | flops 19200 | bytes 140801 | tf_op jit(solution)/shard_map/slice | solution.py:57
  10.2 0.0 copy-done.8
  10.2 0.0 collective-permute-done.3
  10.2 0.1 pad_add_fusion
  10.2 0.1 copy.13
  10.3 0.0 collective-permute-done.4
  10.3 0.8 pad_maximum_fusion.3
  11.1 0.1 copy.14
  11.2 1.2 %select_reduce_fusion = f32[512,160]{0,1:T(8,128)S(1)} fusion(f32[160,16]{1,0:T(8,128)S(1)} %copy.14, s32[512]{0:T(512)S(1)} %broadcast_add_fusion, s32[160,16]{1,0:T(8,128)S(1)} %copy.13), kind=kLoop, calls=%fused_computation | loop fusion | flops 3850240 | bytes 350208 | tf_op jit(solution)/shard_map/reduce_sum | solution.py:80
  12.4 5.2 %collective-permute-done = bf16[80,3072]{1,0:T(8,128)(2,1)S(1)} collective-permute-done((bf16[80,3072]{1,0:T(8,128)(2,1)}, bf16[80,3072]{1,0:T(8,128)(2,1)S(1)}, u32[]{:S(2)}, u32[]{:S(2)}) %collective-permute-start) | collective-permute-done | bytes 491552 | tf_op jit(solution)/shard_map/ppermute | solution.py:22
  17.7 9.0 %collective-permute-done.1 = bf16[80,3072]{1,0:T(8,128)(2,1)S(1)} collective-permute-done((bf16[80,3072]{1,0:T(8,128)(2,1)}, bf16[80,3072]{1,0:T(8,128)(2,1)S(1)}, u32[]{:S(2)}, u32[]{:S(2)}) %collective-permute-start.1) | collective-permute-done | bytes 491552 | tf_op jit(solution)/shard_map/ppermute | solution.py:22
  26.7 0.1 pad_maximum_fusion
  26.8 0.1 collective-permute-start.5
  26.9 7.2 %collective-permute-start.6 = (bf16[80,3072]{1,0:T(8,128)(2,1)S(1)}, bf16[80,3072]{1,0:T(8,128)(2,1)S(1)}, u32[]{:S(2)}, u32[]{:S(2)}) collective-permute-start(bf16[80,3072]{1,0:T(8,128)(2,1)S(1)} %collective-permute-done), channel_id=1, source_target_pairs={{0,254},{1,255},{2,0},{3,1},{4,2},{5,3},{6,4},{7,5},{8,6},{9,7},{1... | collective-permute-start | bytes 1474568 | tf_op jit(solution)/shard_map/ppermute | solution.py:22
  34.1 0.0 collective-permute-start.7
  34.1 0.0 collective-permute-done.2
  34.1 1.4 %fusion.31 = f32[80,3072]{1,0:T(8,128)S(1)} fusion(bf16[80,3072]{1,0:T(8,128)(2,1)} %collective-permute-done.2, pred[]{:T(512)S(6)} %eq.19, bf16[80,720]{1,0:T(8,128)(2,1)} %convert_element_type.14), kind=kOutput, calls=%fused_computation.39 | convolution fusion | flops 39328000 | bytes 1515521 | tf_op jit(solution)/shard_map/dot_general | solution.py:63
  35.5 1.1 %convolution_add_fusion.1 = f32[3072,80]{0,1:T(8,128)S(1)} fusion(f32[3072,80]{0,1:T(8,128)S(1)} %fusion.29, bf16[80,3072]{1,0:T(8,128)(2,1)S(1)} %collective-permute-done, bf16[80,720]{1,0:T(8,128)(2,1)} %convert_element_type.14), kind=kOutput, calls=%fused_computation.2 | convolution fusion | flops 39567360 | bytes 2478080 | tf_op jit(solution)/shard_map/dot_general | solution.py:63
  36.6 8.6 %collective-permute-done.6 = bf16[80,3072]{1,0:T(8,128)(2,1)S(1)} collective-permute-done((bf16[80,3072]{1,0:T(8,128)(2,1)S(1)}, bf16[80,3072]{1,0:T(8,128)(2,1)S(1)}, u32[]{:S(2)}, u32[]{:S(2)}) %collective-permute-start.6) | collective-permute-done | bytes 491552 | tf_op jit(solution)/shard_map/ppermute | solution.py:22
  45.2 2.2 %collective-permute-done.7 = bf16[80,3072]{1,0:T(8,128)(2,1)S(1)} collective-permute-done((bf16[80,3072]{1,0:T(8,128)(2,1)S(1)}, bf16[80,3072]{1,0:T(8,128)(2,1)S(1)}, u32[]{:S(2)}, u32[]{:S(2)}) %collective-permute-start.7) | collective-permute-done | bytes 491552 | tf_op jit(solution)/shard_map/ppermute | solution.py:22
  47.4 0.1 broadcast_select_fusion
  47.4 0.0 copy-start.5
  47.4 0.1 collective-permute-start.8
  47.5 1.1 %fusion.1 = f32[80,3072]{1,0:T(8,128)S(1)} fusion(f32[80,3072]{1,0:T(8,128)S(1)} %fusion.31, f32[3072,80]{0,1:T(8,128)S(1)} %convolution_add_fusion.1, bf16[80,3072]{1,0:T(8,128)(2,1)S(1)} %collective-permute-done.1, bf16[80,720]{1,0:T(8,128)(2,1)} %convert_element_type.14), kind=kOutput, calls=%fused_computation.4 | convolution fusion | flops 39813120 | bytes 3461120 | tf_op jit(solution)/shard_map/dot_general | solution.py:63
  48.6 0.0 collective-permute-done.5
  48.6 0.3 fusion.18
  49.0 0.4 collective-permute-done.8
  49.4 0.0 copy-done.5
  49.4 0.0 copy-start
  49.4 0.5 fusion.10
  49.8 0.2 subtract_convert_fusion.1
  50.1 1.4 %copy-done = bf16[2048,1024]{1,0:T(8,128)(2,1)S(1)} copy-done((bf16[2048,1024]{1,0:T(8,128)(2,1)S(1)}, bf16[2048,1024]{1,0:T(8,128)(2,1)}, u32[]{:S(2)}) %copy-start) | copy-done | bytes 4194328
  51.6 0.9 fusion.40
  52.4 0.2 collective-permute-start.9
  52.7 1.5 %collective-permute-done.9 = f32[80,1024]{1,0:T(8,128)S(1)} collective-permute-done((f32[80,1024]{1,0:T(8,128)S(1)}, f32[80,1024]{1,0:T(8,128)S(1)}, u32[]{:S(2)}, u32[]{:S(2)}) %collective-permute-start.9) | collective-permute-done | bytes 327712 | tf_op jit(solution)/shard_map/ppermute | solution.py:27
  54.2 1.9 %fusion.14 = f32[512,1024]{1,0:T(8,128)S(1)} fusion(f32[512,160]{0,1:T(8,128)S(1)} %select_reduce_fusion, f32[80,1024]{1,0:T(8,128)S(1)} %collective-permute-done.9, f32[80,1024]{1,0:T(8,128)S(1)} %fusion.40), kind=kOutput, calls=%fused_computation.14 | convolution fusion | flops 1006796800 | bytes 3080192 | tf_op jit(solution)/shard_map/dot_general | solution.py:97
  56.0 0.0 copy-done.3
  56.0 33.8 %all_to_all.10 = f32[8,64,1024]{2,1,0:T(8,128)S(1)} all-to-all(f32[8,64,1024]{2,1,0:T(8,128)S(1)} %bitcast.12), channel_id=1, replica_groups=mesh['y'=4,'z'=4,'x'=8,'c'=2] {'x'}, dimensions={0} | all-to-all | bytes 4194304 | tf_op jit(solution)/shard_map/all_to_all | solution.py:101
  89.8 0.1 reduce_sum.28
  90.0 0.1 reshape.14
  90.1 14.3 %all_to_all.11 = f32[16,4,1024]{2,1,0:T(4,128)S(1)} all-to-all(f32[16,4,1024]{2,1,0:T(4,128)S(1)} %reshape.14), channel_id=1, replica_groups=mesh['y'=4,'z'=4,'x'=8,'c'=2] {'z','y'}, dimensions={0} | all-to-all | bytes 524288 | tf_op jit(solution)/shard_map/all_to_all | solution.py:101
  104.3 0.7 reduce_sum.29
  (3 shorter events, 0.0 us)
Async XLA Ops:
  0.6 5.4 %copy-start.6 = (s32[80,16]{0,1:T(8,128)S(1)}, s32[80,16]{0,1:T(8,128)}, u32[]{:S(2)}) copy-start(s32[80,16]{0,1:T(8,128)} %param.10) | copy-start | bytes 15364
  0.6 5.7 %copy-start.7 = (f32[80,16]{0,1:T(8,128)S(1)}, f32[80,16]{0,1:T(8,128)}, u32[]{:S(2)}) copy-start(f32[80,16]{0,1:T(8,128)} %param.11) | copy-start | bytes 15364
  0.7 5.9 %copy-start.4 = (s32[80,720]{1,0:T(8,128)S(1)}, s32[80,720]{1,0:T(8,128)}, u32[]{:S(2)}) copy-start(s32[80,720]{1,0:T(8,128)} %param.9) | copy-start | bytes 691204
  1.7 8.4 %copy-start.8 = (s32[512]{0:T(512)S(1)}, s32[512]{0:T(512)}, u32[]{:S(2)}) copy-start(s32[512]{0:T(512)} %constant.47.clone) | copy-start | bytes 6148
  2.9 3.7 %copy-start.1 = (bf16[80,1024]{1,0:T(8,128)(2,1)}, bf16[80,1024]{1,0:T(8,128)(2,1)S(1)}, u32[]{:S(2)}) copy-start(bf16[80,1024]{1,0:T(8,128)(2,1)S(1)} %get-tuple-element.9) | copy-start | bytes 491524
  2.9 3.6 %copy-start.2 = (bf16[80,1024]{1,0:T(8,128)(2,1)}, bf16[80,1024]{1,0:T(8,128)(2,1)S(1)}, u32[]{:S(2)}) copy-start(bf16[80,1024]{1,0:T(8,128)(2,1)S(1)} %get-tuple-element.10) | copy-start | bytes 491524
  3.8 30.3 %collective-permute-start.2 = (bf16[80,3072]{1,0:T(8,128)(2,1)}, bf16[80,3072]{1,0:T(8,128)(2,1)}, u32[]{:S(2)}, u32[]{:S(2)}) collective-permute-start(bf16[80,3072]{1,0:T(8,128)(2,1)} %pad_maximum_fusion.1), channel_id=1, source_target_pairs={{0,1},{1,0},{2,3},{3,2},{4,5},{5,4},{6,7},{7,6},{8,9},{9,8},{10,11... | collective-permute-start | bytes 1474568 | tf_op jit(solution)/shard_map/ppermute | solution.py:27
  3.8 13.8 %collective-permute-start = (bf16[80,3072]{1,0:T(8,128)(2,1)}, bf16[80,3072]{1,0:T(8,128)(2,1)S(1)}, u32[]{:S(2)}, u32[]{:S(2)}) collective-permute-start(bf16[80,3072]{1,0:T(8,128)(2,1)} %pad_maximum_fusion.1), channel_id=1, source_target_pairs={{0,254},{1,255},{2,0},{3,1},{4,2},{5,3},{6,4},{7,5},{8,6},{9,7},{1... | collective-permute-start | bytes 1474568 | tf_op jit(solution)/shard_map/ppermute | solution.py:22
  6.1 20.6 %collective-permute-start.1 = (bf16[80,3072]{1,0:T(8,128)(2,1)}, bf16[80,3072]{1,0:T(8,128)(2,1)S(1)}, u32[]{:S(2)}, u32[]{:S(2)}) collective-permute-start(bf16[80,3072]{1,0:T(8,128)(2,1)} %pad_maximum_fusion.1), channel_id=1, source_target_pairs={{0,2},{1,3},{2,4},{3,5},{4,6},{5,7},{6,8},{7,9},{8,10},{9,11},{10,... | collective-permute-start | bytes 1474568 | tf_op jit(solution)/shard_map/ppermute | solution.py:22
  6.1 4.1 %collective-permute-start.3 = (s32[80,16]{0,1:T(8,128)S(1)}, s32[80,16]{0,1:T(8,128)S(1)}, u32[]{:S(2)}, u32[]{:S(2)}) collective-permute-start(s32[80,16]{0,1:T(8,128)S(1)} %copy-done.6), channel_id=1, source_target_pairs={{0,1},{1,0},{2,3},{3,2},{4,5},{5,4},{6,7},{7,6},{8,9},{9,8},{10,11... | collective-permute-start | bytes 15368 | tf_op jit(solution)/shard_map/ppermute | solution.py:27
  6.3 4.0 %collective-permute-start.4 = (f32[80,16]{0,1:T(8,128)S(1)}, f32[80,16]{0,1:T(8,128)}, u32[]{:S(2)}, u32[]{:S(2)}) collective-permute-start(f32[80,16]{0,1:T(8,128)S(1)} %copy-done.7), channel_id=1, source_target_pairs={{0,1},{1,0},{2,3},{3,2},{4,5},{5,4},{6,7},{7,6},{8,9},{9,8},{10,11... | collective-permute-start | bytes 15368 | tf_op jit(solution)/shard_map/ppermute | solution.py:27
  26.8 21.8 %collective-permute-start.5 = (bf16[160,3072]{1,0:T(8,128)(2,1)S(1)}, bf16[160,3072]{1,0:T(8,128)(2,1)S(1)}, u32[]{:S(2)}, u32[]{:S(2)}) collective-permute-start(bf16[160,3072]{1,0:T(8,128)(2,1)S(1)} %pad_maximum_fusion), channel_id=1, source_target_pairs={{0,1},{1,0},{2,3},{3,2},{4,5},{5,4},{6,7},{7,6},{8,9},{9,8},{10,11... | collective-permute-start | bytes 2949128 | tf_op jit(solution)/shard_map/ppermute | solution.py:27
  26.9 18.3 %collective-permute-start.6 = (bf16[80,3072]{1,0:T(8,128)(2,1)S(1)}, bf16[80,3072]{1,0:T(8,128)(2,1)S(1)}, u32[]{:S(2)}, u32[]{:S(2)}) collective-permute-start(bf16[80,3072]{1,0:T(8,128)(2,1)S(1)} %collective-permute-done), channel_id=1, source_target_pairs={{0,254},{1,255},{2,0},{3,1},{4,2},{5,3},{6,4},{7,5},{8,6},{9,7},{1... | collective-permute-start | bytes 1474568 | tf_op jit(solution)/shard_map/ppermute | solution.py:22
  34.1 13.3 %collective-permute-start.7 = (bf16[80,3072]{1,0:T(8,128)(2,1)S(1)}, bf16[80,3072]{1,0:T(8,128)(2,1)S(1)}, u32[]{:S(2)}, u32[]{:S(2)}) collective-permute-start(bf16[80,3072]{1,0:T(8,128)(2,1)S(1)} %collective-permute-done.1), channel_id=1, source_target_pairs={{0,2},{1,3},{2,4},{3,5},{4,6},{5,7},{6,8},{7,9},{8,10},{9,11},{10,... | collective-permute-start | bytes 1474568 | tf_op jit(solution)/shard_map/ppermute | solution.py:22
  47.4 2.0 %copy-start.5 = (bf16[80,80]{1,0:T(8,128)(2,1)S(1)}, bf16[80,80]{1,0:T(8,128)(2,1)}, u32[]{:S(2)}) copy-start(bf16[80,80]{1,0:T(8,128)(2,1)} %get-tuple-element.15) | copy-start | bytes 38404
  47.4 2.0 %collective-permute-start.8 = (bf16[80,3072]{1,0:T(8,128)(2,1)S(1)}, bf16[80,3072]{1,0:T(8,128)(2,1)S(1)}, u32[]{:S(2)}, u32[]{:S(2)}) collective-permute-start(bf16[80,3072]{1,0:T(8,128)(2,1)S(1)} %broadcast_select_fusion), channel_id=1, source_target_pairs={{0,1},{1,0},{2,3},{3,2},{4,5},{5,4},{6,7},{7,6},{8,9},{9,8},{10,11... | collective-permute-start | bytes 1474568 | tf_op jit(solution)/shard_map/ppermute | solution.py:27
  49.4 2.2 %copy-start = (bf16[2048,1024]{1,0:T(8,128)(2,1)S(1)}, bf16[2048,1024]{1,0:T(8,128)(2,1)}, u32[]{:S(2)}) copy-start(bf16[2048,1024]{1,0:T(8,128)(2,1)} %param.12) | copy-start | bytes 12582916
  51.6 4.4 %copy-start.3 = (bf16[80,2048]{1,0:T(8,128)(2,1)}, bf16[80,2048]{1,0:T(8,128)(2,1)S(1)}, u32[]{:S(2)}) copy-start(bf16[80,2048]{1,0:T(8,128)(2,1)S(1)} %pad_maximum_fusion.2) | copy-start | bytes 983044
  52.4 1.7 %collective-permute-start.9 = (f32[80,1024]{1,0:T(8,128)S(1)}, f32[80,1024]{1,0:T(8,128)S(1)}, u32[]{:S(2)}, u32[]{:S(2)}) collective-permute-start(f32[80,1024]{1,0:T(8,128)S(1)} %fusion.40), channel_id=1, source_target_pairs={{0,1},{1,0},{2,3},{3,2},{4,5},{5,4},{6,7},{7,6},{8,9},{9,8},{10,11... | collective-permute-start | bytes 983048 | tf_op jit(solution)/shard_map/ppermute | solution.py:27

commit v7 on v6

--- a/solution.py
+++ b/solution.py
@@ -27,6 +27,12 @@
     return lax.ppermute(value, SUB, pairs)
 
 
+def swap_cores(value, core):
+    sent = jnp.broadcast_to(value[None], (SIZES[-1],) + value.shape)
+    got = lax.all_to_all(sent, SUB[-1], 0, 0, tiled=False)
+    return lax.dynamic_index_in_dim(got, 1 - core, 0, keepdims=False)
+
+
 def tile_order():
     y, z, x, c, i = np.meshgrid(
         *[np.arange(n) for n in SIZES], np.arange(TT), indexing="ij"
@@ -51,7 +57,8 @@
         axis=1,
     ).astype(jnp.bfloat16)
     mask_bf = pair_mask.astype(jnp.bfloat16)
-    first = lax.axis_index(SUB) % 2 == 0
+    core = lax.axis_index(SUB) % 2
+    first = core == 0
 
     def cols(offset):
         return mask_bf[:, offset * C : (offset + 1) * C]
@@ -66,23 +73,21 @@
     weights = jnp.concatenate([tile_weights, swap(tile_weights, count)], axis=0)
     ahead = shifted(both, -2, count)
     behind = shifted(both, 2, count)
-    neighbour = swap(both, count)
     ahead2 = shifted(ahead, -2, count)
     behind2 = shifted(behind, 2, count)
     total = jnp.dot(cols(HALF), both, preferred_element_type=jnp.float32)
     total = add(total, cols(HALF + 2), ahead)
     total = add(total, cols(HALF - 2), behind)
-    total = add(total, picked(HALF + 1, HALF - 1), neighbour)
     tile_ids = jnp.asarray(tile_order()[: TT * count // SIZES[-1]]) + TT * (
         lax.axis_index(SUB) % 2
     )
     onehot = (lists[None, :, :] == tile_ids[:, None, None]).astype(jnp.float32)
     tile_map = jnp.sum(onehot * weights[None, :, :], axis=2)
     total, tile_map = lax.optimization_barrier((total, tile_map))
-    swapped = swap(jnp.concatenate([ahead, behind], axis=0), count)
-    columns = [picked(HALF + 3, HALF + 1), picked(HALF - 1, HALF - 3)]
+    swapped = swap_cores(jnp.concatenate([both, ahead, behind], axis=0), core)
+    columns = [picked(HALF + 1, HALF - 1), picked(HALF + 3, HALF + 1), picked(HALF - 1, HALF - 3)]
     total = add(total, jnp.concatenate(columns, axis=1), swapped)
-    last = swap(jnp.where(first, ahead2, behind2), count)
+    last = swap_cores(jnp.where(first, ahead2, behind2), core)
     columns = [cols(HALF + 4), cols(HALF - 4), picked(HALF - 3, HALF + 3)]
     stacked = jnp.concatenate([ahead2, behind2, last], axis=0)
     total = add(total, jnp.concatenate(columns, axis=1), stacked)
@@ -93,7 +98,7 @@
     adj_imag = rec_real * q_imag + rec_imag * q_real - green_imag * psum
     adjoint = jnp.concatenate([adj_real, adj_imag], axis=1).astype(jnp.bfloat16)
     response = jnp.dot(adjoint, tile_green, preferred_element_type=jnp.float32)
-    responses = jnp.concatenate([response, swap(response, count)], axis=0)
+    responses = jnp.concatenate([response, swap_cores(response, core)], axis=0)
     part = jnp.dot(tile_map, responses, precision=lax.Precision.HIGHEST)
     for group in STAGES:
         ways = int(np.prod([SIZES[SUB.index(a)] for a in group]))

time: 106 us -> 119 us (1.12)
  blocking collectives: 48.1 us -> 56.9 us
  starting transfers between devices: 10.4 us -> 14 us
  waiting for transfers between devices: 26.9 us -> 24.1 us
  local copies, waits for them, and re-layouts: 1.76 us -> 3.96 us
  matrix products: 8.41 us -> 10.1 us
    all_to_all x0 -> x2, blocking collectives: none -> 8.78 us  [swap_cores(): got = lax.all_to_all(sent, SUB[-1], 0, 0, tiled=False)]
    all_to_all x0 -> x1, starting transfers between devices: none -> 3.91 us  [swap_cores(): got = lax.all_to_all(sent, SUB[-1], 0, 0, tiled=False)]
    broadcast_in_dim x0 -> x3, local copies, waits for them, and re-layouts: none -> 2.13 us  [swap_cores(): sent = jnp.broadcast_to(value[None], (SIZES[-1],) + value.shape)]
    ppermute x6 -> x2, waiting for transfers between devices: 1.92 us -> 0.01 us  [swap(): return lax.ppermute(value, SUB, pairs)]
    dot_general x5 -> x4, matrix products: 4.36 us -> 6.13 us  [add(): return total + jnp.dot(columns, moving, preferred_element_type=jnp.float32)]
  transfers between devices with their start and end apart: 10 -> 7, of which waited for: 6 -> 4; matrix products, arithmetic and copies ran while one was open for 9% -> 7% of each run, Pallas kernels for 0% -> 0%
where the time goes in v7:
time: 119 us; the launch traced here: 117 us
  blocking collectives  56.9 us (48%)
  waiting for transfers between devices  24.1 us (20%)
  starting transfers between devices  14 us (12%)
  matrix products  10.1 us (8%)
  other arithmetic  7.53 us (6%)
  local copies, waits for them, and re-layouts  3.96 us (3%)
    all_to_all x2, blocking collectives, body(): part = jnp.sum(lax.all_to_all(part, group, 0, 0, tiled=False), axis=0)  48.1 us
    ppermute x4, waiting for transfers between devices, shifted(): return lax.ppermute(value, SUB, pairs)  24.1 us
    ppermute x4, starting transfers between devices, shifted(): return lax.ppermute(value, SUB, pairs)  9.57 us
    all_to_all x2, blocking collectives, swap_cores(): got = lax.all_to_all(sent, SUB[-1], 0, 0, tiled=False)  8.78 us
    dot_general x4, matrix products, add(): return total + jnp.dot(columns, moving, preferred_element_type=jnp.float32)  6.13 us
    all_to_all x1, starting transfers between devices, swap_cores(): got = lax.all_to_all(sent, SUB[-1], 0, 0, tiled=False)  3.91 us
  transfers between devices with their start and end apart: 7, of which 4 were waited for; matrix products, arithmetic and copies ran while one was open for 7% of the time, Pallas kernels for 0%

profile of v7, /device:TPU:2, one launch (start us, length us, event | category | flops | bytes accessed | tf_op | source)
XLA Modules:
  0.0 117.5 jit_solution(12216853436603122172)
XLA Ops:
  0.6 0.0 copy-start.12
  0.6 0.0 copy-start.13
  0.7 0.0 copy-start.10
  0.7 1.1 convert_element_type.12
  1.7 0.0 copy-start
  1.7 0.0 copy-start.14
  1.8 1.3 %convert_element_type.13 = f32[80,2048]{1,0:T(8,128)S(1)} convert(bf16[80,2048]{1,0:T(8,128)(2,1)} %param.8) | non-fusion elementwise | flops 163840 | bytes 983040 | tf_op jit(solution)/shard_map/convert_element_type | solution.py:48
  3.0 0.0 copy-done
  3.0 0.0 copy-start.2
  3.0 0.1 add_convert_fusion.1
  3.2 0.7 copy-done.2
  3.9 2.3 %collective-permute-start = (bf16[80,3072]{1,0:T(8,128)(2,1)S(1)}, bf16[80,3072]{1,0:T(8,128)(2,1)S(1)}, u32[]{:S(2)}, u32[]{:S(2)}) collective-permute-start(bf16[80,3072]{1,0:T(8,128)(2,1)S(1)} %pad_maximum_fusion.1), channel_id=1, source_target_pairs={{0,254},{1,255},{2,0},{3,1},{4,2},{5,3},{6,4},{7,5},{8,6},{9,7},{1... | collective-permute-start | bytes 1474568 | tf_op jit(solution)/shard_map/ppermute | solution.py:22
  6.2 0.0 collective-permute-start.1
  6.2 0.0 copy-done.12
  6.2 0.0 collective-permute-start.2
  6.3 0.0 copy-done.13
  6.3 0.5 collective-permute-start.3
  6.8 0.0 copy-done.10
  6.8 0.0 copy-start.9
  6.8 1.3 %fusion.26 = f32[3072,80]{0,1:T(8,128)} fusion(bf16[80,720]{1,0:T(8,128)(2,1)S(1)} %convert_element_type.14, bf16[80,1024]{1,0:T(8,128)(2,1)S(1)} %get-tuple-element.10, bf16[80,1024]{1,0:T(8,128)(2,1)S(1)} %get-tuple-element.9, bf16[80,1024]{1,0:T(8,128)(2,1)S(1)} %get-tuple-element.8), kind=kOutput, calls=%fused_computation.41 | convolution fusion | flops 40796160 | bytes 1495040 | tf_op jit(solution)/shard_map/dot_general | solution.py:78
  8.1 0.0 copy-done.9
  8.1 0.7 fusion.32
  8.8 0.0 copy-done.14
  8.8 0.0 collective-permute-done.2
  8.8 0.1 pad_add_fusion
  8.9 0.1 copy.13
  9.0 0.0 collective-permute-done.3
  9.0 0.1 pad_maximum_fusion.3
  9.0 0.1 copy.14
  9.2 1.9 %select_reduce_fusion = f32[512,160]{0,1:T(8,128)} fusion(f32[160,16]{1,0:T(8,128)S(1)} %copy.14, s32[512]{0:T(512)S(1)} %broadcast_add_fusion, s32[160,16]{1,0:T(8,128)S(1)} %copy.13), kind=kLoop, calls=%fused_computation | loop fusion | flops 3850240 | bytes 350208 | tf_op jit(solution)/shard_map/reduce_sum | solution.py:85
  11.1 5.9 %collective-permute-done = bf16[80,3072]{1,0:T(8,128)(2,1)S(1)} collective-permute-done((bf16[80,3072]{1,0:T(8,128)(2,1)S(1)}, bf16[80,3072]{1,0:T(8,128)(2,1)S(1)}, u32[]{:S(2)}, u32[]{:S(2)}) %collective-permute-start) | collective-permute-done | bytes 491552 | tf_op jit(solution)/shard_map/ppermute | solution.py:22
  17.0 9.0 %collective-permute-done.1 = bf16[80,3072]{1,0:T(8,128)(2,1)S(1)} collective-permute-done((bf16[80,3072]{1,0:T(8,128)(2,1)S(1)}, bf16[80,3072]{1,0:T(8,128)(2,1)S(1)}, u32[]{:S(2)}, u32[]{:S(2)}) %collective-permute-start.1) | collective-permute-done | bytes 491552 | tf_op jit(solution)/shard_map/ppermute | solution.py:22
  26.0 0.1 pad_maximum_fusion
  26.1 2.0 %broadcast_in_dim.6 = bf16[2,240,3072]{2,1,0:T(8,128)(2,1)} broadcast(bf16[240,3072]{1,0:T(8,128)(2,1)S(1)} %pad_maximum_fusion), dimensions={1,2} | broadcast | bytes 4423680 | tf_op jit(solution)/shard_map/broadcast_in_dim | solution.py:31
  28.0 0.0 copy-done.5
  28.0 3.9 %all-to-all-start = ((bf16[2,240,3072]{2,1,0:T(8,128)(2,1)}), bf16[2,240,3072]{2,1,0:T(8,128)(2,1)S(1)}, u32[]{:S(2)}, u32[]{:S(2)}) async-start(bf16[2,240,3072]{2,1,0:T(8,128)(2,1)} %broadcast_in_dim.6), calls=%async_computation | async-start | bytes 5898240 | tf_op jit(solution)/shard_map/all_to_all | solution.py:32
  32.0 7.2 %collective-permute-start.4 = (bf16[80,3072]{1,0:T(8,128)(2,1)S(1)}, bf16[80,3072]{1,0:T(8,128)(2,1)}, u32[]{:S(2)}, u32[]{:S(2)}) collective-permute-start(bf16[80,3072]{1,0:T(8,128)(2,1)S(1)} %collective-permute-done), channel_id=1, source_target_pairs={{0,254},{1,255},{2,0},{3,1},{4,2},{5,3},{6,4},{7,5},{8,6},{9,7},{1... | collective-permute-start | bytes 1474568 | tf_op jit(solution)/shard_map/ppermute | solution.py:22
  39.2 0.0 collective-permute-start.5
  39.2 1.6 %convolution_add_fusion.1 = f32[3072,80]{0,1:T(8,128)S(1)} fusion(f32[3072,80]{0,1:T(8,128)} %fusion.26, bf16[80,3072]{1,0:T(8,128)(2,1)S(1)} %collective-permute-done, bf16[80,720]{1,0:T(8,128)(2,1)} %copy-done.9), kind=kOutput, calls=%fused_computation.2 | convolution fusion | flops 39567360 | bytes 2478080 | tf_op jit(solution)/shard_map/dot_general | solution.py:70
  40.8 2.3 %fusion = f32[80,3072]{1,0:T(8,128)} fusion(f32[3072,80]{0,1:T(8,128)S(1)} %convolution_add_fusion.1, bf16[80,3072]{1,0:T(8,128)(2,1)} %copy-done.5, bf16[80,720]{1,0:T(8,128)(2,1)} %copy-done.9), kind=kOutput, calls=%fused_computation.3 | convolution fusion | flops 39567360 | bytes 2478080 | tf_op jit(solution)/shard_map/dot_general | solution.py:70
  43.1 0.0 all-to-all-done
  43.1 0.4 fusion.7
  43.6 0.0 copy-start.11
  43.6 6.7 %collective-permute-done.4 = bf16[80,3072]{1,0:T(8,128)(2,1)} collective-permute-done((bf16[80,3072]{1,0:T(8,128)(2,1)S(1)}, bf16[80,3072]{1,0:T(8,128)(2,1)}, u32[]{:S(2)}, u32[]{:S(2)}) %collective-permute-start.4) | collective-permute-done | bytes 491552 | tf_op jit(solution)/shard_map/ppermute | solution.py:22
  50.3 2.5 %collective-permute-done.5 = bf16[80,3072]{1,0:T(8,128)(2,1)} collective-permute-done((bf16[80,3072]{1,0:T(8,128)(2,1)}, bf16[80,3072]{1,0:T(8,128)(2,1)}, u32[]{:S(2)}, u32[]{:S(2)}) %collective-permute-start.5) | collective-permute-done | bytes 491552 | tf_op jit(solution)/shard_map/ppermute | solution.py:22
  52.8 1.1 broadcast_select_fusion
  53.9 0.1 broadcast_in_dim.7
  54.0 4.5 %all_to_all.25 = bf16[2,80,3072]{2,1,0:T(8,128)(2,1)S(1)} all-to-all(bf16[2,80,3072]{2,1,0:T(8,128)(2,1)S(1)} %broadcast_in_dim.7), channel_id=1, replica_groups=mesh['y'=4,'z'=4,'x'=8,'c'=2] {'c'}, dimensions={0} | all-to-all | bytes 1966080 | tf_op jit(solution)/shard_map/all_to_all | solution.py:32
  58.5 0.0 copy-done.8
  58.6 0.0 copy-start.4
  58.6 1.8 %fusion.1 = f32[80,3072]{1,0:T(8,128)S(1)} fusion(bf16[80,3072]{1,0:T(8,128)(2,1)S(1)} %dynamic-slice_bitcast_fusion, bf16[80,3072]{1,0:T(8,128)(2,1)} %collective-permute-done.5, bf16[80,3072]{1,0:T(8,128)(2,1)} %collective-permute-done.4, f32[80,3072]{1,0:T(8,128)S(1)} %copy-done.8, f32[80,3072]{1,0:T(8,128)S(1)} %fusion.7, ...), kind=kOutput, calls=%fused_computation.5 | convolution fusion | flops 123240960 | bytes 4462080 | tf_op jit(solution)/shard_map/dot_general | solution.py:70
  60.4 0.0 copy-done.3
  60.4 0.2 subtract_convert_fusion.1
  60.7 0.7 copy-done.4
  61.4 0.9 fusion.33
  62.3 0.1 broadcast_in_dim.8
  62.4 4.3 %all_to_all.26 = f32[2,80,1024]{2,1,0:T(8,128)S(1)} all-to-all(f32[2,80,1024]{2,1,0:T(8,128)S(1)} %broadcast_in_dim.8), channel_id=1, replica_groups=mesh['y'=4,'z'=4,'x'=8,'c'=2] {'c'}, dimensions={0} | all-to-all | bytes 1310720 | tf_op jit(solution)/shard_map/all_to_all | solution.py:32
  66.6 0.0 copy-done.6
  66.7 1.8 %fusion.10 = f32[512,1024]{1,0:T(8,128)S(1)} fusion(f32[512,160]{0,1:T(8,128)S(1)} %copy-done.7, f32[80,1024]{1,0:T(8,128)S(1)} %dynamic-slice_bitcast_fusion.1, f32[80,1024]{1,0:T(8,128)S(1)} %fusion.33), kind=kOutput, calls=%fused_computation.15 | convolution fusion | flops 1006796800 | bytes 3080192 | tf_op jit(solution)/shard_map/dot_general | solution.py:102
  68.5 33.8 %all_to_all.27 = f32[8,64,1024]{2,1,0:T(8,128)S(1)} all-to-all(f32[8,64,1024]{2,1,0:T(8,128)S(1)} %bitcast.15), channel_id=1, replica_groups=mesh['y'=4,'z'=4,'x'=8,'c'=2] {'x'}, dimensions={0} | all-to-all | bytes 4194304 | tf_op jit(solution)/shard_map/all_to_all | solution.py:106
  102.3 0.1 reduce_sum.28
  102.5 0.1 reshape.17
  102.5 14.3 %all_to_all.28 = f32[16,4,1024]{2,1,0:T(4,128)S(1)} all-to-all(f32[16,4,1024]{2,1,0:T(4,128)S(1)} %reshape.17), channel_id=1, replica_groups=mesh['y'=4,'z'=4,'x'=8,'c'=2] {'z','y'}, dimensions={0} | all-to-all | bytes 524288 | tf_op jit(solution)/shard_map/all_to_all | solution.py:106
  116.8 0.7 reduce_sum.29
  (15 shorter events, 0.1 us)
Async XLA Ops:
  0.6 5.6 %copy-start.12 = (s32[80,16]{0,1:T(8,128)S(1)}, s32[80,16]{0,1:T(8,128)}, u32[]{:S(2)}) copy-start(s32[80,16]{0,1:T(8,128)} %param.10) | copy-start | bytes 15364
  0.6 5.6 %copy-start.13 = (f32[80,16]{0,1:T(8,128)S(1)}, f32[80,16]{0,1:T(8,128)}, u32[]{:S(2)}) copy-start(f32[80,16]{0,1:T(8,128)} %param.11) | copy-start | bytes 15364
  0.7 6.1 %copy-start.10 = (s32[80,720]{1,0:T(8,128)S(1)}, s32[80,720]{1,0:T(8,128)}, u32[]{:S(2)}) copy-start(s32[80,720]{1,0:T(8,128)} %param.9) | copy-start | bytes 691204
  1.7 1.3 %copy-start = (f32[80,2048]{1,0:T(8,128)}, f32[80,2048]{1,0:T(8,128)S(1)}, u32[]{:S(2)}) copy-start(f32[80,2048]{1,0:T(8,128)S(1)} %convert_element_type.12) | copy-start | bytes 1966084
  1.7 7.0 %copy-start.14 = (s32[512]{0:T(512)S(1)}, s32[512]{0:T(512)}, u32[]{:S(2)}) copy-start(s32[512]{0:T(512)} %constant.62.clone) | copy-start | bytes 6148
  3.0 0.9 copy-start.2
  3.9 13.0 %collective-permute-start = (bf16[80,3072]{1,0:T(8,128)(2,1)S(1)}, bf16[80,3072]{1,0:T(8,128)(2,1)S(1)}, u32[]{:S(2)}, u32[]{:S(2)}) collective-permute-start(bf16[80,3072]{1,0:T(8,128)(2,1)S(1)} %pad_maximum_fusion.1), channel_id=1, source_target_pairs={{0,254},{1,255},{2,0},{3,1},{4,2},{5,3},{6,4},{7,5},{8,6},{9,7},{1... | collective-permute-start | bytes 1474568 | tf_op jit(solution)/shard_map/ppermute | solution.py:22
  6.2 19.7 %collective-permute-start.1 = (bf16[80,3072]{1,0:T(8,128)(2,1)S(1)}, bf16[80,3072]{1,0:T(8,128)(2,1)S(1)}, u32[]{:S(2)}, u32[]{:S(2)}) collective-permute-start(bf16[80,3072]{1,0:T(8,128)(2,1)S(1)} %pad_maximum_fusion.1), channel_id=1, source_target_pairs={{0,2},{1,3},{2,4},{3,5},{4,6},{5,7},{6,8},{7,9},{8,10},{9,11},{10,... | collective-permute-start | bytes 1474568 | tf_op jit(solution)/shard_map/ppermute | solution.py:22
  6.2 2.5 %collective-permute-start.2 = (s32[80,16]{0,1:T(8,128)S(1)}, s32[80,16]{0,1:T(8,128)S(1)}, u32[]{:S(2)}, u32[]{:S(2)}) collective-permute-start(s32[80,16]{0,1:T(8,128)S(1)} %copy-done.12), channel_id=1, source_target_pairs={{0,1},{1,0},{2,3},{3,2},{4,5},{5,4},{6,7},{7,6},{8,9},{9,8},{10,11... | collective-permute-start | bytes 15368 | tf_op jit(solution)/shard_map/ppermute | solution.py:27
  6.3 2.7 %collective-permute-start.3 = (f32[80,16]{0,1:T(8,128)S(1)}, f32[80,16]{0,1:T(8,128)S(1)}, u32[]{:S(2)}, u32[]{:S(2)}) collective-permute-start(f32[80,16]{0,1:T(8,128)S(1)} %copy-done.13), channel_id=1, source_target_pairs={{0,1},{1,0},{2,3},{3,2},{4,5},{5,4},{6,7},{7,6},{8,9},{9,8},{10,11... | collective-permute-start | bytes 15368 | tf_op jit(solution)/shard_map/ppermute | solution.py:27
  6.8 1.3 %copy-start.9 = (bf16[80,720]{1,0:T(8,128)(2,1)}, bf16[80,720]{1,0:T(8,128)(2,1)S(1)}, u32[]{:S(2)}) copy-start(bf16[80,720]{1,0:T(8,128)(2,1)S(1)} %convert_element_type.14) | copy-start | bytes 345604
  26.0 2.1 %copy-start.5 = (bf16[80,3072]{1,0:T(8,128)(2,1)}, bf16[80,3072]{1,0:T(8,128)(2,1)S(1)}, u32[]{:S(2)}) copy-start(bf16[80,3072]{1,0:T(8,128)(2,1)S(1)} %collective-permute-done.1) | copy-start | bytes 1474564
  28.0 15.1 %all-to-all-start = ((bf16[2,240,3072]{2,1,0:T(8,128)(2,1)}), bf16[2,240,3072]{2,1,0:T(8,128)(2,1)S(1)}, u32[]{:S(2)}, u32[]{:S(2)}) async-start(bf16[2,240,3072]{2,1,0:T(8,128)(2,1)} %broadcast_in_dim.6), calls=%async_computation | async-start | bytes 5898240 | tf_op jit(solution)/shard_map/all_to_all | solution.py:32
  32.0 18.3 %collective-permute-start.4 = (bf16[80,3072]{1,0:T(8,128)(2,1)S(1)}, bf16[80,3072]{1,0:T(8,128)(2,1)}, u32[]{:S(2)}, u32[]{:S(2)}) collective-permute-start(bf16[80,3072]{1,0:T(8,128)(2,1)S(1)} %collective-permute-done), channel_id=1, source_target_pairs={{0,254},{1,255},{2,0},{3,1},{4,2},{5,3},{6,4},{7,5},{8,6},{9,7},{1... | collective-permute-start | bytes 1474568 | tf_op jit(solution)/shard_map/ppermute | solution.py:22
  39.2 13.6 %collective-permute-start.5 = (bf16[80,3072]{1,0:T(8,128)(2,1)}, bf16[80,3072]{1,0:T(8,128)(2,1)}, u32[]{:S(2)}, u32[]{:S(2)}) collective-permute-start(bf16[80,3072]{1,0:T(8,128)(2,1)} %copy-done.5), channel_id=1, source_target_pairs={{0,2},{1,3},{2,4},{3,5},{4,6},{5,7},{6,8},{7,9},{8,10},{9,11},{10,... | collective-permute-start | bytes 1474568 | tf_op jit(solution)/shard_map/ppermute | solution.py:22
  43.6 15.0 %copy-start.8 = (f32[80,3072]{1,0:T(8,128)S(1)}, f32[80,3072]{1,0:T(8,128)}, u32[]{:S(2)}) copy-start(f32[80,3072]{1,0:T(8,128)} %fusion) | copy-start | bytes 2949124
  43.6 15.0 %copy-start.11 = (bf16[80,80]{1,0:T(8,128)(2,1)S(1)}, bf16[80,80]{1,0:T(8,128)(2,1)}, u32[]{:S(2)}) copy-start(bf16[80,80]{1,0:T(8,128)(2,1)} %get-tuple-element.16) | copy-start | bytes 38404
  58.5 1.9 %copy-start.1 = (f32[80,2048]{1,0:T(8,128)S(1)}, f32[80,2048]{1,0:T(8,128)}, u32[]{:S(2)}) copy-start(f32[80,2048]{1,0:T(8,128)} %copy-done) | copy-start | bytes 1966084
  58.5 1.9 %copy-start.3 = (f32[80,2048]{1,0:T(8,128)S(1)}, f32[80,2048]{1,0:T(8,128)}, u32[]{:S(2)}) copy-start(f32[80,2048]{1,0:T(8,128)} %copy-done.2) | copy-start | bytes 1966084
  58.6 2.8 %copy-start.4 = (bf16[2048,1024]{1,0:T(8,128)(2,1)S(1)}, bf16[2048,1024]{1,0:T(8,128)(2,1)}, u32[]{:S(2)}) copy-start(bf16[2048,1024]{1,0:T(8,128)(2,1)} %param.12) | copy-start | bytes 12582916
  61.4 5.2 %copy-start.6 = (bf16[80,2048]{1,0:T(8,128)(2,1)}, bf16[80,2048]{1,0:T(8,128)(2,1)S(1)}, u32[]{:S(2)}) copy-start(bf16[80,2048]{1,0:T(8,128)(2,1)S(1)} %pad_maximum_fusion.2) | copy-start | bytes 983044
  61.4 5.2 %copy-start.7 = (f32[512,160]{0,1:T(8,128)S(1)}, f32[512,160]{0,1:T(8,128)}, u32[]{:S(2)}) copy-start(f32[512,160]{0,1:T(8,128)} %select_reduce_fusion) | copy-start | bytes 983044

commit v8 on v6

--- a/solution.py
+++ b/solution.py
@@ -42,14 +42,14 @@
     grn = green.astype(jnp.float32)
     rec_real, rec_imag = (rec[:, :F], rec[:, F:])
     green_real, green_imag = (grn[:, :F], grn[:, F:])
-    both = jnp.concatenate(
-        [
-            rec_real * green_real + rec_imag * green_imag,
-            rec_real * green_imag - rec_imag * green_real,
-            green_real * green_real + green_imag * green_imag,
-        ],
-        axis=1,
-    ).astype(jnp.bfloat16)
+    d_real, d_imag = (records[:, :F], records[:, F:])
+    g_real, g_imag = (green[:, :F], green[:, F:])
+    wide = lambda parts: jnp.concatenate(parts, axis=1).astype(jnp.float32)
+    a = wide([d_real, d_real, g_real])
+    b = wide([g_real, g_imag, g_real])
+    c = wide([d_imag, -d_imag, g_imag])
+    d = wide([g_imag, g_real, g_imag])
+    both = (a * b + c * d).astype(jnp.bfloat16)
     mask_bf = pair_mask.astype(jnp.bfloat16)
     first = lax.axis_index(SUB) % 2 == 0
 
@@ -66,21 +66,19 @@
     weights = jnp.concatenate([tile_weights, swap(tile_weights, count)], axis=0)
     ahead = shifted(both, -2, count)
     behind = shifted(both, 2, count)
-    neighbour = swap(both, count)
     ahead2 = shifted(ahead, -2, count)
     behind2 = shifted(behind, 2, count)
     total = jnp.dot(cols(HALF), both, preferred_element_type=jnp.float32)
     total = add(total, cols(HALF + 2), ahead)
     total = add(total, cols(HALF - 2), behind)
-    total = add(total, picked(HALF + 1, HALF - 1), neighbour)
     tile_ids = jnp.asarray(tile_order()[: TT * count // SIZES[-1]]) + TT * (
         lax.axis_index(SUB) % 2
     )
     onehot = (lists[None, :, :] == tile_ids[:, None, None]).astype(jnp.float32)
     tile_map = jnp.sum(onehot * weights[None, :, :], axis=2)
     total, tile_map = lax.optimization_barrier((total, tile_map))
-    swapped = swap(jnp.concatenate([ahead, behind], axis=0), count)
-    columns = [picked(HALF + 3, HALF + 1), picked(HALF - 1, HALF - 3)]
+    swapped = swap(jnp.concatenate([both, ahead, behind], axis=0), count)
+    columns = [picked(HALF + 1, HALF - 1), picked(HALF + 3, HALF + 1), picked(HALF - 1, HALF - 3)]
     total = add(total, jnp.concatenate(columns, axis=1), swapped)
     last = swap(jnp.where(first, ahead2, behind2), count)
     columns = [cols(HALF + 4), cols(HALF - 4), picked(HALF - 3, HALF + 3)]

time: 106 us -> 106 us (level)
  waiting for transfers between devices: 26.9 us -> 30.6 us
  other arithmetic: 8.57 us -> 6.58 us
  matrix products: 8.41 us -> 6.63 us
    ppermute x4, waiting for transfers between devices: 25 us -> 29.2 us  [shifted(): return lax.ppermute(value, SUB, pairs)]
    slice x1, other arithmetic: 1.56 us -> 0.1 us  [cols(): return mask_bf[:, offset * C:(offset + 1) * C]]
    convert_element_type x0 -> x1, other arithmetic: none -> 1.34 us  [body(): both = (a * b + c * d).astype(jnp.bfloat16)]
    slice x0 -> x1, other arithmetic: none -> 1.28 us  [body(): d_real, d_imag = (records[:, :F], records[:, F:])]
    dot_general x5 -> x4, matrix products: 4.36 us -> 3.6 us  [add(): return total + jnp.dot(columns, moving, preferred_element_type=jnp.float32)]
  transfers between devices with their start and end apart: 10 -> 9, of which waited for: 6 -> 7; matrix products, arithmetic and copies ran while one was open for 9% -> 5% of each run, Pallas kernels for 0% -> 0%
where the time goes in v8:
time: 106 us
  blocking collectives  48.4 us (46%)
  waiting for transfers between devices  30.6 us (29%)
  starting transfers between devices  10.8 us (10%)
  matrix products  6.63 us (6%)
  other arithmetic  6.58 us (6%)
  local copies, waits for them, and re-layouts  1.75 us (2%)
    all_to_all x2, blocking collectives, body(): part = jnp.sum(lax.all_to_all(part, group, 0, 0, tiled=False), axis=0)  48.4 us
    ppermute x4, waiting for transfers between devices, shifted(): return lax.ppermute(value, SUB, pairs)  29.2 us
    ppermute x4, starting transfers between devices, shifted(): return lax.ppermute(value, SUB, pairs)  9.57 us
    dot_general x4, matrix products, add(): return total + jnp.dot(columns, moving, preferred_element_type=jnp.float32)  3.6 us
  transfers between devices with their start and end apart: 9, of which 7 were waited for; matrix products, arithmetic and copies ran while one was open for 5% of the time, Pallas kernels for 0%

profile of v8, /device:TPU:2, one launch (start us, length us, event | category | flops | bytes accessed | tf_op | source)
XLA Modules:
  0.0 105.6 jit_solution(3139991518188975767)
XLA Ops:
  0.6 0.0 copy-start.7
  0.6 0.0 copy-start.3
  0.7 0.0 copy-start.1
  0.7 0.0 copy-start.5
  0.7 0.0 copy-start.6
  0.7 0.0 copy-start.4
  0.7 1.3 %fusion.39 = (bf16[80,1024]{1,0:T(8,128)(2,1)S(1)}, bf16[80,1024]{1,0:T(8,128)(2,1)S(1)}, bf16[80,1024]{1,0:T(8,128)(2,1)S(1)}, bf16[80,1024]{1,0:T(8,128)(2,1)S(1)}, bf16[80,1024]{1,0:T(8,128)(2,1)S(1)}) fusion(bf16[80,2048]{1,0:T(8,128)(2,1)} %param.7, bf16[80,2048]{1,0:T(8,128)(2,1)} %param.8), kind=kLoop, calls=%fused_computation.54 | loop fusion | flops 81920 | bytes 1474560 | tf_op jit(solution)/shard_map/slice | solution.py:45
  2.0 1.3 %add_convert_fusion = bf16[80,3072]{1,0:T(8,128)(2,1)S(1)} fusion(bf16[80,1024]{1,0:T(8,128)(2,1)S(1)} %get-tuple-element.19, bf16[80,1024]{1,0:T(8,128)(2,1)S(1)} %get-tuple-element.10, bf16[80,2048]{1,0:T(8,128)(2,1)} %param.8, bf16[80,1024]{1,0:T(8,128)(2,1)S(1)} %get-tuple-element.20, bf16[80,1024]{1,0:T(8,128)(2,1)S(1)} %get-tuple-element.9, ...), kind=kLoop, calls=%fused_computation.13 | loop fusion | flops 5652480 | bytes 1638400 | tf_op jit(solution)/shard_map/convert_element_type | solution.py:52
  3.3 2.3 %collective-permute-start = (bf16[80,3072]{1,0:T(8,128)(2,1)S(1)}, bf16[80,3072]{1,0:T(8,128)(2,1)}, u32[]{:S(2)}, u32[]{:S(2)}) collective-permute-start(bf16[80,3072]{1,0:T(8,128)(2,1)S(1)} %add_convert_fusion), channel_id=1, source_target_pairs={{0,254},{1,255},{2,0},{3,1},{4,2},{5,3},{6,4},{7,5},{8,6},{9,7},{1... | collective-permute-start | bytes 1474568 | tf_op jit(solution)/shard_map/ppermute | solution.py:22
  5.6 0.0 collective-permute-start.1
  5.6 0.0 copy-done.5
  5.6 0.0 collective-permute-start.2
  5.6 0.0 copy-done.6
  5.7 0.5 collective-permute-start.3
  6.2 0.0 copy-done.4
  6.2 0.3 fusion.34
  6.5 0.1 fusion.41
  6.6 0.0 copy-done.7
  6.6 0.0 copy-done.3
  6.7 0.0 copy-done.1
  6.8 0.1 collective-permute-done.2
  6.8 0.1 pad_add_fusion
  6.9 0.1 copy.13
  7.0 0.0 collective-permute-done.3
  7.0 0.1 pad_maximum_fusion.4
  7.1 0.1 copy.14
  7.2 9.3 %collective-permute-done = bf16[80,3072]{1,0:T(8,128)(2,1)} collective-permute-done((bf16[80,3072]{1,0:T(8,128)(2,1)S(1)}, bf16[80,3072]{1,0:T(8,128)(2,1)}, u32[]{:S(2)}, u32[]{:S(2)}) %collective-permute-start) | collective-permute-done | bytes 491552 | tf_op jit(solution)/shard_map/ppermute | solution.py:22
  16.5 9.0 %collective-permute-done.1 = bf16[80,3072]{1,0:T(8,128)(2,1)} collective-permute-done((bf16[80,3072]{1,0:T(8,128)(2,1)S(1)}, bf16[80,3072]{1,0:T(8,128)(2,1)}, u32[]{:S(2)}, u32[]{:S(2)}) %collective-permute-start.1) | collective-permute-done | bytes 491552 | tf_op jit(solution)/shard_map/ppermute | solution.py:22
  25.5 1.3 %pad_maximum_fusion = bf16[240,3072]{1,0:T(8,128)(2,1)S(1)} fusion(bf16[80,3072]{1,0:T(8,128)(2,1)} %collective-permute-done.1, bf16[80,3072]{1,0:T(8,128)(2,1)} %collective-permute-done, bf16[80,3072]{1,0:T(8,128)(2,1)S(1)} %add_convert_fusion), kind=kLoop, calls=%fused_computation.4 | loop fusion | flops 4423680 | bytes 2949120 | tf_op jit(solution)/shard_map/concatenate | solution.py:80
  26.8 0.1 collective-permute-start.4
  26.9 7.2 %collective-permute-start.5 = (bf16[80,3072]{1,0:T(8,128)(2,1)}, bf16[80,3072]{1,0:T(8,128)(2,1)S(1)}, u32[]{:S(2)}, u32[]{:S(2)}) collective-permute-start(bf16[80,3072]{1,0:T(8,128)(2,1)} %collective-permute-done), channel_id=1, source_target_pairs={{0,254},{1,255},{2,0},{3,1},{4,2},{5,3},{6,4},{7,5},{8,6},{9,7},{1... | collective-permute-start | bytes 1474568 | tf_op jit(solution)/shard_map/ppermute | solution.py:22
  34.1 0.0 collective-permute-start.6
  34.1 1.2 %select_reduce_fusion = f32[512,160]{0,1:T(8,128)S(1)} fusion(f32[160,16]{1,0:T(8,128)S(1)} %copy.14, s32[512]{0:T(512)S(1)} %broadcast_add_fusion, s32[160,16]{1,0:T(8,128)S(1)} %copy.13), kind=kLoop, calls=%fused_computation | loop fusion | flops 3850240 | bytes 350208 | tf_op jit(solution)/shard_map/reduce_sum | solution.py:78
  35.3 1.4 %convolution_add_fusion.1 = f32[3072,80]{0,1:T(8,128)S(1)} fusion(f32[3072,80]{0,1:T(8,128)S(1)} %fusion.34, bf16[80,3072]{1,0:T(8,128)(2,1)} %collective-permute-done, bf16[80,720]{1,0:T(8,128)(2,1)S(1)} %convert_element_type.32), kind=kOutput, calls=%fused_computation.2 | convolution fusion | flops 39567360 | bytes 2478080 | tf_op jit(solution)/shard_map/dot_general | solution.py:63
  36.7 8.8 %collective-permute-done.5 = bf16[80,3072]{1,0:T(8,128)(2,1)S(1)} collective-permute-done((bf16[80,3072]{1,0:T(8,128)(2,1)}, bf16[80,3072]{1,0:T(8,128)(2,1)S(1)}, u32[]{:S(2)}, u32[]{:S(2)}) %collective-permute-start.5) | collective-permute-done | bytes 491552 | tf_op jit(solution)/shard_map/ppermute | solution.py:22
  45.5 2.1 %collective-permute-done.6 = bf16[80,3072]{1,0:T(8,128)(2,1)S(1)} collective-permute-done((bf16[80,3072]{1,0:T(8,128)(2,1)}, bf16[80,3072]{1,0:T(8,128)(2,1)S(1)}, u32[]{:S(2)}, u32[]{:S(2)}) %collective-permute-start.6) | collective-permute-done | bytes 491552 | tf_op jit(solution)/shard_map/ppermute | solution.py:22
  47.6 0.1 broadcast_select_fusion
  47.6 0.1 collective-permute-start.7
  47.7 1.3 %fusion = f32[80,3072]{1,0:T(8,128)S(1)} fusion(f32[3072,80]{0,1:T(8,128)S(1)} %convolution_add_fusion.1, bf16[80,3072]{1,0:T(8,128)(2,1)} %collective-permute-done.1, bf16[80,720]{1,0:T(8,128)(2,1)S(1)} %convert_element_type.32), kind=kOutput, calls=%fused_computation.3 | convolution fusion | flops 39567360 | bytes 2478080 | tf_op jit(solution)/shard_map/dot_general | solution.py:63
  49.1 0.0 collective-permute-done.4
  49.1 0.4 fusion.21
  49.5 0.1 collective-permute-done.7
  49.6 0.0 copy-start
  49.6 0.5 fusion.9
  50.1 0.2 fusion.20
  50.3 1.4 %copy-done = bf16[2048,1024]{1,0:T(8,128)(2,1)S(1)} copy-done((bf16[2048,1024]{1,0:T(8,128)(2,1)S(1)}, bf16[2048,1024]{1,0:T(8,128)(2,1)}, u32[]{:S(2)}) %copy-start) | copy-done | bytes 4194328
  51.8 0.0 copy-start.2
  51.8 0.9 fusion.42
  52.6 0.5 collective-permute-start.8
  53.2 1.3 %collective-permute-done.8 = f32[80,1024]{1,0:T(8,128)S(1)} collective-permute-done((f32[80,1024]{1,0:T(8,128)S(1)}, f32[80,1024]{1,0:T(8,128)S(1)}, u32[]{:S(2)}, u32[]{:S(2)}) %collective-permute-start.8) | collective-permute-done | bytes 327712 | tf_op jit(solution)/shard_map/ppermute | solution.py:27
  54.4 1.8 %fusion.13 = f32[512,1024]{1,0:T(8,128)S(1)} fusion(f32[512,160]{0,1:T(8,128)S(1)} %select_reduce_fusion, f32[80,1024]{1,0:T(8,128)S(1)} %collective-permute-done.8, f32[80,1024]{1,0:T(8,128)S(1)} %fusion.42), kind=kOutput, calls=%fused_computation.14 | convolution fusion | flops 1006796800 | bytes 3080192 | tf_op jit(solution)/shard_map/dot_general | solution.py:95
  56.3 0.0 copy-done.2
  56.3 33.9 %all_to_all.10 = f32[8,64,1024]{2,1,0:T(8,128)S(1)} all-to-all(f32[8,64,1024]{2,1,0:T(8,128)S(1)} %bitcast.10), channel_id=1, replica_groups=mesh['y'=4,'z'=4,'x'=8,'c'=2] {'x'}, dimensions={0} | all-to-all | bytes 4194304 | tf_op jit(solution)/shard_map/all_to_all | solution.py:99
  90.2 0.1 reduce_sum.28
  90.4 0.1 reshape.14
  90.5 14.5 %all_to_all.11 = f32[16,4,1024]{2,1,0:T(4,128)S(1)} all-to-all(f32[16,4,1024]{2,1,0:T(4,128)S(1)} %reshape.14), channel_id=1, replica_groups=mesh['y'=4,'z'=4,'x'=8,'c'=2] {'z','y'}, dimensions={0} | all-to-all | bytes 524288 | tf_op jit(solution)/shard_map/all_to_all | solution.py:99
  104.9 0.7 reduce_sum.29
  (5 shorter events, 0.1 us)
Async XLA Ops:
  0.6 6.0 %copy-start.7 = (s32[512]{0:T(512)S(1)}, s32[512]{0:T(512)}, u32[]{:S(2)}) copy-start(s32[512]{0:T(512)} %constant.47.clone) | copy-start | bytes 6148
  0.6 6.0 %copy-start.3 = (bf16[80,2048]{1,0:T(8,128)(2,1)S(1)}, bf16[80,2048]{1,0:T(8,128)(2,1)}, u32[]{:S(2)}) copy-start(bf16[80,2048]{1,0:T(8,128)(2,1)} %param.7) | copy-start | bytes 983044
  0.7 6.0 %copy-start.1 = (bf16[80,2048]{1,0:T(8,128)(2,1)S(1)}, bf16[80,2048]{1,0:T(8,128)(2,1)}, u32[]{:S(2)}) copy-start(bf16[80,2048]{1,0:T(8,128)(2,1)} %param.8) | copy-start | bytes 983044
  0.7 5.0 %copy-start.5 = (s32[80,16]{0,1:T(8,128)S(1)}, s32[80,16]{0,1:T(8,128)}, u32[]{:S(2)}) copy-start(s32[80,16]{0,1:T(8,128)} %param.10) | copy-start | bytes 15364
  0.7 5.0 %copy-start.6 = (f32[80,16]{0,1:T(8,128)S(1)}, f32[80,16]{0,1:T(8,128)}, u32[]{:S(2)}) copy-start(f32[80,16]{0,1:T(8,128)} %param.11) | copy-start | bytes 15364
  0.7 5.5 %copy-start.4 = (s32[80,720]{1,0:T(8,128)S(1)}, s32[80,720]{1,0:T(8,128)}, u32[]{:S(2)}) copy-start(s32[80,720]{1,0:T(8,128)} %param.9) | copy-start | bytes 691204
  3.3 13.1 %collective-permute-start = (bf16[80,3072]{1,0:T(8,128)(2,1)S(1)}, bf16[80,3072]{1,0:T(8,128)(2,1)}, u32[]{:S(2)}, u32[]{:S(2)}) collective-permute-start(bf16[80,3072]{1,0:T(8,128)(2,1)S(1)} %add_convert_fusion), channel_id=1, source_target_pairs={{0,254},{1,255},{2,0},{3,1},{4,2},{5,3},{6,4},{7,5},{8,6},{9,7},{1... | collective-permute-start | bytes 1474568 | tf_op jit(solution)/shard_map/ppermute | solution.py:22
  5.6 19.8 %collective-permute-start.1 = (bf16[80,3072]{1,0:T(8,128)(2,1)S(1)}, bf16[80,3072]{1,0:T(8,128)(2,1)}, u32[]{:S(2)}, u32[]{:S(2)}) collective-permute-start(bf16[80,3072]{1,0:T(8,128)(2,1)S(1)} %add_convert_fusion), channel_id=1, source_target_pairs={{0,2},{1,3},{2,4},{3,5},{4,6},{5,7},{6,8},{7,9},{8,10},{9,11},{10,... | collective-permute-start | bytes 1474568 | tf_op jit(solution)/shard_map/ppermute | solution.py:22
  5.6 1.2 %collective-permute-start.2 = (s32[80,16]{0,1:T(8,128)S(1)}, s32[80,16]{0,1:T(8,128)S(1)}, u32[]{:S(2)}, u32[]{:S(2)}) collective-permute-start(s32[80,16]{0,1:T(8,128)S(1)} %copy-done.5), channel_id=1, source_target_pairs={{0,1},{1,0},{2,3},{3,2},{4,5},{5,4},{6,7},{7,6},{8,9},{9,8},{10,11... | collective-permute-start | bytes 15368 | tf_op jit(solution)/shard_map/ppermute | solution.py:27
  5.7 1.3 %collective-permute-start.3 = (f32[80,16]{0,1:T(8,128)S(1)}, f32[80,16]{0,1:T(8,128)S(1)}, u32[]{:S(2)}, u32[]{:S(2)}) collective-permute-start(f32[80,16]{0,1:T(8,128)S(1)} %copy-done.6), channel_id=1, source_target_pairs={{0,1},{1,0},{2,3},{3,2},{4,5},{5,4},{6,7},{7,6},{8,9},{9,8},{10,11... | collective-permute-start | bytes 15368 | tf_op jit(solution)/shard_map/ppermute | solution.py:27
  26.8 22.3 %collective-permute-start.4 = (bf16[240,3072]{1,0:T(8,128)(2,1)S(1)}, bf16[240,3072]{1,0:T(8,128)(2,1)S(1)}, u32[]{:S(2)}, u32[]{:S(2)}) collective-permute-start(bf16[240,3072]{1,0:T(8,128)(2,1)S(1)} %pad_maximum_fusion), channel_id=1, source_target_pairs={{0,1},{1,0},{2,3},{3,2},{4,5},{5,4},{6,7},{7,6},{8,9},{9,8},{10,11... | collective-permute-start | bytes 4423688 | tf_op jit(solution)/shard_map/ppermute | solution.py:27
  26.9 18.6 %collective-permute-start.5 = (bf16[80,3072]{1,0:T(8,128)(2,1)}, bf16[80,3072]{1,0:T(8,128)(2,1)S(1)}, u32[]{:S(2)}, u32[]{:S(2)}) collective-permute-start(bf16[80,3072]{1,0:T(8,128)(2,1)} %collective-permute-done), channel_id=1, source_target_pairs={{0,254},{1,255},{2,0},{3,1},{4,2},{5,3},{6,4},{7,5},{8,6},{9,7},{1... | collective-permute-start | bytes 1474568 | tf_op jit(solution)/shard_map/ppermute | solution.py:22
  34.1 13.5 %collective-permute-start.6 = (bf16[80,3072]{1,0:T(8,128)(2,1)}, bf16[80,3072]{1,0:T(8,128)(2,1)S(1)}, u32[]{:S(2)}, u32[]{:S(2)}) collective-permute-start(bf16[80,3072]{1,0:T(8,128)(2,1)} %collective-permute-done.1), channel_id=1, source_target_pairs={{0,2},{1,3},{2,4},{3,5},{4,6},{5,7},{6,8},{7,9},{8,10},{9,11},{10,... | collective-permute-start | bytes 1474568 | tf_op jit(solution)/shard_map/ppermute | solution.py:22
  47.6 2.0 %collective-permute-start.7 = (bf16[80,3072]{1,0:T(8,128)(2,1)S(1)}, bf16[80,3072]{1,0:T(8,128)(2,1)S(1)}, u32[]{:S(2)}, u32[]{:S(2)}) collective-permute-start(bf16[80,3072]{1,0:T(8,128)(2,1)S(1)} %broadcast_select_fusion), channel_id=1, source_target_pairs={{0,1},{1,0},{2,3},{3,2},{4,5},{5,4},{6,7},{7,6},{8,9},{9,8},{10,11... | collective-permute-start | bytes 1474568 | tf_op jit(solution)/shard_map/ppermute | solution.py:27
  49.6 2.2 %copy-start = (bf16[2048,1024]{1,0:T(8,128)(2,1)S(1)}, bf16[2048,1024]{1,0:T(8,128)(2,1)}, u32[]{:S(2)}) copy-start(bf16[2048,1024]{1,0:T(8,128)(2,1)} %param.12) | copy-start | bytes 12582916
  51.8 4.5 %copy-start.2 = (bf16[80,2048]{1,0:T(8,128)(2,1)}, bf16[80,2048]{1,0:T(8,128)(2,1)S(1)}, u32[]{:S(2)}) copy-start(bf16[80,2048]{1,0:T(8,128)(2,1)S(1)} %pad_maximum_fusion.3) | copy-start | bytes 983044
  52.6 1.8 %collective-permute-start.8 = (f32[80,1024]{1,0:T(8,128)S(1)}, f32[80,1024]{1,0:T(8,128)S(1)}, u32[]{:S(2)}, u32[]{:S(2)}) collective-permute-start(f32[80,1024]{1,0:T(8,128)S(1)} %fusion.42), channel_id=1, source_target_pairs={{0,1},{1,0},{2,3},{3,2},{4,5},{5,4},{6,7},{7,6},{8,9},{9,8},{10,11... | collective-permute-start | bytes 983048 | tf_op jit(solution)/shard_map/ppermute | solution.py:27

commit v9 on v8

--- a/solution.py
+++ b/solution.py
@@ -91,8 +91,9 @@
     adj_imag = rec_real * q_imag + rec_imag * q_real - green_imag * psum
     adjoint = jnp.concatenate([adj_real, adj_imag], axis=1).astype(jnp.bfloat16)
     response = jnp.dot(adjoint, tile_green, preferred_element_type=jnp.float32)
-    responses = jnp.concatenate([response, swap(response, count)], axis=0)
-    part = jnp.dot(tile_map, responses, precision=lax.Precision.HIGHEST)
+    part = jnp.dot(tile_map[:, :C], response, precision=lax.Precision.HIGHEST)
+    partner = swap(response, count)
+    part = part + jnp.dot(tile_map[:, C:], partner, precision=lax.Precision.HIGHEST)
     for group in STAGES:
         ways = int(np.prod([SIZES[SUB.index(a)] for a in group]))
         part = part.reshape(ways, -1, part.shape[1])

time: 106 us -> 107 us (level)
  matrix products: 6.63 us -> 8.48 us
  waiting for transfers between devices: 30.6 us -> 29.3 us
    dot_general x1 -> x2, matrix products: 1.84 us -> 3.67 us  [the longest x1 1.84 us: body(): jnp.dot(tile_map[:, C:], partner, precision=lax.Precision.HIGHEST)]
    ppermute x5, waiting for transfers between devices: 1.37 us -> 0.1 us  [swap(): return lax.ppermute(value, SUB, pairs)]
  transfers between devices with their start and end apart: 9 -> 9, of which waited for: 7 -> 4; matrix products, arithmetic and copies ran while one was open for 5% -> 7% of each run, Pallas kernels for 0% -> 0%
where the time goes in v9:
time: 107 us; the launch traced here: 106 us
  blocking collectives  47.9 us (45%)
  waiting for transfers between devices  29.3 us (27%)
  starting transfers between devices  11 us (10%)
  matrix products  8.48 us (8%)
  other arithmetic  6.59 us (6%)
  local copies, waits for them, and re-layouts  1.75 us (2%)
    all_to_all x2, blocking collectives, body(): part = jnp.sum(lax.all_to_all(part, group, 0, 0, tiled=False), axis=0)  47.9 us
    ppermute x4, waiting for transfers between devices, shifted(): return lax.ppermute(value, SUB, pairs)  29.2 us
    ppermute x4, starting transfers between devices, shifted(): return lax.ppermute(value, SUB, pairs)  9.57 us
    dot_general x4, matrix products, add(): return total + jnp.dot(columns, moving, preferred_element_type=jnp.float32)  3.61 us
  transfers between devices with their start and end apart: 9, of which 4 were waited for; matrix products, arithmetic and copies ran while one was open for 7% of the time, Pallas kernels for 0%

profile of v9, /device:TPU:2, one launch (start us, length us, event | category | flops | bytes accessed | tf_op | source)
XLA Modules:
  0.0 105.9 jit_solution(10554331536443948441)
XLA Ops:
  0.6 0.0 copy-start.5
  0.6 0.0 copy-start.6
  0.7 0.0 copy-start.4
  0.7 1.3 %fusion.37 = (bf16[80,1024]{1,0:T(8,128)(2,1)S(1)}, bf16[80,1024]{1,0:T(8,128)(2,1)S(1)}, bf16[80,1024]{1,0:T(8,128)(2,1)S(1)}, bf16[80,1024]{1,0:T(8,128)(2,1)S(1)}, bf16[80,1024]{1,0:T(8,128)(2,1)S(1)}) fusion(bf16[80,2048]{1,0:T(8,128)(2,1)} %param.7, bf16[80,2048]{1,0:T(8,128)(2,1)} %param.8), kind=kLoop, calls=%fused_computation.53 | loop fusion | flops 81920 | bytes 1474560 | tf_op jit(solution)/shard_map/slice | solution.py:45
  1.9 0.0 copy-start.7
  1.9 0.0 copy-start.3
  1.9 0.0 copy-start.1
  2.0 1.4 %add_convert_fusion = bf16[80,3072]{1,0:T(8,128)(2,1)S(1)} fusion(bf16[80,1024]{1,0:T(8,128)(2,1)S(1)} %get-tuple-element.19, bf16[80,1024]{1,0:T(8,128)(2,1)S(1)} %get-tuple-element.10, bf16[80,2048]{1,0:T(8,128)(2,1)} %param.8, bf16[80,1024]{1,0:T(8,128)(2,1)S(1)} %get-tuple-element.20, bf16[80,1024]{1,0:T(8,128)(2,1)S(1)} %get-tuple-element.9, ...), kind=kLoop, calls=%fused_computation.14 | loop fusion | flops 5652480 | bytes 1638400 | tf_op jit(solution)/shard_map/convert_element_type | solution.py:52
  3.3 2.3 %collective-permute-start = (bf16[80,3072]{1,0:T(8,128)(2,1)S(1)}, bf16[80,3072]{1,0:T(8,128)(2,1)}, u32[]{:S(2)}, u32[]{:S(2)}) collective-permute-start(bf16[80,3072]{1,0:T(8,128)(2,1)S(1)} %add_convert_fusion), channel_id=1, source_target_pairs={{0,254},{1,255},{2,0},{3,1},{4,2},{5,3},{6,4},{7,5},{8,6},{9,7},{1... | collective-permute-start | bytes 1474568 | tf_op jit(solution)/shard_map/ppermute | solution.py:22
  5.6 0.0 collective-permute-start.1
  5.7 0.0 copy-done.5
  5.7 0.0 collective-permute-start.2
  5.7 0.0 copy-done.6
  5.7 0.5 collective-permute-start.3
  6.2 0.0 copy-done.4
  6.2 0.3 fusion.33
  6.5 0.1 fusion.39
  6.6 0.0 copy-done.7
  6.6 0.0 copy-done.3
  6.7 0.0 copy-done.1
  6.8 0.0 collective-permute-done.2
  6.8 0.1 pad_add_fusion
  6.9 0.1 copy.13
  7.0 0.0 collective-permute-done.3
  7.0 0.1 pad_maximum_fusion.4
  7.1 0.1 copy.14
  7.2 9.3 %collective-permute-done = bf16[80,3072]{1,0:T(8,128)(2,1)} collective-permute-done((bf16[80,3072]{1,0:T(8,128)(2,1)S(1)}, bf16[80,3072]{1,0:T(8,128)(2,1)}, u32[]{:S(2)}, u32[]{:S(2)}) %collective-permute-start) | collective-permute-done | bytes 491552 | tf_op jit(solution)/shard_map/ppermute | solution.py:22
  16.5 9.0 %collective-permute-done.1 = bf16[80,3072]{1,0:T(8,128)(2,1)} collective-permute-done((bf16[80,3072]{1,0:T(8,128)(2,1)S(1)}, bf16[80,3072]{1,0:T(8,128)(2,1)}, u32[]{:S(2)}, u32[]{:S(2)}) %collective-permute-start.1) | collective-permute-done | bytes 491552 | tf_op jit(solution)/shard_map/ppermute | solution.py:22
  25.5 1.3 %pad_maximum_fusion = bf16[240,3072]{1,0:T(8,128)(2,1)S(1)} fusion(bf16[80,3072]{1,0:T(8,128)(2,1)} %collective-permute-done.1, bf16[80,3072]{1,0:T(8,128)(2,1)} %collective-permute-done, bf16[80,3072]{1,0:T(8,128)(2,1)S(1)} %add_convert_fusion), kind=kLoop, calls=%fused_computation.5 | loop fusion | flops 4423680 | bytes 2949120 | tf_op jit(solution)/shard_map/concatenate | solution.py:80
  26.8 0.1 collective-permute-start.4
  26.9 7.2 %collective-permute-start.5 = (bf16[80,3072]{1,0:T(8,128)(2,1)}, bf16[80,3072]{1,0:T(8,128)(2,1)S(1)}, u32[]{:S(2)}, u32[]{:S(2)}) collective-permute-start(bf16[80,3072]{1,0:T(8,128)(2,1)} %collective-permute-done), channel_id=1, source_target_pairs={{0,254},{1,255},{2,0},{3,1},{4,2},{5,3},{6,4},{7,5},{8,6},{9,7},{1... | collective-permute-start | bytes 1474568 | tf_op jit(solution)/shard_map/ppermute | solution.py:22
  34.1 0.0 collective-permute-start.6
  34.1 1.2 %select_reduce_fusion = f32[512,160]{0,1:T(8,128)S(1)} fusion(f32[160,16]{1,0:T(8,128)S(1)} %copy.14, s32[512]{0:T(512)S(1)} %broadcast_add_fusion, s32[160,16]{1,0:T(8,128)S(1)} %copy.13), kind=kLoop, calls=%fused_computation | loop fusion | flops 3850240 | bytes 350208 | tf_op jit(solution)/shard_map/reduce_sum | solution.py:78
  35.3 1.4 %convolution_add_fusion.1 = f32[3072,80]{0,1:T(8,128)S(1)} fusion(f32[3072,80]{0,1:T(8,128)S(1)} %fusion.33, bf16[80,3072]{1,0:T(8,128)(2,1)} %collective-permute-done, bf16[80,720]{1,0:T(8,128)(2,1)S(1)} %convert_element_type.32), kind=kOutput, calls=%fused_computation.2 | convolution fusion | flops 39567360 | bytes 2478080 | tf_op jit(solution)/shard_map/dot_general | solution.py:63
  36.7 8.8 %collective-permute-done.5 = bf16[80,3072]{1,0:T(8,128)(2,1)S(1)} collective-permute-done((bf16[80,3072]{1,0:T(8,128)(2,1)}, bf16[80,3072]{1,0:T(8,128)(2,1)S(1)}, u32[]{:S(2)}, u32[]{:S(2)}) %collective-permute-start.5) | collective-permute-done | bytes 491552 | tf_op jit(solution)/shard_map/ppermute | solution.py:22
  45.5 2.1 %collective-permute-done.6 = bf16[80,3072]{1,0:T(8,128)(2,1)S(1)} collective-permute-done((bf16[80,3072]{1,0:T(8,128)(2,1)}, bf16[80,3072]{1,0:T(8,128)(2,1)S(1)}, u32[]{:S(2)}, u32[]{:S(2)}) %collective-permute-start.6) | collective-permute-done | bytes 491552 | tf_op jit(solution)/shard_map/ppermute | solution.py:22
  47.6 0.1 broadcast_select_fusion
  47.6 0.1 collective-permute-start.7
  47.7 1.4 %fusion = f32[80,3072]{1,0:T(8,128)S(1)} fusion(f32[3072,80]{0,1:T(8,128)S(1)} %convolution_add_fusion.1, bf16[80,3072]{1,0:T(8,128)(2,1)} %collective-permute-done.1, bf16[80,720]{1,0:T(8,128)(2,1)S(1)} %convert_element_type.32), kind=kOutput, calls=%fused_computation.3 | convolution fusion | flops 39567360 | bytes 2478080 | tf_op jit(solution)/shard_map/dot_general | solution.py:63
  49.1 0.0 collective-permute-done.4
  49.1 0.4 fusion.20
  49.6 0.0 collective-permute-done.7
  49.6 0.0 copy-start
  49.6 0.5 fusion.9
  50.1 0.2 fusion.16
  50.4 1.4 %copy-done = bf16[2048,1024]{1,0:T(8,128)(2,1)S(1)} copy-done((bf16[2048,1024]{1,0:T(8,128)(2,1)S(1)}, bf16[2048,1024]{1,0:T(8,128)(2,1)}, u32[]{:S(2)}) %copy-start) | copy-done | bytes 4194328
  51.8 0.0 copy-start.2
  51.8 0.9 fusion.40
  52.7 0.0 copy-done.2
  52.7 0.7 collective-permute-start.8
  53.4 1.8 %fusion.18 = f32[512,1024]{1,0:T(8,128)S(1)} fusion(f32[80,1024]{1,0:T(8,128)S(1)} %fusion.40, f32[512,160]{0,1:T(8,128)S(1)} %select_reduce_fusion), kind=kOutput, calls=%fused_computation.26 | convolution fusion | flops 503316480 | bytes 2588672 | tf_op jit(solution)/shard_map/dot_general | solution.py:94
  55.2 0.0 collective-permute-done.8
  55.2 1.8 %convolution_add_fusion.2 = f32[512,1024]{1,0:T(8,128)S(1)} fusion(f32[512,1024]{1,0:T(8,128)S(1)} %fusion.18, f32[80,1024]{1,0:T(8,128)S(1)} %collective-permute-done.8, f32[512,160]{0,1:T(8,128)S(1)} %select_reduce_fusion), kind=kOutput, calls=%fused_computation.4 | convolution fusion | flops 503840768 | bytes 4685824 | tf_op jit(solution)/shard_map/dot_general | solution.py:96
  57.1 33.7 %all_to_all.10 = f32[8,64,1024]{2,1,0:T(8,128)S(1)} all-to-all(f32[8,64,1024]{2,1,0:T(8,128)S(1)} %bitcast.11), channel_id=1, replica_groups=mesh['y'=4,'z'=4,'x'=8,'c'=2] {'x'}, dimensions={0} | all-to-all | bytes 4194304 | tf_op jit(solution)/shard_map/all_to_all | solution.py:100
  90.8 0.1 reduce_sum.28
  91.0 0.1 reshape.14
  91.0 14.2 %all_to_all.11 = f32[16,4,1024]{2,1,0:T(4,128)S(1)} all-to-all(f32[16,4,1024]{2,1,0:T(4,128)S(1)} %reshape.14), channel_id=1, replica_groups=mesh['y'=4,'z'=4,'x'=8,'c'=2] {'z','y'}, dimensions={0} | all-to-all | bytes 524288 | tf_op jit(solution)/shard_map/all_to_all | solution.py:100
  105.2 0.7 reduce_sum.29
  (5 shorter events, 0.1 us)
Async XLA Ops:
  0.6 5.0 %copy-start.5 = (s32[80,16]{0,1:T(8,128)S(1)}, s32[80,16]{0,1:T(8,128)}, u32[]{:S(2)}) copy-start(s32[80,16]{0,1:T(8,128)} %param.10) | copy-start | bytes 15364
  0.6 5.0 %copy-start.6 = (f32[80,16]{0,1:T(8,128)S(1)}, f32[80,16]{0,1:T(8,128)}, u32[]{:S(2)}) copy-start(f32[80,16]{0,1:T(8,128)} %param.11) | copy-start | bytes 15364
  0.7 5.5 %copy-start.4 = (s32[80,720]{1,0:T(8,128)S(1)}, s32[80,720]{1,0:T(8,128)}, u32[]{:S(2)}) copy-start(s32[80,720]{1,0:T(8,128)} %param.9) | copy-start | bytes 691204
  1.9 4.7 %copy-start.7 = (s32[512]{0:T(512)S(1)}, s32[512]{0:T(512)}, u32[]{:S(2)}) copy-start(s32[512]{0:T(512)} %constant.47.clone) | copy-start | bytes 6148
  1.9 4.7 %copy-start.3 = (bf16[80,2048]{1,0:T(8,128)(2,1)S(1)}, bf16[80,2048]{1,0:T(8,128)(2,1)}, u32[]{:S(2)}) copy-start(bf16[80,2048]{1,0:T(8,128)(2,1)} %param.7) | copy-start | bytes 983044
  1.9 4.8 %copy-start.1 = (bf16[80,2048]{1,0:T(8,128)(2,1)S(1)}, bf16[80,2048]{1,0:T(8,128)(2,1)}, u32[]{:S(2)}) copy-start(bf16[80,2048]{1,0:T(8,128)(2,1)} %param.8) | copy-start | bytes 983044
  3.3 13.1 %collective-permute-start = (bf16[80,3072]{1,0:T(8,128)(2,1)S(1)}, bf16[80,3072]{1,0:T(8,128)(2,1)}, u32[]{:S(2)}, u32[]{:S(2)}) collective-permute-start(bf16[80,3072]{1,0:T(8,128)(2,1)S(1)} %add_convert_fusion), channel_id=1, source_target_pairs={{0,254},{1,255},{2,0},{3,1},{4,2},{5,3},{6,4},{7,5},{8,6},{9,7},{1... | collective-permute-start | bytes 1474568 | tf_op jit(solution)/shard_map/ppermute | solution.py:22
  5.6 19.8 %collective-permute-start.1 = (bf16[80,3072]{1,0:T(8,128)(2,1)S(1)}, bf16[80,3072]{1,0:T(8,128)(2,1)}, u32[]{:S(2)}, u32[]{:S(2)}) collective-permute-start(bf16[80,3072]{1,0:T(8,128)(2,1)S(1)} %add_convert_fusion), channel_id=1, source_target_pairs={{0,2},{1,3},{2,4},{3,5},{4,6},{5,7},{6,8},{7,9},{8,10},{9,11},{10,... | collective-permute-start | bytes 1474568 | tf_op jit(solution)/shard_map/ppermute | solution.py:22
  5.7 1.2 %collective-permute-start.2 = (s32[80,16]{0,1:T(8,128)S(1)}, s32[80,16]{0,1:T(8,128)S(1)}, u32[]{:S(2)}, u32[]{:S(2)}) collective-permute-start(s32[80,16]{0,1:T(8,128)S(1)} %copy-done.5), channel_id=1, source_target_pairs={{0,1},{1,0},{2,3},{3,2},{4,5},{5,4},{6,7},{7,6},{8,9},{9,8},{10,11... | collective-permute-start | bytes 15368 | tf_op jit(solution)/shard_map/ppermute | solution.py:27
  5.7 1.3 %collective-permute-start.3 = (f32[80,16]{0,1:T(8,128)S(1)}, f32[80,16]{0,1:T(8,128)S(1)}, u32[]{:S(2)}, u32[]{:S(2)}) collective-permute-start(f32[80,16]{0,1:T(8,128)S(1)} %copy-done.6), channel_id=1, source_target_pairs={{0,1},{1,0},{2,3},{3,2},{4,5},{5,4},{6,7},{7,6},{8,9},{9,8},{10,11... | collective-permute-start | bytes 15368 | tf_op jit(solution)/shard_map/ppermute | solution.py:27
  26.8 22.4 %collective-permute-start.4 = (bf16[240,3072]{1,0:T(8,128)(2,1)S(1)}, bf16[240,3072]{1,0:T(8,128)(2,1)S(1)}, u32[]{:S(2)}, u32[]{:S(2)}) collective-permute-start(bf16[240,3072]{1,0:T(8,128)(2,1)S(1)} %pad_maximum_fusion), channel_id=1, source_target_pairs={{0,1},{1,0},{2,3},{3,2},{4,5},{5,4},{6,7},{7,6},{8,9},{9,8},{10,11... | collective-permute-start | bytes 4423688 | tf_op jit(solution)/shard_map/ppermute | solution.py:27
  26.9 18.6 %collective-permute-start.5 = (bf16[80,3072]{1,0:T(8,128)(2,1)}, bf16[80,3072]{1,0:T(8,128)(2,1)S(1)}, u32[]{:S(2)}, u32[]{:S(2)}) collective-permute-start(bf16[80,3072]{1,0:T(8,128)(2,1)} %collective-permute-done), channel_id=1, source_target_pairs={{0,254},{1,255},{2,0},{3,1},{4,2},{5,3},{6,4},{7,5},{8,6},{9,7},{1... | collective-permute-start | bytes 1474568 | tf_op jit(solution)/shard_map/ppermute | solution.py:22
  34.1 13.5 %collective-permute-start.6 = (bf16[80,3072]{1,0:T(8,128)(2,1)}, bf16[80,3072]{1,0:T(8,128)(2,1)S(1)}, u32[]{:S(2)}, u32[]{:S(2)}) collective-permute-start(bf16[80,3072]{1,0:T(8,128)(2,1)} %collective-permute-done.1), channel_id=1, source_target_pairs={{0,2},{1,3},{2,4},{3,5},{4,6},{5,7},{6,8},{7,9},{8,10},{9,11},{10,... | collective-permute-start | bytes 1474568 | tf_op jit(solution)/shard_map/ppermute | solution.py:22
  47.6 2.0 %collective-permute-start.7 = (bf16[80,3072]{1,0:T(8,128)(2,1)S(1)}, bf16[80,3072]{1,0:T(8,128)(2,1)S(1)}, u32[]{:S(2)}, u32[]{:S(2)}) collective-permute-start(bf16[80,3072]{1,0:T(8,128)(2,1)S(1)} %broadcast_select_fusion), channel_id=1, source_target_pairs={{0,1},{1,0},{2,3},{3,2},{4,5},{5,4},{6,7},{7,6},{8,9},{9,8},{10,11... | collective-permute-start | bytes 1474568 | tf_op jit(solution)/shard_map/ppermute | solution.py:27
  49.6 2.2 %copy-start = (bf16[2048,1024]{1,0:T(8,128)(2,1)S(1)}, bf16[2048,1024]{1,0:T(8,128)(2,1)}, u32[]{:S(2)}) copy-start(bf16[2048,1024]{1,0:T(8,128)(2,1)} %param.12) | copy-start | bytes 12582916
  51.8 0.9 copy-start.2
  52.7 2.6 %collective-permute-start.8 = (f32[80,1024]{1,0:T(8,128)S(1)}, f32[80,1024]{1,0:T(8,128)S(1)}, u32[]{:S(2)}, u32[]{:S(2)}) collective-permute-start(f32[80,1024]{1,0:T(8,128)S(1)} %fusion.40), channel_id=1, source_target_pairs={{0,1},{1,0},{2,3},{3,2},{4,5},{5,4},{6,7},{7,6},{8,9},{9,8},{10,11... | collective-permute-start | bytes 983048 | tf_op jit(solution)/shard_map/ppermute | solution.py:27

commit v10 on v6

--- a/solution.py
+++ b/solution.py
@@ -25,6 +25,11 @@
 def swap(value, count):
     pairs = [(source, source ^ 1) for source in range(count)]
     return lax.ppermute(value, SUB, pairs)
+
+
+def across(value, count):
+    pairs = [(s, s - 1 if s % 2 == 0 else s + 1) for s in range(count)]
+    return lax.ppermute(value, SUB, [(s, t % count) for s, t in pairs])
 
 
 def tile_order():
@@ -66,23 +71,21 @@
     weights = jnp.concatenate([tile_weights, swap(tile_weights, count)], axis=0)
     ahead = shifted(both, -2, count)
     behind = shifted(both, 2, count)
-    neighbour = swap(both, count)
     ahead2 = shifted(ahead, -2, count)
     behind2 = shifted(behind, 2, count)
+    last = across(jnp.where(first, ahead, behind), count)
     total = jnp.dot(cols(HALF), both, preferred_element_type=jnp.float32)
     total = add(total, cols(HALF + 2), ahead)
     total = add(total, cols(HALF - 2), behind)
-    total = add(total, picked(HALF + 1, HALF - 1), neighbour)
     tile_ids = jnp.asarray(tile_order()[: TT * count // SIZES[-1]]) + TT * (
         lax.axis_index(SUB) % 2
     )
     onehot = (lists[None, :, :] == tile_ids[:, None, None]).astype(jnp.float32)
     tile_map = jnp.sum(onehot * weights[None, :, :], axis=2)
     total, tile_map = lax.optimization_barrier((total, tile_map))
-    swapped = swap(jnp.concatenate([ahead, behind], axis=0), count)
-    columns = [picked(HALF + 3, HALF + 1), picked(HALF - 1, HALF - 3)]
+    swapped = swap(jnp.concatenate([both, ahead, behind], axis=0), count)
+    columns = [picked(HALF + 1, HALF - 1), picked(HALF + 3, HALF + 1), picked(HALF - 1, HALF - 3)]
     total = add(total, jnp.concatenate(columns, axis=1), swapped)
-    last = swap(jnp.where(first, ahead2, behind2), count)
     columns = [cols(HALF + 4), cols(HALF - 4), picked(HALF - 3, HALF + 3)]
     stacked = jnp.concatenate([ahead2, behind2, last], axis=0)
     total = add(total, jnp.concatenate(columns, axis=1), stacked)

time: 106 us -> 112 us (1.057)
  other arithmetic: 8.57 us -> 11 us
  starting transfers between devices: 10.4 us -> 12.7 us
  local copies, waits for them, and re-layouts: 1.76 us -> 3.82 us
  blocking collectives: 48.1 us -> 49.8 us
  matrix products: 8.41 us -> 7.16 us
    ppermute x0 -> x1, starting transfers between devices: none -> 7.32 us  [across(): return lax.ppermute(value, SUB, [(s, t % count) for s, t in pairs])]
    ppermute x4, waiting for transfers between devices: 25 us -> 18.2 us  [shifted(): return lax.ppermute(value, SUB, pairs)]
    ppermute x0 -> x1, waiting for transfers between devices: none -> 6.42 us  [across(): return lax.ppermute(value, SUB, [(s, t % count) for s, t in pairs])]
    ppermute x4, starting transfers between devices: 9.46 us -> 4.27 us  [shifted(): return lax.ppermute(value, SUB, pairs)]
    all_to_all x2, blocking collectives: 48.1 us -> 49.8 us  [body(): part = jnp.sum(lax.all_to_all(part, group, 0, 0, tiled=False), axis=0)]
    concatenate x1, local copies, waits for them, and re-layouts: 0.1 us -> 1.45 us  [body(): weights = jnp.concatenate([tile_weights, swap(tile_weights, count)], axis=0)]
    dot_general x5 -> x4, matrix products: 4.36 us -> 3.07 us  [add(): return total + jnp.dot(columns, moving, preferred_element_type=jnp.float32)]
  transfers between devices with their start and end apart: 10 -> 9, of which waited for: 6 -> 5; matrix products, arithmetic and copies ran while one was open for 9% -> 9% of each run, Pallas kernels for 0% -> 0%
where the time goes in v10:
time: 112 us; the launch traced here: 111 us
  blocking collectives  49.8 us (44%)
  waiting for transfers between devices  25.9 us (23%)
  starting transfers between devices  12.7 us (11%)
  other arithmetic  11 us (10%)
  matrix products  7.16 us (6%)
  local copies, waits for them, and re-layouts  3.82 us (3%)
    all_to_all x2, blocking collectives, body(): part = jnp.sum(lax.all_to_all(part, group, 0, 0, tiled=False), axis=0)  49.8 us
    ppermute x4, waiting for transfers between devices, shifted(): return lax.ppermute(value, SUB, pairs)  18.2 us
    ppermute x1, starting transfers between devices, across(): return lax.ppermute(value, SUB, [(s, t % count) for s, t in pairs])  7.32 us
    ppermute x1, waiting for transfers between devices, across(): return lax.ppermute(value, SUB, [(s, t % count) for s, t in pairs])  6.42 us
    ppermute x4, starting transfers between devices, shifted(): return lax.ppermute(value, SUB, pairs)  4.27 us
    dot_general x4, matrix products, add(): return total + jnp.dot(columns, moving, preferred_element_type=jnp.float32)  3.07 us
  transfers between devices with their start and end apart: 9, of which 5 were waited for; matrix products, arithmetic and copies ran while one was open for 9% of the time, Pallas kernels for 0%

profile of v10, /device:TPU:2, one launch (start us, length us, event | category | flops | bytes accessed | tf_op | source)
XLA Modules:
  0.0 111.3 jit_solution(366022192097417971)
XLA Ops:
  0.6 0.0 copy-start.10
  0.6 0.0 copy-start.11
  0.7 0.0 copy-start.4
  0.7 1.1 convert_element_type.12
  1.7 0.0 copy-start.12
  1.7 1.0 convert_element_type.13
  2.8 0.9 add_convert_fusion.1
  3.7 1.8 %pad_maximum_fusion.1 = bf16[80,3072]{1,0:T(8,128)(2,1)} fusion(bf16[80,1024]{1,0:T(8,128)(2,1)} %get-tuple-element.10, bf16[80,1024]{1,0:T(8,128)(2,1)} %get-tuple-element.9, bf16[80,1024]{1,0:T(8,128)(2,1)S(1)} %get-tuple-element.8), kind=kLoop, calls=%fused_computation.17 | loop fusion | flops 1474560 | bytes 983040 | tf_op jit(solution)/shard_map/concatenate | solution.py:50
  5.5 2.2 %collective-permute-start = (bf16[80,3072]{1,0:T(8,128)(2,1)}, bf16[80,3072]{1,0:T(8,128)(2,1)S(1)}, u32[]{:S(2)}, u32[]{:S(2)}) collective-permute-start(bf16[80,3072]{1,0:T(8,128)(2,1)} %pad_maximum_fusion.1), channel_id=1, source_target_pairs={{0,254},{1,255},{2,0},{3,1},{4,2},{5,3},{6,4},{7,5},{8,6},{9,7},{1... | collective-permute-start | bytes 1474568 | tf_op jit(solution)/shard_map/ppermute | solution.py:22
  7.7 0.0 collective-permute-start.1
  7.7 0.0 copy-done.10
  7.7 0.0 collective-permute-start.2
  7.7 0.0 copy-done.11
  7.7 0.5 collective-permute-start.3
  8.2 0.0 copy-done.4
  8.2 0.0 copy-start.2
  8.3 1.4 %fusion.30 = f32[3072,80]{0,1:T(8,128)S(1)} fusion(bf16[80,720]{1,0:T(8,128)(2,1)S(1)} %convert_element_type.14, bf16[80,1024]{1,0:T(8,128)(2,1)} %get-tuple-element.10, bf16[80,1024]{1,0:T(8,128)(2,1)} %get-tuple-element.9, bf16[80,1024]{1,0:T(8,128)(2,1)S(1)} %get-tuple-element.8), kind=kOutput, calls=%fused_computation.38 | convolution fusion | flops 40796160 | bytes 1495040 | tf_op jit(solution)/shard_map/dot_general | solution.py:77
  9.6 0.0 copy-done.2
  9.6 0.7 fusion.35
  10.4 0.0 copy-done.12
  10.4 0.0 collective-permute-done.2
  10.4 0.7 pad_add_fusion
  11.1 0.8 copy.13
  11.9 0.0 collective-permute-done.3
  11.9 1.4 %pad_maximum_fusion.3 = f32[160,16]{0,1:T(8,128)} fusion(f32[80,16]{0,1:T(8,128)} %collective-permute-done.3, f32[80,16]{0,1:T(8,128)S(1)} %copy-done.11), kind=kLoop, calls=%fused_computation.45 | loop fusion | flops 2560 | bytes 20480 | tf_op jit(solution)/shard_map/concatenate | solution.py:71
  13.3 1.4 %copy.14 = f32[160,16]{1,0:T(8,128)} copy(f32[160,16]{0,1:T(8,128)} %pad_maximum_fusion.3) | data formatting | bytes 20480 | tf_op jit(solution)/shard_map/concatenate | solution.py:71
  14.7 3.9 %collective-permute-done = bf16[80,3072]{1,0:T(8,128)(2,1)S(1)} collective-permute-done((bf16[80,3072]{1,0:T(8,128)(2,1)}, bf16[80,3072]{1,0:T(8,128)(2,1)S(1)}, u32[]{:S(2)}, u32[]{:S(2)}) %collective-permute-start) | collective-permute-done | bytes 491552 | tf_op jit(solution)/shard_map/ppermute | solution.py:22
  18.6 9.0 %collective-permute-done.1 = bf16[80,3072]{1,0:T(8,128)(2,1)S(1)} collective-permute-done((bf16[80,3072]{1,0:T(8,128)(2,1)}, bf16[80,3072]{1,0:T(8,128)(2,1)S(1)}, u32[]{:S(2)}, u32[]{:S(2)}) %collective-permute-start.1) | collective-permute-done | bytes 491552 | tf_op jit(solution)/shard_map/ppermute | solution.py:22
  27.7 1.1 pad_maximum_fusion
  28.8 0.1 collective-permute-start.4
  28.9 0.0 copy-done.3
  28.9 1.2 %select_reduce_fusion = f32[512,160]{0,1:T(8,128)S(1)} fusion(f32[160,16]{1,0:T(8,128)S(1)} %copy-done.3, s32[512]{0:T(512)S(1)} %broadcast_add_fusion, s32[160,16]{1,0:T(8,128)S(1)} %copy.13), kind=kLoop, calls=%fused_computation | loop fusion | flops 3850240 | bytes 350208 | tf_op jit(solution)/shard_map/reduce_sum | solution.py:84
  30.1 0.0 copy-start.5
  30.1 0.0 copy-start.6
  30.1 0.1 broadcast_select_fusion
  30.2 7.3 %collective-permute-start.7 = (bf16[80,3072]{1,0:T(8,128)(2,1)S(1)}, bf16[80,3072]{1,0:T(8,128)(2,1)S(1)}, u32[]{:S(2)}, u32[]{:S(2)}) collective-permute-start(bf16[80,3072]{1,0:T(8,128)(2,1)S(1)} %broadcast_select_fusion), channel_id=1, source_target_pairs={{0,255},{1,2},{2,1},{3,4},{4,3},{5,6},{6,5},{7,8},{8,7},{9,10},{10... | collective-permute-start | bytes 1474568 | tf_op jit(solution)/shard_map/ppermute | solution.py:32
  37.5 0.3 collective-permute-start.5
  37.8 1.7 %collective-permute-start.6 = (bf16[80,3072]{1,0:T(8,128)(2,1)S(1)}, bf16[80,3072]{1,0:T(8,128)(2,1)S(1)}, u32[]{:S(2)}, u32[]{:S(2)}) collective-permute-start(bf16[80,3072]{1,0:T(8,128)(2,1)S(1)} %collective-permute-done.1), channel_id=1, source_target_pairs={{0,2},{1,3},{2,4},{3,5},{4,6},{5,7},{6,8},{7,9},{8,10},{9,11},{10,... | collective-permute-start | bytes 1474568 | tf_op jit(solution)/shard_map/ppermute | solution.py:22
  39.5 1.1 convolution_add_fusion.1
  40.6 0.0 copy-start.7
  40.7 0.0 copy-start.8
  40.7 0.0 copy-start.9
  40.7 1.1 fusion
  41.8 0.0 collective-permute-done.4
  41.8 0.0 copy-done.5
  41.8 0.0 copy-done.6
  41.8 0.4 fusion.17
  42.2 6.4 %collective-permute-done.7 = bf16[80,3072]{1,0:T(8,128)(2,1)S(1)} collective-permute-done((bf16[80,3072]{1,0:T(8,128)(2,1)S(1)}, bf16[80,3072]{1,0:T(8,128)(2,1)S(1)}, u32[]{:S(2)}, u32[]{:S(2)}) %collective-permute-start.7) | collective-permute-done | bytes 491552 | tf_op jit(solution)/shard_map/ppermute | solution.py:32
  48.6 5.3 %collective-permute-done.5 = bf16[80,3072]{1,0:T(8,128)(2,1)S(1)} collective-permute-done((bf16[80,3072]{1,0:T(8,128)(2,1)S(1)}, bf16[80,3072]{1,0:T(8,128)(2,1)S(1)}, u32[]{:S(2)}, u32[]{:S(2)}) %collective-permute-start.5) | collective-permute-done | bytes 491552 | tf_op jit(solution)/shard_map/ppermute | solution.py:22
  53.9 0.0 collective-permute-done.6
  53.9 0.0 copy-done.7
  53.9 0.0 copy-start
  53.9 0.5 fusion.9
  54.4 0.2 subtract_convert_fusion.1
  54.7 1.4 %copy-done = bf16[2048,1024]{1,0:T(8,128)(2,1)S(1)} copy-done((bf16[2048,1024]{1,0:T(8,128)(2,1)S(1)}, bf16[2048,1024]{1,0:T(8,128)(2,1)}, u32[]{:S(2)}) %copy-start) | copy-done | bytes 4194328
  56.1 0.9 fusion.36
  57.0 0.6 collective-permute-start.8
  57.5 1.3 %collective-permute-done.8 = f32[80,1024]{1,0:T(8,128)S(1)} collective-permute-done((f32[80,1024]{1,0:T(8,128)S(1)}, f32[80,1024]{1,0:T(8,128)S(1)}, u32[]{:S(2)}, u32[]{:S(2)}) %collective-permute-start.8) | collective-permute-done | bytes 327712 | tf_op jit(solution)/shard_map/ppermute | solution.py:27
  58.8 1.9 %fusion.13 = f32[512,1024]{1,0:T(8,128)S(1)} fusion(f32[512,160]{0,1:T(8,128)S(1)} %select_reduce_fusion, f32[80,1024]{1,0:T(8,128)S(1)} %collective-permute-done.8, f32[80,1024]{1,0:T(8,128)S(1)} %fusion.36), kind=kOutput, calls=%fused_computation.13 | convolution fusion | flops 1006796800 | bytes 3080192 | tf_op jit(solution)/shard_map/dot_general | solution.py:100
  60.7 35.3 %all_to_all.10 = f32[8,64,1024]{2,1,0:T(8,128)S(1)} all-to-all(f32[8,64,1024]{2,1,0:T(8,128)S(1)} %bitcast.9), channel_id=1, replica_groups=mesh['y'=4,'z'=4,'x'=8,'c'=2] {'x'}, dimensions={0} | all-to-all | bytes 4194304 | tf_op jit(solution)/shard_map/all_to_all | solution.py:104
  96.0 0.1 reduce_sum.28
  96.1 0.1 reshape.14
  96.2 14.5 %all_to_all.11 = f32[16,4,1024]{2,1,0:T(4,128)S(1)} all-to-all(f32[16,4,1024]{2,1,0:T(4,128)S(1)} %reshape.14), channel_id=1, replica_groups=mesh['y'=4,'z'=4,'x'=8,'c'=2] {'z','y'}, dimensions={0} | all-to-all | bytes 524288 | tf_op jit(solution)/shard_map/all_to_all | solution.py:104
  110.7 0.7 reduce_sum.29
  (8 shorter events, 0.1 us)
Async XLA Ops:
  0.6 7.1 %copy-start.10 = (s32[80,16]{0,1:T(8,128)S(1)}, s32[80,16]{0,1:T(8,128)}, u32[]{:S(2)}) copy-start(s32[80,16]{0,1:T(8,128)} %param.10) | copy-start | bytes 15364
  0.6 7.1 %copy-start.11 = (f32[80,16]{0,1:T(8,128)S(1)}, f32[80,16]{0,1:T(8,128)}, u32[]{:S(2)}) copy-start(f32[80,16]{0,1:T(8,128)} %param.11) | copy-start | bytes 15364
  0.7 7.6 %copy-start.4 = (s32[80,720]{1,0:T(8,128)S(1)}, s32[80,720]{1,0:T(8,128)}, u32[]{:S(2)}) copy-start(s32[80,720]{1,0:T(8,128)} %param.9) | copy-start | bytes 691204
  1.7 8.6 %copy-start.12 = (s32[512]{0:T(512)S(1)}, s32[512]{0:T(512)}, u32[]{:S(2)}) copy-start(s32[512]{0:T(512)} %constant.47.clone) | copy-start | bytes 6148
  5.5 13.2 %collective-permute-start = (bf16[80,3072]{1,0:T(8,128)(2,1)}, bf16[80,3072]{1,0:T(8,128)(2,1)S(1)}, u32[]{:S(2)}, u32[]{:S(2)}) collective-permute-start(bf16[80,3072]{1,0:T(8,128)(2,1)} %pad_maximum_fusion.1), channel_id=1, source_target_pairs={{0,254},{1,255},{2,0},{3,1},{4,2},{5,3},{6,4},{7,5},{8,6},{9,7},{1... | collective-permute-start | bytes 1474568 | tf_op jit(solution)/shard_map/ppermute | solution.py:22
  7.7 20.0 %collective-permute-start.1 = (bf16[80,3072]{1,0:T(8,128)(2,1)}, bf16[80,3072]{1,0:T(8,128)(2,1)S(1)}, u32[]{:S(2)}, u32[]{:S(2)}) collective-permute-start(bf16[80,3072]{1,0:T(8,128)(2,1)} %pad_maximum_fusion.1), channel_id=1, source_target_pairs={{0,2},{1,3},{2,4},{3,5},{4,6},{5,7},{6,8},{7,9},{8,10},{9,11},{10,... | collective-permute-start | bytes 1474568 | tf_op jit(solution)/shard_map/ppermute | solution.py:22
  7.7 2.7 %collective-permute-start.2 = (s32[80,16]{0,1:T(8,128)S(1)}, s32[80,16]{0,1:T(8,128)S(1)}, u32[]{:S(2)}, u32[]{:S(2)}) collective-permute-start(s32[80,16]{0,1:T(8,128)S(1)} %copy-done.10), channel_id=1, source_target_pairs={{0,1},{1,0},{2,3},{3,2},{4,5},{5,4},{6,7},{7,6},{8,9},{9,8},{10,11... | collective-permute-start | bytes 15368 | tf_op jit(solution)/shard_map/ppermute | solution.py:27
  7.7 4.1 %collective-permute-start.3 = (f32[80,16]{0,1:T(8,128)S(1)}, f32[80,16]{0,1:T(8,128)}, u32[]{:S(2)}, u32[]{:S(2)}) collective-permute-start(f32[80,16]{0,1:T(8,128)S(1)} %copy-done.11), channel_id=1, source_target_pairs={{0,1},{1,0},{2,3},{3,2},{4,5},{5,4},{6,7},{7,6},{8,9},{9,8},{10,11... | collective-permute-start | bytes 15368 | tf_op jit(solution)/shard_map/ppermute | solution.py:27
  8.2 1.4 %copy-start.2 = (bf16[80,720]{1,0:T(8,128)(2,1)}, bf16[80,720]{1,0:T(8,128)(2,1)S(1)}, u32[]{:S(2)}) copy-start(bf16[80,720]{1,0:T(8,128)(2,1)S(1)} %convert_element_type.14) | copy-start | bytes 345604
  14.7 14.2 %copy-start.3 = (f32[160,16]{1,0:T(8,128)S(1)}, f32[160,16]{1,0:T(8,128)}, u32[]{:S(2)}) copy-start(f32[160,16]{1,0:T(8,128)} %copy.14) | copy-start | bytes 30724
  28.8 13.0 %collective-permute-start.4 = (bf16[240,3072]{1,0:T(8,128)(2,1)S(1)}, bf16[240,3072]{1,0:T(8,128)(2,1)S(1)}, u32[]{:S(2)}, u32[]{:S(2)}) collective-permute-start(bf16[240,3072]{1,0:T(8,128)(2,1)S(1)} %pad_maximum_fusion), channel_id=1, source_target_pairs={{0,1},{1,0},{2,3},{3,2},{4,5},{5,4},{6,7},{7,6},{8,9},{9,8},{10,11... | collective-permute-start | bytes 4423688 | tf_op jit(solution)/shard_map/ppermute | solution.py:27
  30.1 11.7 %copy-start.5 = (bf16[80,80]{1,0:T(8,128)(2,1)S(1)}, bf16[80,80]{1,0:T(8,128)(2,1)}, u32[]{:S(2)}) copy-start(bf16[80,80]{1,0:T(8,128)(2,1)} %get-tuple-element.14) | copy-start | bytes 38404
  30.1 11.7 %copy-start.6 = (bf16[80,80]{1,0:T(8,128)(2,1)S(1)}, bf16[80,80]{1,0:T(8,128)(2,1)}, u32[]{:S(2)}) copy-start(bf16[80,80]{1,0:T(8,128)(2,1)} %get-tuple-element.15) | copy-start | bytes 38404
  30.2 18.4 %collective-permute-start.7 = (bf16[80,3072]{1,0:T(8,128)(2,1)S(1)}, bf16[80,3072]{1,0:T(8,128)(2,1)S(1)}, u32[]{:S(2)}, u32[]{:S(2)}) collective-permute-start(bf16[80,3072]{1,0:T(8,128)(2,1)S(1)} %broadcast_select_fusion), channel_id=1, source_target_pairs={{0,255},{1,2},{2,1},{3,4},{4,3},{5,6},{6,5},{7,8},{8,7},{9,10},{10... | collective-permute-start | bytes 1474568 | tf_op jit(solution)/shard_map/ppermute | solution.py:32
  37.5 16.4 %collective-permute-start.5 = (bf16[80,3072]{1,0:T(8,128)(2,1)S(1)}, bf16[80,3072]{1,0:T(8,128)(2,1)S(1)}, u32[]{:S(2)}, u32[]{:S(2)}) collective-permute-start(bf16[80,3072]{1,0:T(8,128)(2,1)S(1)} %collective-permute-done), channel_id=1, source_target_pairs={{0,254},{1,255},{2,0},{3,1},{4,2},{5,3},{6,4},{7,5},{8,6},{9,7},{1... | collective-permute-start | bytes 1474568 | tf_op jit(solution)/shard_map/ppermute | solution.py:22
  37.8 16.1 %collective-permute-start.6 = (bf16[80,3072]{1,0:T(8,128)(2,1)S(1)}, bf16[80,3072]{1,0:T(8,128)(2,1)S(1)}, u32[]{:S(2)}, u32[]{:S(2)}) collective-permute-start(bf16[80,3072]{1,0:T(8,128)(2,1)S(1)} %collective-permute-done.1), channel_id=1, source_target_pairs={{0,2},{1,3},{2,4},{3,5},{4,6},{5,7},{6,8},{7,9},{8,10},{9,11},{10,... | collective-permute-start | bytes 1474568 | tf_op jit(solution)/shard_map/ppermute | solution.py:22
  40.6 13.3 %copy-start.7 = (bf16[80,80]{1,0:T(8,128)(2,1)S(1)}, bf16[80,80]{1,0:T(8,128)(2,1)}, u32[]{:S(2)}) copy-start(bf16[80,80]{1,0:T(8,128)(2,1)} %get-tuple-element.11) | copy-start | bytes 38404
  40.7 13.3 %copy-start.8 = (bf16[80,80]{1,0:T(8,128)(2,1)S(1)}, bf16[80,80]{1,0:T(8,128)(2,1)}, u32[]{:S(2)}) copy-start(bf16[80,80]{1,0:T(8,128)(2,1)} %get-tuple-element.12) | copy-start | bytes 38404
  40.7 13.3 %copy-start.9 = (bf16[80,80]{1,0:T(8,128)(2,1)S(1)}, bf16[80,80]{1,0:T(8,128)(2,1)}, u32[]{:S(2)}) copy-start(bf16[80,80]{1,0:T(8,128)(2,1)} %get-tuple-element.16) | copy-start | bytes 38404
  53.9 2.2 %copy-start = (bf16[2048,1024]{1,0:T(8,128)(2,1)S(1)}, bf16[2048,1024]{1,0:T(8,128)(2,1)}, u32[]{:S(2)}) copy-start(bf16[2048,1024]{1,0:T(8,128)(2,1)} %param.12) | copy-start | bytes 12582916
  56.1 4.5 %copy-start.1 = (bf16[80,2048]{1,0:T(8,128)(2,1)}, bf16[80,2048]{1,0:T(8,128)(2,1)S(1)}, u32[]{:S(2)}) copy-start(bf16[80,2048]{1,0:T(8,128)(2,1)S(1)} %pad_maximum_fusion.2) | copy-start | bytes 983044
  57.0 1.8 %collective-permute-start.8 = (f32[80,1024]{1,0:T(8,128)S(1)}, f32[80,1024]{1,0:T(8,128)S(1)}, u32[]{:S(2)}, u32[]{:S(2)}) collective-permute-start(f32[80,1024]{1,0:T(8,128)S(1)} %fusion.36), channel_id=1, source_target_pairs={{0,1},{1,0},{2,3},{3,2},{4,5},{5,4},{6,7},{7,6},{8,9},{9,8},{10,11... | collective-permute-start | bytes 983048 | tf_op jit(solution)/shard_map/ppermute | solution.py:27

commit v11 on v10

--- a/solution.py
+++ b/solution.py
@@ -25,11 +25,6 @@
 def swap(value, count):
     pairs = [(source, source ^ 1) for source in range(count)]
     return lax.ppermute(value, SUB, pairs)
-
-
-def across(value, count):
-    pairs = [(s, s - 1 if s % 2 == 0 else s + 1) for s in range(count)]
-    return lax.ppermute(value, SUB, [(s, t % count) for s, t in pairs])
 
 
 def tile_order():
@@ -73,7 +68,6 @@
     behind = shifted(both, 2, count)
     ahead2 = shifted(ahead, -2, count)
     behind2 = shifted(behind, 2, count)
-    last = across(jnp.where(first, ahead, behind), count)
     total = jnp.dot(cols(HALF), both, preferred_element_type=jnp.float32)
     total = add(total, cols(HALF + 2), ahead)
     total = add(total, cols(HALF - 2), behind)
@@ -86,6 +80,7 @@
     swapped = swap(jnp.concatenate([both, ahead, behind], axis=0), count)
     columns = [picked(HALF + 1, HALF - 1), picked(HALF + 3, HALF + 1), picked(HALF - 1, HALF - 3)]
     total = add(total, jnp.concatenate(columns, axis=1), swapped)
+    last = swap(jnp.where(first, ahead2, behind2), count)
     columns = [cols(HALF + 4), cols(HALF - 4), picked(HALF - 3, HALF + 3)]
     stacked = jnp.concatenate([ahead2, behind2, last], axis=0)
     total = add(total, jnp.concatenate(columns, axis=1), stacked)
@@ -97,7 +92,7 @@
     adjoint = jnp.concatenate([adj_real, adj_imag], axis=1).astype(jnp.bfloat16)
     response = jnp.dot(adjoint, tile_green, preferred_element_type=jnp.float32)
     responses = jnp.concatenate([response, swap(response, count)], axis=0)
-    part = jnp.dot(tile_map, responses, precision=lax.Precision.HIGHEST)
+    part = jnp.dot(tile_map, responses, precision=lax.Precision.HIGH)
     for group in STAGES:
         ways = int(np.prod([SIZES[SUB.index(a)] for a in group]))
         part = part.reshape(ways, -1, part.shape[1])

time: 112 us -> 106 us (0.946)
  matrix products: 7.16 us -> 4.82 us
  starting transfers between devices: 12.7 us -> 10.4 us
  other arithmetic: 11 us -> 9.27 us
  blocking collectives: 49.8 us -> 48.2 us
  waiting for transfers between devices: 25.9 us -> 27.3 us
    ppermute x1 -> x0, starting transfers between devices: 7.32 us -> none  [across(): return lax.ppermute(value, SUB, [(s, t % count) for s, t in pairs])]
    ppermute x4, waiting for transfers between devices: 18.2 us -> 24.7 us  [shifted(): return lax.ppermute(value, SUB, pairs)]
    ppermute x1 -> x0, waiting for transfers between devices: 6.42 us -> none  [across(): return lax.ppermute(value, SUB, [(s, t % count) for s, t in pairs])]
    ppermute x4, starting transfers between devices: 4.27 us -> 9.46 us  [shifted(): return lax.ppermute(value, SUB, pairs)]
    all_to_all x2, blocking collectives: 49.8 us -> 48.2 us  [body(): part = jnp.sum(lax.all_to_all(part, group, 0, 0, tiled=False), axis=0)]
    ppermute x4 -> x5, waiting for transfers between devices: 1.26 us -> 2.58 us  [swap(): return lax.ppermute(value, SUB, pairs)]
  transfers between devices with their start and end apart: 9 -> 9, of which waited for: 5 -> 6; matrix products, arithmetic and copies ran while one was open for 9% -> 8% of each run, Pallas kernels for 0% -> 0%
where the time goes in v11:
time: 106 us; the launch traced here: 105 us
  blocking collectives  48.2 us (45%)
  waiting for transfers between devices  27.3 us (26%)
  starting transfers between devices  10.4 us (10%)
  other arithmetic  9.27 us (9%)
  matrix products  4.82 us (5%)
  local copies, waits for them, and re-layouts  3.81 us (4%)
    all_to_all x2, blocking collectives, body(): part = jnp.sum(lax.all_to_all(part, group, 0, 0, tiled=False), axis=0)  48.2 us
    ppermute x4, waiting for transfers between devices, shifted(): return lax.ppermute(value, SUB, pairs)  24.7 us
    ppermute x4, starting transfers between devices, shifted(): return lax.ppermute(value, SUB, pairs)  9.46 us
    dot_general x4, matrix products, add(): return total + jnp.dot(columns, moving, preferred_element_type=jnp.float32)  2.59 us
    ppermute x5, waiting for transfers between devices, swap(): return lax.ppermute(value, SUB, pairs)  2.58 us
  transfers between devices with their start and end apart: 9, of which 6 were waited for; matrix products, arithmetic and copies ran while one was open for 8% of the time, Pallas kernels for 0%

profile of v11, /device:TPU:2, one launch (start us, length us, event | category | flops | bytes accessed | tf_op | source)
XLA Modules:
  0.0 104.6 jit_solution(4192967375593708402)
XLA Ops:
  0.6 0.0 copy-start.7
  0.6 0.0 copy-start.8
  0.7 0.0 copy-start.3
  0.7 1.1 %convert_element_type.12 = f32[80,2048]{1,0:T(8,128)S(1)} convert(bf16[80,2048]{1,0:T(8,128)(2,1)} %param.7) | non-fusion elementwise | flops 163840 | bytes 983040 | tf_op jit(solution)/shard_map/convert_element_type | solution.py:41
  1.7 0.0 copy-start.9
  1.7 1.0 convert_element_type.13
  2.8 0.1 add_convert_fusion.1
  2.9 0.8 pad_maximum_fusion.1
  3.7 2.2 %collective-permute-start = (bf16[80,3072]{1,0:T(8,128)(2,1)}, bf16[80,3072]{1,0:T(8,128)(2,1)}, u32[]{:S(2)}, u32[]{:S(2)}) collective-permute-start(bf16[80,3072]{1,0:T(8,128)(2,1)} %pad_maximum_fusion.1), channel_id=1, source_target_pairs={{0,254},{1,255},{2,0},{3,1},{4,2},{5,3},{6,4},{7,5},{8,6},{9,7},{1... | collective-permute-start | bytes 1474568 | tf_op jit(solution)/shard_map/ppermute | solution.py:22
  6.0 0.0 collective-permute-start.1
  6.0 0.0 copy-done.7
  6.0 0.0 collective-permute-start.2
  6.0 0.0 copy-done.8
  6.0 0.5 collective-permute-start.3
  6.5 0.0 copy-done.3
  6.5 0.3 fusion.30
  6.9 0.7 fusion.35
  7.6 0.0 copy-done.9
  7.6 0.0 collective-permute-done.2
  7.6 0.7 pad_add_fusion
  8.2 0.8 copy.13
  9.1 0.0 collective-permute-done.3
  9.1 1.4 %pad_maximum_fusion.3 = f32[160,16]{0,1:T(8,128)} fusion(f32[80,16]{0,1:T(8,128)} %collective-permute-done.3, f32[80,16]{0,1:T(8,128)S(1)} %copy-done.8), kind=kLoop, calls=%fused_computation.45 | loop fusion | flops 2560 | bytes 20480 | tf_op jit(solution)/shard_map/concatenate | solution.py:66
  10.4 1.5 %copy.14 = f32[160,16]{1,0:T(8,128)} copy(f32[160,16]{0,1:T(8,128)} %pad_maximum_fusion.3) | data formatting | bytes 20480 | tf_op jit(solution)/shard_map/concatenate | solution.py:66
  11.9 0.0 copy-start.2
  11.9 5.1 %collective-permute-done = bf16[80,3072]{1,0:T(8,128)(2,1)} collective-permute-done((bf16[80,3072]{1,0:T(8,128)(2,1)}, bf16[80,3072]{1,0:T(8,128)(2,1)}, u32[]{:S(2)}, u32[]{:S(2)}) %collective-permute-start) | collective-permute-done | bytes 491552 | tf_op jit(solution)/shard_map/ppermute | solution.py:22
  17.0 8.9 %collective-permute-done.1 = bf16[80,3072]{1,0:T(8,128)(2,1)S(1)} collective-permute-done((bf16[80,3072]{1,0:T(8,128)(2,1)}, bf16[80,3072]{1,0:T(8,128)(2,1)S(1)}, u32[]{:S(2)}, u32[]{:S(2)}) %collective-permute-start.1) | collective-permute-done | bytes 491552 | tf_op jit(solution)/shard_map/ppermute | solution.py:22
  26.0 1.1 %pad_maximum_fusion = bf16[240,3072]{1,0:T(8,128)(2,1)S(1)} fusion(bf16[80,3072]{1,0:T(8,128)(2,1)S(1)} %collective-permute-done.1, bf16[80,3072]{1,0:T(8,128)(2,1)} %collective-permute-done, bf16[80,1024]{1,0:T(8,128)(2,1)S(1)} %get-tuple-element.10, bf16[80,1024]{1,0:T(8,128)(2,1)S(1)} %get-tuple-element.9, bf16[80,1024]{1,0:T(8,128)(2,1)S(1)} %get-tuple-element.8), kind=kLoop, calls=%fused_computation.4 | loop fusion | flops 7372800 | bytes 2949120 | tf_op jit(solution)/shard_map/concatenate | solution.py:80
  27.1 0.1 collective-permute-start.4
  27.2 7.2 %collective-permute-start.5 = (bf16[80,3072]{1,0:T(8,128)(2,1)}, bf16[80,3072]{1,0:T(8,128)(2,1)S(1)}, u32[]{:S(2)}, u32[]{:S(2)}) collective-permute-start(bf16[80,3072]{1,0:T(8,128)(2,1)} %collective-permute-done), channel_id=1, source_target_pairs={{0,254},{1,255},{2,0},{3,1},{4,2},{5,3},{6,4},{7,5},{8,6},{9,7},{1... | collective-permute-start | bytes 1474568 | tf_op jit(solution)/shard_map/ppermute | solution.py:22
  34.4 0.0 collective-permute-start.6
  34.4 0.0 copy-done.2
  34.4 1.2 %select_reduce_fusion = f32[512,160]{0,1:T(8,128)S(1)} fusion(f32[160,16]{1,0:T(8,128)S(1)} %copy-done.2, s32[512]{0:T(512)S(1)} %broadcast_add_fusion, s32[160,16]{1,0:T(8,128)S(1)} %copy.13), kind=kLoop, calls=%fused_computation | loop fusion | flops 3850240 | bytes 350208 | tf_op jit(solution)/shard_map/reduce_sum | solution.py:78
  35.6 1.4 %convolution_add_fusion.1 = f32[3072,80]{0,1:T(8,128)S(1)} fusion(f32[3072,80]{0,1:T(8,128)S(1)} %fusion.30, bf16[80,3072]{1,0:T(8,128)(2,1)} %collective-permute-done, bf16[80,720]{1,0:T(8,128)(2,1)S(1)} %convert_element_type.14), kind=kOutput, calls=%fused_computation.2 | convolution fusion | flops 39567360 | bytes 2478080 | tf_op jit(solution)/shard_map/dot_general | solution.py:63
  37.0 0.0 copy-start.4
  37.0 0.0 copy-start.5
  37.0 0.0 copy-start.6
  37.0 8.8 %collective-permute-done.5 = bf16[80,3072]{1,0:T(8,128)(2,1)S(1)} collective-permute-done((bf16[80,3072]{1,0:T(8,128)(2,1)}, bf16[80,3072]{1,0:T(8,128)(2,1)S(1)}, u32[]{:S(2)}, u32[]{:S(2)}) %collective-permute-start.5) | collective-permute-done | bytes 491552 | tf_op jit(solution)/shard_map/ppermute | solution.py:22
  45.8 1.9 %collective-permute-done.6 = bf16[80,3072]{1,0:T(8,128)(2,1)S(1)} collective-permute-done((bf16[80,3072]{1,0:T(8,128)(2,1)S(1)}, bf16[80,3072]{1,0:T(8,128)(2,1)S(1)}, u32[]{:S(2)}, u32[]{:S(2)}) %collective-permute-start.6) | collective-permute-done | bytes 491552 | tf_op jit(solution)/shard_map/ppermute | solution.py:22
  47.7 0.1 broadcast_select_fusion
  47.7 0.1 collective-permute-start.7
  47.8 0.3 fusion
  48.2 0.0 collective-permute-done.4
  48.2 0.4 fusion.17
  48.6 1.1 %collective-permute-done.7 = bf16[80,3072]{1,0:T(8,128)(2,1)S(1)} collective-permute-done((bf16[80,3072]{1,0:T(8,128)(2,1)S(1)}, bf16[80,3072]{1,0:T(8,128)(2,1)S(1)}, u32[]{:S(2)}, u32[]{:S(2)}) %collective-permute-start.7) | collective-permute-done | bytes 491552 | tf_op jit(solution)/shard_map/ppermute | solution.py:27
  49.7 0.0 copy-done.4
  49.7 0.0 copy-done.5
  49.7 0.0 copy-done.6
  49.7 0.0 copy-start
  49.7 0.5 fusion.9
  50.2 0.2 subtract_convert_fusion.1
  50.5 1.4 %copy-done = bf16[2048,1024]{1,0:T(8,128)(2,1)S(1)} copy-done((bf16[2048,1024]{1,0:T(8,128)(2,1)S(1)}, bf16[2048,1024]{1,0:T(8,128)(2,1)}, u32[]{:S(2)}) %copy-start) | copy-done | bytes 4194328
  51.9 0.0 copy-start.1
  51.9 0.9 fusion.36
  52.8 0.2 collective-permute-start.8
  53.0 1.5 %collective-permute-done.8 = f32[80,1024]{1,0:T(8,128)S(1)} collective-permute-done((f32[80,1024]{1,0:T(8,128)S(1)}, f32[80,1024]{1,0:T(8,128)S(1)}, u32[]{:S(2)}, u32[]{:S(2)}) %collective-permute-start.8) | collective-permute-done | bytes 327712 | tf_op jit(solution)/shard_map/ppermute | solution.py:27
  54.5 1.0 fusion.13
  55.5 0.0 copy-done.1
  55.5 33.9 %all_to_all.10 = f32[8,64,1024]{2,1,0:T(8,128)S(1)} all-to-all(f32[8,64,1024]{2,1,0:T(8,128)S(1)} %bitcast.9), channel_id=1, replica_groups=mesh['y'=4,'z'=4,'x'=8,'c'=2] {'x'}, dimensions={0} | all-to-all | bytes 4194304 | tf_op jit(solution)/shard_map/all_to_all | solution.py:99
  89.4 0.1 reduce_sum.28
  89.6 0.1 reshape.14
  89.6 14.3 %all_to_all.11 = f32[16,4,1024]{2,1,0:T(4,128)S(1)} all-to-all(f32[16,4,1024]{2,1,0:T(4,128)S(1)} %reshape.14), channel_id=1, replica_groups=mesh['y'=4,'z'=4,'x'=8,'c'=2] {'z','y'}, dimensions={0} | all-to-all | bytes 524288 | tf_op jit(solution)/shard_map/all_to_all | solution.py:99
  103.9 0.7 reduce_sum.29
  (3 shorter events, 0.0 us)
Async XLA Ops:
  0.6 5.4 %copy-start.7 = (s32[80,16]{0,1:T(8,128)S(1)}, s32[80,16]{0,1:T(8,128)}, u32[]{:S(2)}) copy-start(s32[80,16]{0,1:T(8,128)} %param.10) | copy-start | bytes 15364
  0.6 5.4 %copy-start.8 = (f32[80,16]{0,1:T(8,128)S(1)}, f32[80,16]{0,1:T(8,128)}, u32[]{:S(2)}) copy-start(f32[80,16]{0,1:T(8,128)} %param.11) | copy-start | bytes 15364
  0.7 5.9 %copy-start.3 = (s32[80,720]{1,0:T(8,128)S(1)}, s32[80,720]{1,0:T(8,128)}, u32[]{:S(2)}) copy-start(s32[80,720]{1,0:T(8,128)} %param.9) | copy-start | bytes 691204
  1.7 5.8 %copy-start.9 = (s32[512]{0:T(512)S(1)}, s32[512]{0:T(512)}, u32[]{:S(2)}) copy-start(s32[512]{0:T(512)} %constant.47.clone) | copy-start | bytes 6148
  3.7 13.3 %collective-permute-start = (bf16[80,3072]{1,0:T(8,128)(2,1)}, bf16[80,3072]{1,0:T(8,128)(2,1)}, u32[]{:S(2)}, u32[]{:S(2)}) collective-permute-start(bf16[80,3072]{1,0:T(8,128)(2,1)} %pad_maximum_fusion.1), channel_id=1, source_target_pairs={{0,254},{1,255},{2,0},{3,1},{4,2},{5,3},{6,4},{7,5},{8,6},{9,7},{1... | collective-permute-start | bytes 1474568 | tf_op jit(solution)/shard_map/ppermute | solution.py:22
  6.0 20.0 %collective-permute-start.1 = (bf16[80,3072]{1,0:T(8,128)(2,1)}, bf16[80,3072]{1,0:T(8,128)(2,1)S(1)}, u32[]{:S(2)}, u32[]{:S(2)}) collective-permute-start(bf16[80,3072]{1,0:T(8,128)(2,1)} %pad_maximum_fusion.1), channel_id=1, source_target_pairs={{0,2},{1,3},{2,4},{3,5},{4,6},{5,7},{6,8},{7,9},{8,10},{9,11},{10,... | collective-permute-start | bytes 1474568 | tf_op jit(solution)/shard_map/ppermute | solution.py:22
  6.0 1.6 %collective-permute-start.2 = (s32[80,16]{0,1:T(8,128)S(1)}, s32[80,16]{0,1:T(8,128)S(1)}, u32[]{:S(2)}, u32[]{:S(2)}) collective-permute-start(s32[80,16]{0,1:T(8,128)S(1)} %copy-done.7), channel_id=1, source_target_pairs={{0,1},{1,0},{2,3},{3,2},{4,5},{5,4},{6,7},{7,6},{8,9},{9,8},{10,11... | collective-permute-start | bytes 15368 | tf_op jit(solution)/shard_map/ppermute | solution.py:27
  6.0 3.1 %collective-permute-start.3 = (f32[80,16]{0,1:T(8,128)S(1)}, f32[80,16]{0,1:T(8,128)}, u32[]{:S(2)}, u32[]{:S(2)}) collective-permute-start(f32[80,16]{0,1:T(8,128)S(1)} %copy-done.8), channel_id=1, source_target_pairs={{0,1},{1,0},{2,3},{3,2},{4,5},{5,4},{6,7},{7,6},{8,9},{9,8},{10,11... | collective-permute-start | bytes 15368 | tf_op jit(solution)/shard_map/ppermute | solution.py:27
  11.9 22.5 %copy-start.2 = (f32[160,16]{1,0:T(8,128)S(1)}, f32[160,16]{1,0:T(8,128)}, u32[]{:S(2)}) copy-start(f32[160,16]{1,0:T(8,128)} %copy.14) | copy-start | bytes 30724
  27.1 21.1 %collective-permute-start.4 = (bf16[240,3072]{1,0:T(8,128)(2,1)S(1)}, bf16[240,3072]{1,0:T(8,128)(2,1)S(1)}, u32[]{:S(2)}, u32[]{:S(2)}) collective-permute-start(bf16[240,3072]{1,0:T(8,128)(2,1)S(1)} %pad_maximum_fusion), channel_id=1, source_target_pairs={{0,1},{1,0},{2,3},{3,2},{4,5},{5,4},{6,7},{7,6},{8,9},{9,8},{10,11... | collective-permute-start | bytes 4423688 | tf_op jit(solution)/shard_map/ppermute | solution.py:27
  27.2 18.6 %collective-permute-start.5 = (bf16[80,3072]{1,0:T(8,128)(2,1)}, bf16[80,3072]{1,0:T(8,128)(2,1)S(1)}, u32[]{:S(2)}, u32[]{:S(2)}) collective-permute-start(bf16[80,3072]{1,0:T(8,128)(2,1)} %collective-permute-done), channel_id=1, source_target_pairs={{0,254},{1,255},{2,0},{3,1},{4,2},{5,3},{6,4},{7,5},{8,6},{9,7},{1... | collective-permute-start | bytes 1474568 | tf_op jit(solution)/shard_map/ppermute | solution.py:22
  34.4 13.3 %collective-permute-start.6 = (bf16[80,3072]{1,0:T(8,128)(2,1)S(1)}, bf16[80,3072]{1,0:T(8,128)(2,1)S(1)}, u32[]{:S(2)}, u32[]{:S(2)}) collective-permute-start(bf16[80,3072]{1,0:T(8,128)(2,1)S(1)} %collective-permute-done.1), channel_id=1, source_target_pairs={{0,2},{1,3},{2,4},{3,5},{4,6},{5,7},{6,8},{7,9},{8,10},{9,11},{10,... | collective-permute-start | bytes 1474568 | tf_op jit(solution)/shard_map/ppermute | solution.py:22
  37.0 12.7 %copy-start.4 = (bf16[80,80]{1,0:T(8,128)(2,1)S(1)}, bf16[80,80]{1,0:T(8,128)(2,1)}, u32[]{:S(2)}) copy-start(bf16[80,80]{1,0:T(8,128)(2,1)} %get-tuple-element.11) | copy-start | bytes 38404
  37.0 12.7 %copy-start.5 = (bf16[80,80]{1,0:T(8,128)(2,1)S(1)}, bf16[80,80]{1,0:T(8,128)(2,1)}, u32[]{:S(2)}) copy-start(bf16[80,80]{1,0:T(8,128)(2,1)} %get-tuple-element.12) | copy-start | bytes 38404
  37.0 12.7 %copy-start.6 = (bf16[80,80]{1,0:T(8,128)(2,1)S(1)}, bf16[80,80]{1,0:T(8,128)(2,1)}, u32[]{:S(2)}) copy-start(bf16[80,80]{1,0:T(8,128)(2,1)} %get-tuple-element.16) | copy-start | bytes 38404
  47.7 2.0 %collective-permute-start.7 = (bf16[80,3072]{1,0:T(8,128)(2,1)S(1)}, bf16[80,3072]{1,0:T(8,128)(2,1)S(1)}, u32[]{:S(2)}, u32[]{:S(2)}) collective-permute-start(bf16[80,3072]{1,0:T(8,128)(2,1)S(1)} %broadcast_select_fusion), channel_id=1, source_target_pairs={{0,1},{1,0},{2,3},{3,2},{4,5},{5,4},{6,7},{7,6},{8,9},{9,8},{10,11... | collective-permute-start | bytes 1474568 | tf_op jit(solution)/shard_map/ppermute | solution.py:27
  49.7 2.2 %copy-start = (bf16[2048,1024]{1,0:T(8,128)(2,1)S(1)}, bf16[2048,1024]{1,0:T(8,128)(2,1)}, u32[]{:S(2)}) copy-start(bf16[2048,1024]{1,0:T(8,128)(2,1)} %param.12) | copy-start | bytes 12582916
  51.9 3.6 %copy-start.1 = (bf16[80,2048]{1,0:T(8,128)(2,1)}, bf16[80,2048]{1,0:T(8,128)(2,1)S(1)}, u32[]{:S(2)}) copy-start(bf16[80,2048]{1,0:T(8,128)(2,1)S(1)} %pad_maximum_fusion.2) | copy-start | bytes 983044
  52.8 1.7 %collective-permute-start.8 = (f32[80,1024]{1,0:T(8,128)S(1)}, f32[80,1024]{1,0:T(8,128)S(1)}, u32[]{:S(2)}, u32[]{:S(2)}) collective-permute-start(f32[80,1024]{1,0:T(8,128)S(1)} %fusion.36), channel_id=1, source_target_pairs={{0,1},{1,0},{2,3},{3,2},{4,5},{5,4},{6,7},{7,6},{8,9},{9,8},{10,11... | collective-permute-start | bytes 983048 | tf_op jit(solution)/shard_map/ppermute | solution.py:27

commit v12 on v11

--- a/solution.py
+++ b/solution.py
@@ -93,10 +93,14 @@
     response = jnp.dot(adjoint, tile_green, preferred_element_type=jnp.float32)
     responses = jnp.concatenate([response, swap(response, count)], axis=0)
     part = jnp.dot(tile_map, responses, precision=lax.Precision.HIGH)
+    width = part.shape[1]
     for group in STAGES:
         ways = int(np.prod([SIZES[SUB.index(a)] for a in group]))
-        part = part.reshape(ways, -1, part.shape[1])
+        rows = part.shape[0] // ways
+        fold = 8 // rows if rows < 8 else 1
+        part = part.reshape(ways, rows * fold, width // fold)
         part = jnp.sum(lax.all_to_all(part, group, 0, 0, tiled=False), axis=0)
+        part = part.reshape(rows, width)
     return (adjoint, part)
 
 

time: 106 us -> 106 us (level)
  no operation moved by 1% of the time
where the time goes in v12:
time: 106 us; the launch traced here: 105 us
  blocking collectives  48.2 us (45%)
  waiting for transfers between devices  27.3 us (26%)
  starting transfers between devices  10.4 us (10%)
  other arithmetic  8.63 us (8%)
  matrix products  4.82 us (5%)
  local copies, waits for them, and re-layouts  4.39 us (4%)
    all_to_all x2, blocking collectives, body(): part = jnp.sum(lax.all_to_all(part, group, 0, 0, tiled=False), axis=0)  48.2 us
    ppermute x4, waiting for transfers between devices, shifted(): return lax.ppermute(value, SUB, pairs)  24.7 us
    ppermute x4, starting transfers between devices, shifted(): return lax.ppermute(value, SUB, pairs)  9.46 us
    dot_general x4, matrix products, add(): return total + jnp.dot(columns, moving, preferred_element_type=jnp.float32)  2.59 us
    ppermute x5, waiting for transfers between devices, swap(): return lax.ppermute(value, SUB, pairs)  2.58 us
  transfers between devices with their start and end apart: 9, of which 6 were waited for; matrix products, arithmetic and copies ran while one was open for 8% of the time, Pallas kernels for 0%

profile of v12, /device:TPU:2, one launch (start us, length us, event | category | flops | bytes accessed | tf_op | source)
XLA Modules:
  0.0 104.5 jit_solution(6306031850441122557)
XLA Ops:
  0.6 0.0 copy-start.7
  0.6 0.0 copy-start.8
  0.7 0.0 copy-start.3
  0.7 1.1 %convert_element_type.12 = f32[80,2048]{1,0:T(8,128)S(1)} convert(bf16[80,2048]{1,0:T(8,128)(2,1)} %param.7) | non-fusion elementwise | flops 163840 | bytes 983040 | tf_op jit(solution)/shard_map/convert_element_type | solution.py:41
  1.7 0.0 copy-start.9
  1.7 1.0 convert_element_type.13
  2.8 0.1 add_convert_fusion.1
  2.9 0.8 pad_maximum_fusion.1
  3.7 2.2 %collective-permute-start = (bf16[80,3072]{1,0:T(8,128)(2,1)}, bf16[80,3072]{1,0:T(8,128)(2,1)}, u32[]{:S(2)}, u32[]{:S(2)}) collective-permute-start(bf16[80,3072]{1,0:T(8,128)(2,1)} %pad_maximum_fusion.1), channel_id=1, source_target_pairs={{0,254},{1,255},{2,0},{3,1},{4,2},{5,3},{6,4},{7,5},{8,6},{9,7},{1... | collective-permute-start | bytes 1474568 | tf_op jit(solution)/shard_map/ppermute | solution.py:22
  6.0 0.0 collective-permute-start.1
  6.0 0.0 copy-done.7
  6.0 0.0 collective-permute-start.2
  6.0 0.0 copy-done.8
  6.0 0.5 collective-permute-start.3
  6.5 0.0 copy-done.3
  6.5 0.3 fusion.30
  6.9 0.7 fusion.35
  7.6 0.0 copy-done.9
  7.6 0.0 collective-permute-done.2
  7.6 0.7 pad_add_fusion
  8.2 0.8 copy.11
  9.1 0.0 collective-permute-done.3
  9.1 1.4 %pad_maximum_fusion.3 = f32[160,16]{0,1:T(8,128)} fusion(f32[80,16]{0,1:T(8,128)} %collective-permute-done.3, f32[80,16]{0,1:T(8,128)S(1)} %copy-done.8), kind=kLoop, calls=%fused_computation.45 | loop fusion | flops 2560 | bytes 20480 | tf_op jit(solution)/shard_map/concatenate | solution.py:66
  10.4 1.5 %copy.12 = f32[160,16]{1,0:T(8,128)} copy(f32[160,16]{0,1:T(8,128)} %pad_maximum_fusion.3) | data formatting | bytes 20480 | tf_op jit(solution)/shard_map/concatenate | solution.py:66
  11.9 0.0 copy-start.2
  11.9 5.1 %collective-permute-done = bf16[80,3072]{1,0:T(8,128)(2,1)} collective-permute-done((bf16[80,3072]{1,0:T(8,128)(2,1)}, bf16[80,3072]{1,0:T(8,128)(2,1)}, u32[]{:S(2)}, u32[]{:S(2)}) %collective-permute-start) | collective-permute-done | bytes 491552 | tf_op jit(solution)/shard_map/ppermute | solution.py:22
  17.0 8.9 %collective-permute-done.1 = bf16[80,3072]{1,0:T(8,128)(2,1)S(1)} collective-permute-done((bf16[80,3072]{1,0:T(8,128)(2,1)}, bf16[80,3072]{1,0:T(8,128)(2,1)S(1)}, u32[]{:S(2)}, u32[]{:S(2)}) %collective-permute-start.1) | collective-permute-done | bytes 491552 | tf_op jit(solution)/shard_map/ppermute | solution.py:22
  26.0 1.1 %pad_maximum_fusion = bf16[240,3072]{1,0:T(8,128)(2,1)S(1)} fusion(bf16[80,3072]{1,0:T(8,128)(2,1)S(1)} %collective-permute-done.1, bf16[80,3072]{1,0:T(8,128)(2,1)} %collective-permute-done, bf16[80,1024]{1,0:T(8,128)(2,1)S(1)} %get-tuple-element.10, bf16[80,1024]{1,0:T(8,128)(2,1)S(1)} %get-tuple-element.9, bf16[80,1024]{1,0:T(8,128)(2,1)S(1)} %get-tuple-element.8), kind=kLoop, calls=%fused_computation.4 | loop fusion | flops 7372800 | bytes 2949120 | tf_op jit(solution)/shard_map/concatenate | solution.py:80
  27.1 0.1 collective-permute-start.4
  27.2 7.2 %collective-permute-start.5 = (bf16[80,3072]{1,0:T(8,128)(2,1)}, bf16[80,3072]{1,0:T(8,128)(2,1)S(1)}, u32[]{:S(2)}, u32[]{:S(2)}) collective-permute-start(bf16[80,3072]{1,0:T(8,128)(2,1)} %collective-permute-done), channel_id=1, source_target_pairs={{0,254},{1,255},{2,0},{3,1},{4,2},{5,3},{6,4},{7,5},{8,6},{9,7},{1... | collective-permute-start | bytes 1474568 | tf_op jit(solution)/shard_map/ppermute | solution.py:22
  34.4 0.0 collective-permute-start.6
  34.4 0.0 copy-done.2
  34.4 1.2 %select_reduce_fusion = f32[512,160]{0,1:T(8,128)S(1)} fusion(f32[160,16]{1,0:T(8,128)S(1)} %copy-done.2, s32[512]{0:T(512)S(1)} %broadcast_add_fusion, s32[160,16]{1,0:T(8,128)S(1)} %copy.11), kind=kLoop, calls=%fused_computation | loop fusion | flops 3850240 | bytes 350208 | tf_op jit(solution)/shard_map/reduce_sum | solution.py:78
  35.6 1.4 %convolution_add_fusion.1 = f32[3072,80]{0,1:T(8,128)S(1)} fusion(f32[3072,80]{0,1:T(8,128)S(1)} %fusion.30, bf16[80,3072]{1,0:T(8,128)(2,1)} %collective-permute-done, bf16[80,720]{1,0:T(8,128)(2,1)S(1)} %convert_element_type.14), kind=kOutput, calls=%fused_computation.2 | convolution fusion | flops 39567360 | bytes 2478080 | tf_op jit(solution)/shard_map/dot_general | solution.py:63
  37.0 0.0 copy-start.4
  37.0 0.0 copy-start.5
  37.0 0.0 copy-start.6
  37.0 8.8 %collective-permute-done.5 = bf16[80,3072]{1,0:T(8,128)(2,1)S(1)} collective-permute-done((bf16[80,3072]{1,0:T(8,128)(2,1)}, bf16[80,3072]{1,0:T(8,128)(2,1)S(1)}, u32[]{:S(2)}, u32[]{:S(2)}) %collective-permute-start.5) | collective-permute-done | bytes 491552 | tf_op jit(solution)/shard_map/ppermute | solution.py:22
  45.8 1.9 %collective-permute-done.6 = bf16[80,3072]{1,0:T(8,128)(2,1)S(1)} collective-permute-done((bf16[80,3072]{1,0:T(8,128)(2,1)S(1)}, bf16[80,3072]{1,0:T(8,128)(2,1)S(1)}, u32[]{:S(2)}, u32[]{:S(2)}) %collective-permute-start.6) | collective-permute-done | bytes 491552 | tf_op jit(solution)/shard_map/ppermute | solution.py:22
  47.7 0.1 broadcast_select_fusion
  47.7 0.1 collective-permute-start.7
  47.8 0.3 fusion
  48.2 0.0 collective-permute-done.4
  48.2 0.4 fusion.17
  48.6 1.1 %collective-permute-done.7 = bf16[80,3072]{1,0:T(8,128)(2,1)S(1)} collective-permute-done((bf16[80,3072]{1,0:T(8,128)(2,1)S(1)}, bf16[80,3072]{1,0:T(8,128)(2,1)S(1)}, u32[]{:S(2)}, u32[]{:S(2)}) %collective-permute-start.7) | collective-permute-done | bytes 491552 | tf_op jit(solution)/shard_map/ppermute | solution.py:27
  49.7 0.0 copy-done.4
  49.7 0.0 copy-done.5
  49.7 0.0 copy-done.6
  49.7 0.0 copy-start
  49.7 0.5 fusion.9
  50.2 0.2 subtract_convert_fusion.1
  50.5 1.4 %copy-done = bf16[2048,1024]{1,0:T(8,128)(2,1)S(1)} copy-done((bf16[2048,1024]{1,0:T(8,128)(2,1)S(1)}, bf16[2048,1024]{1,0:T(8,128)(2,1)}, u32[]{:S(2)}) %copy-start) | copy-done | bytes 4194328
  51.9 0.0 copy-start.1
  51.9 0.9 fusion.36
  52.8 0.2 collective-permute-start.8
  53.0 1.5 %collective-permute-done.8 = f32[80,1024]{1,0:T(8,128)S(1)} collective-permute-done((f32[80,1024]{1,0:T(8,128)S(1)}, f32[80,1024]{1,0:T(8,128)S(1)}, u32[]{:S(2)}, u32[]{:S(2)}) %collective-permute-start.8) | collective-permute-done | bytes 327712 | tf_op jit(solution)/shard_map/ppermute | solution.py:27
  54.5 1.0 fusion.13
  55.5 0.0 copy-done.1
  55.5 33.9 %all_to_all.10 = f32[8,64,1024]{2,1,0:T(8,128)S(1)} all-to-all(f32[8,64,1024]{2,1,0:T(8,128)S(1)} %bitcast.9), channel_id=1, replica_groups=mesh['y'=4,'z'=4,'x'=8,'c'=2] {'x'}, dimensions={0} | all-to-all | bytes 4194304 | tf_op jit(solution)/shard_map/all_to_all | solution.py:102
  89.4 0.1 reduce_sum.28
  89.6 14.3 %all_to_all.11 = f32[16,8,512]{2,1,0:T(8,128)S(1)} all-to-all(f32[16,8,512]{2,1,0:T(8,128)S(1)} %reshape.17), channel_id=1, replica_groups=mesh['y'=4,'z'=4,'x'=8,'c'=2] {'z','y'}, dimensions={0} | all-to-all | bytes 524288 | tf_op jit(solution)/shard_map/all_to_all | solution.py:102
  103.9 0.6 reshape.18
  (5 shorter events, 0.1 us)
Async XLA Ops:
  0.6 5.4 %copy-start.7 = (s32[80,16]{0,1:T(8,128)S(1)}, s32[80,16]{0,1:T(8,128)}, u32[]{:S(2)}) copy-start(s32[80,16]{0,1:T(8,128)} %param.10) | copy-start | bytes 15364
  0.6 5.4 %copy-start.8 = (f32[80,16]{0,1:T(8,128)S(1)}, f32[80,16]{0,1:T(8,128)}, u32[]{:S(2)}) copy-start(f32[80,16]{0,1:T(8,128)} %param.11) | copy-start | bytes 15364
  0.7 5.9 %copy-start.3 = (s32[80,720]{1,0:T(8,128)S(1)}, s32[80,720]{1,0:T(8,128)}, u32[]{:S(2)}) copy-start(s32[80,720]{1,0:T(8,128)} %param.9) | copy-start | bytes 691204
  1.7 5.8 %copy-start.9 = (s32[512]{0:T(512)S(1)}, s32[512]{0:T(512)}, u32[]{:S(2)}) copy-start(s32[512]{0:T(512)} %constant.47.clone) | copy-start | bytes 6148
  3.7 13.3 %collective-permute-start = (bf16[80,3072]{1,0:T(8,128)(2,1)}, bf16[80,3072]{1,0:T(8,128)(2,1)}, u32[]{:S(2)}, u32[]{:S(2)}) collective-permute-start(bf16[80,3072]{1,0:T(8,128)(2,1)} %pad_maximum_fusion.1), channel_id=1, source_target_pairs={{0,254},{1,255},{2,0},{3,1},{4,2},{5,3},{6,4},{7,5},{8,6},{9,7},{1... | collective-permute-start | bytes 1474568 | tf_op jit(solution)/shard_map/ppermute | solution.py:22
  6.0 20.0 %collective-permute-start.1 = (bf16[80,3072]{1,0:T(8,128)(2,1)}, bf16[80,3072]{1,0:T(8,128)(2,1)S(1)}, u32[]{:S(2)}, u32[]{:S(2)}) collective-permute-start(bf16[80,3072]{1,0:T(8,128)(2,1)} %pad_maximum_fusion.1), channel_id=1, source_target_pairs={{0,2},{1,3},{2,4},{3,5},{4,6},{5,7},{6,8},{7,9},{8,10},{9,11},{10,... | collective-permute-start | bytes 1474568 | tf_op jit(solution)/shard_map/ppermute | solution.py:22
  6.0 1.6 %collective-permute-start.2 = (s32[80,16]{0,1:T(8,128)S(1)}, s32[80,16]{0,1:T(8,128)S(1)}, u32[]{:S(2)}, u32[]{:S(2)}) collective-permute-start(s32[80,16]{0,1:T(8,128)S(1)} %copy-done.7), channel_id=1, source_target_pairs={{0,1},{1,0},{2,3},{3,2},{4,5},{5,4},{6,7},{7,6},{8,9},{9,8},{10,11... | collective-permute-start | bytes 15368 | tf_op jit(solution)/shard_map/ppermute | solution.py:27
  6.0 3.1 %collective-permute-start.3 = (f32[80,16]{0,1:T(8,128)S(1)}, f32[80,16]{0,1:T(8,128)}, u32[]{:S(2)}, u32[]{:S(2)}) collective-permute-start(f32[80,16]{0,1:T(8,128)S(1)} %copy-done.8), channel_id=1, source_target_pairs={{0,1},{1,0},{2,3},{3,2},{4,5},{5,4},{6,7},{7,6},{8,9},{9,8},{10,11... | collective-permute-start | bytes 15368 | tf_op jit(solution)/shard_map/ppermute | solution.py:27
  11.9 22.5 %copy-start.2 = (f32[160,16]{1,0:T(8,128)S(1)}, f32[160,16]{1,0:T(8,128)}, u32[]{:S(2)}) copy-start(f32[160,16]{1,0:T(8,128)} %copy.12) | copy-start | bytes 30724
  27.1 21.1 %collective-permute-start.4 = (bf16[240,3072]{1,0:T(8,128)(2,1)S(1)}, bf16[240,3072]{1,0:T(8,128)(2,1)S(1)}, u32[]{:S(2)}, u32[]{:S(2)}) collective-permute-start(bf16[240,3072]{1,0:T(8,128)(2,1)S(1)} %pad_maximum_fusion), channel_id=1, source_target_pairs={{0,1},{1,0},{2,3},{3,2},{4,5},{5,4},{6,7},{7,6},{8,9},{9,8},{10,11... | collective-permute-start | bytes 4423688 | tf_op jit(solution)/shard_map/ppermute | solution.py:27
  27.2 18.6 %collective-permute-start.5 = (bf16[80,3072]{1,0:T(8,128)(2,1)}, bf16[80,3072]{1,0:T(8,128)(2,1)S(1)}, u32[]{:S(2)}, u32[]{:S(2)}) collective-permute-start(bf16[80,3072]{1,0:T(8,128)(2,1)} %collective-permute-done), channel_id=1, source_target_pairs={{0,254},{1,255},{2,0},{3,1},{4,2},{5,3},{6,4},{7,5},{8,6},{9,7},{1... | collective-permute-start | bytes 1474568 | tf_op jit(solution)/shard_map/ppermute | solution.py:22
  34.4 13.3 %collective-permute-start.6 = (bf16[80,3072]{1,0:T(8,128)(2,1)S(1)}, bf16[80,3072]{1,0:T(8,128)(2,1)S(1)}, u32[]{:S(2)}, u32[]{:S(2)}) collective-permute-start(bf16[80,3072]{1,0:T(8,128)(2,1)S(1)} %collective-permute-done.1), channel_id=1, source_target_pairs={{0,2},{1,3},{2,4},{3,5},{4,6},{5,7},{6,8},{7,9},{8,10},{9,11},{10,... | collective-permute-start | bytes 1474568 | tf_op jit(solution)/shard_map/ppermute | solution.py:22
  37.0 12.7 %copy-start.4 = (bf16[80,80]{1,0:T(8,128)(2,1)S(1)}, bf16[80,80]{1,0:T(8,128)(2,1)}, u32[]{:S(2)}) copy-start(bf16[80,80]{1,0:T(8,128)(2,1)} %get-tuple-element.11) | copy-start | bytes 38404
  37.0 12.7 %copy-start.5 = (bf16[80,80]{1,0:T(8,128)(2,1)S(1)}, bf16[80,80]{1,0:T(8,128)(2,1)}, u32[]{:S(2)}) copy-start(bf16[80,80]{1,0:T(8,128)(2,1)} %get-tuple-element.12) | copy-start | bytes 38404
  37.0 12.7 %copy-start.6 = (bf16[80,80]{1,0:T(8,128)(2,1)S(1)}, bf16[80,80]{1,0:T(8,128)(2,1)}, u32[]{:S(2)}) copy-start(bf16[80,80]{1,0:T(8,128)(2,1)} %get-tuple-element.16) | copy-start | bytes 38404
  47.7 2.0 %collective-permute-start.7 = (bf16[80,3072]{1,0:T(8,128)(2,1)S(1)}, bf16[80,3072]{1,0:T(8,128)(2,1)S(1)}, u32[]{:S(2)}, u32[]{:S(2)}) collective-permute-start(bf16[80,3072]{1,0:T(8,128)(2,1)S(1)} %broadcast_select_fusion), channel_id=1, source_target_pairs={{0,1},{1,0},{2,3},{3,2},{4,5},{5,4},{6,7},{7,6},{8,9},{9,8},{10,11... | collective-permute-start | bytes 1474568 | tf_op jit(solution)/shard_map/ppermute | solution.py:27
  49.7 2.2 %copy-start = (bf16[2048,1024]{1,0:T(8,128)(2,1)S(1)}, bf16[2048,1024]{1,0:T(8,128)(2,1)}, u32[]{:S(2)}) copy-start(bf16[2048,1024]{1,0:T(8,128)(2,1)} %param.12) | copy-start | bytes 12582916
  51.9 3.6 %copy-start.1 = (bf16[80,2048]{1,0:T(8,128)(2,1)}, bf16[80,2048]{1,0:T(8,128)(2,1)S(1)}, u32[]{:S(2)}) copy-start(bf16[80,2048]{1,0:T(8,128)(2,1)S(1)} %pad_maximum_fusion.2) | copy-start | bytes 983044
  52.8 1.7 %collective-permute-start.8 = (f32[80,1024]{1,0:T(8,128)S(1)}, f32[80,1024]{1,0:T(8,128)S(1)}, u32[]{:S(2)}, u32[]{:S(2)}) collective-permute-start(f32[80,1024]{1,0:T(8,128)S(1)} %fusion.36), channel_id=1, source_target_pairs={{0,1},{1,0},{2,3},{3,2},{4,5},{5,4},{6,7},{7,6},{8,9},{9,8},{10,11... | collective-permute-start | bytes 983048 | tf_op jit(solution)/shard_map/ppermute | solution.py:27

commit v13 on v11

--- a/solution.py
+++ b/solution.py
@@ -62,8 +62,9 @@
     def add(total, columns, moving):
         return total + jnp.dot(columns, moving, preferred_element_type=jnp.float32)
 
-    lists = jnp.concatenate([tile_lists, swap(tile_lists, count)], axis=0)
-    weights = jnp.concatenate([tile_weights, swap(tile_weights, count)], axis=0)
+    listed = jnp.concatenate([tile_lists.astype(jnp.float32), tile_weights], axis=1)
+    listed = jnp.concatenate([listed, swap(listed, count)], axis=0)
+    lists, weights = (listed[:, : tile_lists.shape[1]], listed[:, tile_lists.shape[1] :])
     ahead = shifted(both, -2, count)
     behind = shifted(both, 2, count)
     ahead2 = shifted(ahead, -2, count)
@@ -74,6 +75,7 @@
     tile_ids = jnp.asarray(tile_order()[: TT * count // SIZES[-1]]) + TT * (
         lax.axis_index(SUB) % 2
     )
+    tile_ids = tile_ids.astype(jnp.float32)
     onehot = (lists[None, :, :] == tile_ids[:, None, None]).astype(jnp.float32)
     tile_map = jnp.sum(onehot * weights[None, :, :], axis=2)
     total, tile_map = lax.optimization_barrier((total, tile_map))

time: 106 us -> 106 us (level)
  other arithmetic: 9.27 us -> 7.3 us
  waiting for transfers between devices: 27.3 us -> 29 us
    slice x0 -> x3, local copies, waits for them, and re-layouts: none -> 2.88 us  [the longest x1 1.45 us: body(): listed[:, tile_lists.shape[1]:]]
    concatenate x2 -> x0, local copies, waits for them, and re-layouts: 2.27 us -> none  [the longest x1 1.45 us: body(): weights = jnp.concatenate([tile_weights, swap(tile_weights, count)], axis=0)]
    concatenate x2, other arithmetic: 2.06 us -> 0.08 us  [the longest x1 0.08 us: body(): listed = jnp.concatenate([listed, swap(listed, count)], axis=0)]
    ppermute x4, waiting for transfers between devices: 24.7 us -> 26.4 us  [shifted(): return lax.ppermute(value, SUB, pairs)]
    ppermute x5 -> x4, waiting for transfers between devices: 2.58 us -> 2.66 us  [swap(): return lax.ppermute(value, SUB, pairs)]
  transfers between devices with their start and end apart: 9 -> 8, of which waited for: 6 -> 7; matrix products, arithmetic and copies ran while one was open for 8% -> 7% of each run, Pallas kernels for 0% -> 0%
where the time goes in v13:
time: 106 us; the launch traced here: 105 us
  blocking collectives  48.2 us (45%)
  waiting for transfers between devices  29 us (27%)
  starting transfers between devices  9.96 us (9%)
  other arithmetic  7.3 us (7%)
  matrix products  4.82 us (5%)
  local copies, waits for them, and re-layouts  4.42 us (4%)
    all_to_all x2, blocking collectives, body(): part = jnp.sum(lax.all_to_all(part, group, 0, 0, tiled=False), axis=0)  48.2 us
    ppermute x4, waiting for transfers between devices, shifted(): return lax.ppermute(value, SUB, pairs)  26.4 us
    ppermute x4, starting transfers between devices, shifted(): return lax.ppermute(value, SUB, pairs)  9.46 us
    ppermute x4, waiting for transfers between devices, swap(): return lax.ppermute(value, SUB, pairs)  2.66 us
    dot_general x4, matrix products, add(): return total + jnp.dot(columns, moving, preferred_element_type=jnp.float32)  2.59 us
  transfers between devices with their start and end apart: 8, of which 7 were waited for; matrix products, arithmetic and copies ran while one was open for 7% of the time, Pallas kernels for 0%

profile of v13, /device:TPU:2, one launch (start us, length us, event | category | flops | bytes accessed | tf_op | source)
XLA Modules:
  0.0 104.6 jit_solution(505369054786123861)
XLA Ops:
  0.6 0.0 copy-start.8
  0.6 0.0 copy-start.4
  0.7 0.0 copy-start.3
  0.7 1.1 %convert_element_type.18 = f32[80,2048]{1,0:T(8,128)S(1)} convert(bf16[80,2048]{1,0:T(8,128)(2,1)} %param.7) | non-fusion elementwise | flops 163840 | bytes 983040 | tf_op jit(solution)/shard_map/convert_element_type | solution.py:41
  1.7 0.0 copy-start.9
  1.7 1.0 convert_element_type.19
  2.8 0.1 add_convert_fusion.1
  2.9 0.8 pad_maximum_fusion.1
  3.7 2.2 %collective-permute-start = (bf16[80,3072]{1,0:T(8,128)(2,1)}, bf16[80,3072]{1,0:T(8,128)(2,1)}, u32[]{:S(2)}, u32[]{:S(2)}) collective-permute-start(bf16[80,3072]{1,0:T(8,128)(2,1)} %pad_maximum_fusion.1), channel_id=1, source_target_pairs={{0,254},{1,255},{2,0},{3,1},{4,2},{5,3},{6,4},{7,5},{8,6},{9,7},{1... | collective-permute-start | bytes 1474568 | tf_op jit(solution)/shard_map/ppermute | solution.py:22
  6.0 0.0 collective-permute-start.1
  6.0 0.0 copy-done.8
  6.0 0.0 copy-done.4
  6.0 0.1 collective-permute-start.2
  6.1 0.0 copy-done.3
  6.2 0.3 fusion.30
  6.5 0.7 fusion.35
  7.2 0.0 copy-done.9
  7.2 0.1 collective-permute-done.2
  7.3 0.1 pad_maximum_fusion.3
  7.4 0.6 fusion.36
  8.0 0.8 copy.13
  8.8 1.5 %copy.14 = f32[160,16]{1,0:T(8,128)} copy(f32[160,16]{0,1:T(8,128)} %get-tuple-element.18) | data formatting | bytes 20480 | tf_op jit(solution)/shard_map/slice | solution.py:67
  10.2 0.0 copy-start.2
  10.3 6.8 %collective-permute-done = bf16[80,3072]{1,0:T(8,128)(2,1)} collective-permute-done((bf16[80,3072]{1,0:T(8,128)(2,1)}, bf16[80,3072]{1,0:T(8,128)(2,1)}, u32[]{:S(2)}, u32[]{:S(2)}) %collective-permute-start) | collective-permute-done | bytes 491552 | tf_op jit(solution)/shard_map/ppermute | solution.py:22
  17.0 8.9 %collective-permute-done.1 = bf16[80,3072]{1,0:T(8,128)(2,1)S(1)} collective-permute-done((bf16[80,3072]{1,0:T(8,128)(2,1)}, bf16[80,3072]{1,0:T(8,128)(2,1)S(1)}, u32[]{:S(2)}, u32[]{:S(2)}) %collective-permute-start.1) | collective-permute-done | bytes 491552 | tf_op jit(solution)/shard_map/ppermute | solution.py:22
  26.0 1.1 %pad_maximum_fusion = bf16[240,3072]{1,0:T(8,128)(2,1)S(1)} fusion(bf16[80,3072]{1,0:T(8,128)(2,1)S(1)} %collective-permute-done.1, bf16[80,3072]{1,0:T(8,128)(2,1)} %collective-permute-done, bf16[80,1024]{1,0:T(8,128)(2,1)S(1)} %get-tuple-element.10, bf16[80,1024]{1,0:T(8,128)(2,1)S(1)} %get-tuple-element.9, bf16[80,1024]{1,0:T(8,128)(2,1)S(1)} %get-tuple-element.8), kind=kLoop, calls=%fused_computation.4 | loop fusion | flops 7372800 | bytes 2949120 | tf_op jit(solution)/shard_map/concatenate | solution.py:82
  27.1 0.1 collective-permute-start.3
  27.2 7.2 %collective-permute-start.4 = (bf16[80,3072]{1,0:T(8,128)(2,1)}, bf16[80,3072]{1,0:T(8,128)(2,1)S(1)}, u32[]{:S(2)}, u32[]{:S(2)}) collective-permute-start(bf16[80,3072]{1,0:T(8,128)(2,1)} %collective-permute-done), channel_id=1, source_target_pairs={{0,254},{1,255},{2,0},{3,1},{4,2},{5,3},{6,4},{7,5},{8,6},{9,7},{1... | collective-permute-start | bytes 1474568 | tf_op jit(solution)/shard_map/ppermute | solution.py:22
  34.4 0.0 collective-permute-start.5
  34.4 0.0 copy-done.2
  34.4 1.2 %select_reduce_fusion = f32[512,160]{0,1:T(8,128)S(1)} fusion(f32[160,16]{1,0:T(8,128)S(1)} %copy-done.2, f32[512]{0:T(512)S(1)} %add_convert_fusion.2, f32[160,16]{1,0:T(8,128)S(1)} %copy.13), kind=kLoop, calls=%fused_computation | loop fusion | flops 3850240 | bytes 350208 | tf_op jit(solution)/shard_map/reduce_sum | solution.py:80
  35.6 1.4 %convolution_add_fusion.1 = f32[3072,80]{0,1:T(8,128)S(1)} fusion(f32[3072,80]{0,1:T(8,128)S(1)} %fusion.30, bf16[80,3072]{1,0:T(8,128)(2,1)} %collective-permute-done, bf16[80,720]{1,0:T(8,128)(2,1)S(1)} %convert_element_type.20), kind=kOutput, calls=%fused_computation.2 | convolution fusion | flops 39567360 | bytes 2478080 | tf_op jit(solution)/shard_map/dot_general | solution.py:63
  37.0 0.0 copy-start.5
  37.0 0.0 copy-start.6
  37.0 0.0 copy-start.7
  37.0 8.8 %collective-permute-done.4 = bf16[80,3072]{1,0:T(8,128)(2,1)S(1)} collective-permute-done((bf16[80,3072]{1,0:T(8,128)(2,1)}, bf16[80,3072]{1,0:T(8,128)(2,1)S(1)}, u32[]{:S(2)}, u32[]{:S(2)}) %collective-permute-start.4) | collective-permute-done | bytes 491552 | tf_op jit(solution)/shard_map/ppermute | solution.py:22
  45.8 1.9 %collective-permute-done.5 = bf16[80,3072]{1,0:T(8,128)(2,1)S(1)} collective-permute-done((bf16[80,3072]{1,0:T(8,128)(2,1)S(1)}, bf16[80,3072]{1,0:T(8,128)(2,1)S(1)}, u32[]{:S(2)}, u32[]{:S(2)}) %collective-permute-start.5) | collective-permute-done | bytes 491552 | tf_op jit(solution)/shard_map/ppermute | solution.py:22
  47.7 0.1 broadcast_select_fusion
  47.7 0.1 collective-permute-start.6
  47.8 0.3 fusion
  48.2 0.0 collective-permute-done.3
  48.2 0.4 fusion.17
  48.6 1.1 %collective-permute-done.6 = bf16[80,3072]{1,0:T(8,128)(2,1)S(1)} collective-permute-done((bf16[80,3072]{1,0:T(8,128)(2,1)S(1)}, bf16[80,3072]{1,0:T(8,128)(2,1)S(1)}, u32[]{:S(2)}, u32[]{:S(2)}) %collective-permute-start.6) | collective-permute-done | bytes 491552 | tf_op jit(solution)/shard_map/ppermute | solution.py:27
  49.7 0.0 copy-done.5
  49.7 0.0 copy-done.6
  49.7 0.0 copy-done.7
  49.7 0.0 copy-start
  49.7 0.5 fusion.9
  50.2 0.2 subtract_convert_fusion.1
  50.5 1.4 %copy-done = bf16[2048,1024]{1,0:T(8,128)(2,1)S(1)} copy-done((bf16[2048,1024]{1,0:T(8,128)(2,1)S(1)}, bf16[2048,1024]{1,0:T(8,128)(2,1)}, u32[]{:S(2)}) %copy-start) | copy-done | bytes 4194328
  51.9 0.0 copy-start.1
  51.9 0.9 fusion.37
  52.8 0.2 collective-permute-start.7
  53.0 1.5 %collective-permute-done.7 = f32[80,1024]{1,0:T(8,128)S(1)} collective-permute-done((f32[80,1024]{1,0:T(8,128)S(1)}, f32[80,1024]{1,0:T(8,128)S(1)}, u32[]{:S(2)}, u32[]{:S(2)}) %collective-permute-start.7) | collective-permute-done | bytes 327712 | tf_op jit(solution)/shard_map/ppermute | solution.py:27
  54.5 1.0 fusion.13
  55.5 0.0 copy-done.1
  55.5 33.9 %all_to_all.10 = f32[8,64,1024]{2,1,0:T(8,128)S(1)} all-to-all(f32[8,64,1024]{2,1,0:T(8,128)S(1)} %bitcast.9), channel_id=1, replica_groups=mesh['y'=4,'z'=4,'x'=8,'c'=2] {'x'}, dimensions={0} | all-to-all | bytes 4194304 | tf_op jit(solution)/shard_map/all_to_all | solution.py:101
  89.4 0.1 reduce_sum.28
  89.6 0.1 reshape.14
  89.6 14.3 %all_to_all.11 = f32[16,4,1024]{2,1,0:T(4,128)S(1)} all-to-all(f32[16,4,1024]{2,1,0:T(4,128)S(1)} %reshape.14), channel_id=1, replica_groups=mesh['y'=4,'z'=4,'x'=8,'c'=2] {'z','y'}, dimensions={0} | all-to-all | bytes 524288 | tf_op jit(solution)/shard_map/all_to_all | solution.py:101
  103.9 0.7 reduce_sum.29
  (5 shorter events, 0.1 us)
Async XLA Ops:
  0.6 5.4 %copy-start.8 = (s32[80,16]{0,1:T(8,128)S(1)}, s32[80,16]{0,1:T(8,128)}, u32[]{:S(2)}) copy-start(s32[80,16]{0,1:T(8,128)} %param.10) | copy-start | bytes 15364
  0.6 5.4 %copy-start.4 = (f32[80,16]{0,1:T(8,128)S(1)}, f32[80,16]{0,1:T(8,128)}, u32[]{:S(2)}) copy-start(f32[80,16]{0,1:T(8,128)} %param.11) | copy-start | bytes 15364
  0.7 5.5 %copy-start.3 = (s32[80,720]{1,0:T(8,128)S(1)}, s32[80,720]{1,0:T(8,128)}, u32[]{:S(2)}) copy-start(s32[80,720]{1,0:T(8,128)} %param.9) | copy-start | bytes 691204
  1.7 5.5 %copy-start.9 = (s32[512]{0:T(512)S(1)}, s32[512]{0:T(512)}, u32[]{:S(2)}) copy-start(s32[512]{0:T(512)} %constant.47.clone) | copy-start | bytes 6148
  3.7 13.3 %collective-permute-start = (bf16[80,3072]{1,0:T(8,128)(2,1)}, bf16[80,3072]{1,0:T(8,128)(2,1)}, u32[]{:S(2)}, u32[]{:S(2)}) collective-permute-start(bf16[80,3072]{1,0:T(8,128)(2,1)} %pad_maximum_fusion.1), channel_id=1, source_target_pairs={{0,254},{1,255},{2,0},{3,1},{4,2},{5,3},{6,4},{7,5},{8,6},{9,7},{1... | collective-permute-start | bytes 1474568 | tf_op jit(solution)/shard_map/ppermute | solution.py:22
  6.0 20.0 %collective-permute-start.1 = (bf16[80,3072]{1,0:T(8,128)(2,1)}, bf16[80,3072]{1,0:T(8,128)(2,1)S(1)}, u32[]{:S(2)}, u32[]{:S(2)}) collective-permute-start(bf16[80,3072]{1,0:T(8,128)(2,1)} %pad_maximum_fusion.1), channel_id=1, source_target_pairs={{0,2},{1,3},{2,4},{3,5},{4,6},{5,7},{6,8},{7,9},{8,10},{9,11},{10,... | collective-permute-start | bytes 1474568 | tf_op jit(solution)/shard_map/ppermute | solution.py:22
  6.0 1.3 %collective-permute-start.2 = (f32[80,32]{0,1:T(8,128)S(1)}, f32[80,32]{0,1:T(8,128)S(1)}, u32[]{:S(2)}, u32[]{:S(2)}) collective-permute-start(f32[80,32]{0,1:T(8,128)S(1)} %pad_maximum_fusion.4), channel_id=1, source_target_pairs={{0,1},{1,0},{2,3},{3,2},{4,5},{5,4},{6,7},{7,6},{8,9},{9,8},{10,11... | collective-permute-start | bytes 30728 | tf_op jit(solution)/shard_map/ppermute | solution.py:27
  10.2 24.2 %copy-start.2 = (f32[160,16]{1,0:T(8,128)S(1)}, f32[160,16]{1,0:T(8,128)}, u32[]{:S(2)}) copy-start(f32[160,16]{1,0:T(8,128)} %copy.14) | copy-start | bytes 30724
  27.1 21.1 %collective-permute-start.3 = (bf16[240,3072]{1,0:T(8,128)(2,1)S(1)}, bf16[240,3072]{1,0:T(8,128)(2,1)S(1)}, u32[]{:S(2)}, u32[]{:S(2)}) collective-permute-start(bf16[240,3072]{1,0:T(8,128)(2,1)S(1)} %pad_maximum_fusion), channel_id=1, source_target_pairs={{0,1},{1,0},{2,3},{3,2},{4,5},{5,4},{6,7},{7,6},{8,9},{9,8},{10,11... | collective-permute-start | bytes 4423688 | tf_op jit(solution)/shard_map/ppermute | solution.py:27
  27.2 18.6 %collective-permute-start.4 = (bf16[80,3072]{1,0:T(8,128)(2,1)}, bf16[80,3072]{1,0:T(8,128)(2,1)S(1)}, u32[]{:S(2)}, u32[]{:S(2)}) collective-permute-start(bf16[80,3072]{1,0:T(8,128)(2,1)} %collective-permute-done), channel_id=1, source_target_pairs={{0,254},{1,255},{2,0},{3,1},{4,2},{5,3},{6,4},{7,5},{8,6},{9,7},{1... | collective-permute-start | bytes 1474568 | tf_op jit(solution)/shard_map/ppermute | solution.py:22
  34.4 13.3 %collective-permute-start.5 = (bf16[80,3072]{1,0:T(8,128)(2,1)S(1)}, bf16[80,3072]{1,0:T(8,128)(2,1)S(1)}, u32[]{:S(2)}, u32[]{:S(2)}) collective-permute-start(bf16[80,3072]{1,0:T(8,128)(2,1)S(1)} %collective-permute-done.1), channel_id=1, source_target_pairs={{0,2},{1,3},{2,4},{3,5},{4,6},{5,7},{6,8},{7,9},{8,10},{9,11},{10,... | collective-permute-start | bytes 1474568 | tf_op jit(solution)/shard_map/ppermute | solution.py:22
  37.0 12.7 %copy-start.5 = (bf16[80,80]{1,0:T(8,128)(2,1)S(1)}, bf16[80,80]{1,0:T(8,128)(2,1)}, u32[]{:S(2)}) copy-start(bf16[80,80]{1,0:T(8,128)(2,1)} %get-tuple-element.11) | copy-start | bytes 38404
  37.0 12.7 %copy-start.6 = (bf16[80,80]{1,0:T(8,128)(2,1)S(1)}, bf16[80,80]{1,0:T(8,128)(2,1)}, u32[]{:S(2)}) copy-start(bf16[80,80]{1,0:T(8,128)(2,1)} %get-tuple-element.12) | copy-start | bytes 38404
  37.0 12.7 %copy-start.7 = (bf16[80,80]{1,0:T(8,128)(2,1)S(1)}, bf16[80,80]{1,0:T(8,128)(2,1)}, u32[]{:S(2)}) copy-start(bf16[80,80]{1,0:T(8,128)(2,1)} %get-tuple-element.16) | copy-start | bytes 38404
  47.7 2.0 %collective-permute-start.6 = (bf16[80,3072]{1,0:T(8,128)(2,1)S(1)}, bf16[80,3072]{1,0:T(8,128)(2,1)S(1)}, u32[]{:S(2)}, u32[]{:S(2)}) collective-permute-start(bf16[80,3072]{1,0:T(8,128)(2,1)S(1)} %broadcast_select_fusion), channel_id=1, source_target_pairs={{0,1},{1,0},{2,3},{3,2},{4,5},{5,4},{6,7},{7,6},{8,9},{9,8},{10,11... | collective-permute-start | bytes 1474568 | tf_op jit(solution)/shard_map/ppermute | solution.py:27
  49.7 2.2 %copy-start = (bf16[2048,1024]{1,0:T(8,128)(2,1)S(1)}, bf16[2048,1024]{1,0:T(8,128)(2,1)}, u32[]{:S(2)}) copy-start(bf16[2048,1024]{1,0:T(8,128)(2,1)} %param.12) | copy-start | bytes 12582916
  51.9 3.6 %copy-start.1 = (bf16[80,2048]{1,0:T(8,128)(2,1)}, bf16[80,2048]{1,0:T(8,128)(2,1)S(1)}, u32[]{:S(2)}) copy-start(bf16[80,2048]{1,0:T(8,128)(2,1)S(1)} %pad_maximum_fusion.2) | copy-start | bytes 983044
  52.8 1.7 %collective-permute-start.7 = (f32[80,1024]{1,0:T(8,128)S(1)}, f32[80,1024]{1,0:T(8,128)S(1)}, u32[]{:S(2)}, u32[]{:S(2)}) collective-permute-start(f32[80,1024]{1,0:T(8,128)S(1)} %fusion.37), channel_id=1, source_target_pairs={{0,1},{1,0},{2,3},{3,2},{4,5},{5,4},{6,7},{7,6},{8,9},{9,8},{10,11... | collective-permute-start | bytes 983048 | tf_op jit(solution)/shard_map/ppermute | solution.py:27
